TPU v7x, 32 devices: a whole 2x2x4 slice. The times are simulated.
32 devices in a mesh: groups: 2 (over y), seq: 4 (over x, core), chan: 4 (over z).
Axes of the slice: x: 2, y: 2, z: 4, core: 2. Of those that a mesh axis runs over, the one named last changes fastest.
Arguments:
- hidden: bfloat16 [4096, 2048], P(('groups', 'seq')), parts along dimension 0, may hold values from -15 to 15
- bases: int32 [4096], P(('groups', 'seq')), parts along dimension 0, may hold values from 0 to 4
- w_gate: bfloat16 [2048, 4096], P(None, 'chan'), may hold values from -0.125 to 0.125
- w_values: bfloat16 [2048, 4096], P(None, 'chan'), may hold values from -0.125 to 0.125
- w_state_io: bfloat16 [2048, 2048], P(None, 'chan'), may hold values from -0.125 to 0.125
- w_step: bfloat16 [2048, 64], P(None, 'chan'), may hold values from -0.125 to 0.125
- conv_values: float32 [4, 4096], P(None, 'chan'), may hold values from -3 to 3
- conv_values_bias: float32 [4096], P('chan'), may hold values from -3 to 3
- conv_state_io: float32 [4, 2048], P(None, 'chan'), may hold values from -3 to 3
- conv_state_bias: float32 [2048], P('chan'), may hold values from -3 to 3
- step_bias: float32 [64], P('chan'), may hold values from -2 to 0
- decay_rate: float32 [64], P('chan'), may hold values from 0.0009765625 to 0.05, as said below
- skip_gain: float32 [64], P('chan'), may hold values from 0.5 to 1.5
- norm_gain: float32 [4096], P('chan'), may hold values from 0.1 to 1.9
- w_out: bfloat16 [4096, 2048], P('chan'), may hold values from -0.125 to 0.125
Outputs:
- mixed: bfloat16 [4096, 2048], P(('groups', 'seq'), 'chan'), parts along dimension 0
There are 2 independent parts, one for each index of `groups`. A program takes and returns all parts, laid end to end along the dimension named above; an argument that names none is the same for every part. Nothing has to cross between parts.
Inputs may be any that keep to these rules, and one draw needn't show every extreme that they name: `decay_rate`: positive rates.
All inputs are finite; a program needn't handle non-finite values.
Results may differ from a plain program's by a relative error of at most 0.014.
Values may be sent and summed in bfloat16 or wider, within the bound.
No kernel may reach another device: no remote copies, remote signals or barrier semaphores. Data moves between devices by JAX's collectives and lax.ppermute only.
A program may use at most 128 MiB of HBM per device.

v0:
```python
import jax
import jax.numpy as jnp
from jax import lax
from jax.sharding import PartitionSpec as P
from jax.experimental import pallas as pl

P_SIZE = 64
N = 128
K = 4
Q = 128
LANE = 128


EPSILON = 1e-05
HIGHEST = lax.Precision.HIGHEST
F32 = jnp.float32
BF16 = jnp.bfloat16


def shifted(value, axis, steps):
    count = lax.axis_size(axis)
    pairs = [(source, source + steps) for source in range(count) if 0 <= source + steps < count]
    if not pairs:
        return jax.tree.map(jnp.zeros_like, value)
    return lax.ppermute(value, axis, pairs)


def exclusive_carry(total_log, state, sign):
    count = lax.axis_size("seq")
    heads = state.shape[0]
    flat = state.reshape(heads, -1)
    size = flat.shape[1]

    def send(log, st, distance):
        packed = jnp.concatenate([st, jnp.broadcast_to(log[:, None], (heads, LANE))], axis=1)
        got = shifted(packed, "seq", sign * distance)
        return got[:, size], got[:, :size]

    got_log, got_state = send(total_log, flat, 1)
    x_log, x_state = got_log, got_state
    i_log = got_log + total_log
    i_state = jnp.exp(total_log)[:, None] * got_state + flat
    covered, window = 1, 2
    while covered < count - 1:
        r_log, r_state = send(i_log, i_state, window)
        x_state = jnp.exp(x_log)[:, None] * r_state + x_state
        x_log = x_log + r_log
        covered += window
        if covered < count - 1:
            i_state = jnp.exp(i_log)[:, None] * r_state + i_state
            i_log = i_log + r_log
            window *= 2
    return x_state.reshape(state.shape)


def group_layout(acc, delta, groups, per_group):
    rows = acc.shape[0]
    acc_g = jnp.transpose(acc.reshape(rows, groups, per_group), (1, 0, 2))
    delta_g = jnp.transpose(delta.reshape(rows, groups, per_group), (1, 0, 2))
    return acc_g, delta_g, jnp.transpose(acc_g, (0, 2, 1)), jnp.transpose(delta_g, (0, 2, 1))


def block_states(state_c, values_t, acc_t, delta_t, forward, interpret=False):
    rows = values_t.shape[1]
    groups, per_group, _ = acc_t.shape
    blocks = rows // Q
    width_g = per_group * P_SIZE

    def kernel(b_ref, xt_ref, at_ref, dt_ref, s_ref):
        b_blk = b_ref[...]
        for j in range(per_group):
            a_row = at_ref[0, j : j + 1, :]
            d_row = dt_ref[0, j : j + 1, :]
            a_end = a_row[:, Q - 1 : Q] if forward else a_row[:, 0:1]
            xt_j = xt_ref[j * P_SIZE : (j + 1) * P_SIZE, :]
            tx = (jnp.exp(a_end - a_row) * d_row) * xt_j.astype(F32)
            t_hi = tx.astype(BF16)
            t_lo = (tx - t_hi.astype(F32)).astype(BF16)
            s_ref[0, j] = jnp.dot(t_hi, b_blk, preferred_element_type=F32) + jnp.dot(
                t_lo, b_blk, preferred_element_type=F32
            )

    return pl.pallas_call(
        kernel,
        grid=(blocks, groups),
        in_specs=[
            pl.BlockSpec((Q, N), lambda b, g: (b, 2 * g)),
            pl.BlockSpec((width_g, Q), lambda b, g: (g, b)),
            pl.BlockSpec((1, per_group, Q), lambda b, g: (g, 0, b)),
            pl.BlockSpec((1, per_group, Q), lambda b, g: (g, 0, b)),
        ],
        out_specs=pl.BlockSpec((1, per_group, P_SIZE, N), lambda b, g: (b, g, 0, 0)),
        out_shape=jax.ShapeDtypeStruct((blocks, groups * per_group, P_SIZE, N), F32),
        interpret=interpret,
    )(state_c, values_t, acc_t, delta_t)


def block_intra(state_c, values_c, acc_g, acc_t, delta_t, forward, interpret=False):
    rows = values_c.shape[0]
    groups, _, per_group = acc_g.shape
    blocks = rows // Q
    width_g = per_group * P_SIZE

    def kernel(c_ref, b_ref, x_ref, a_ref, at_ref, dt_ref, y_ref):
        inner = lax.dot_general(
            c_ref[...], b_ref[...], (((1,), (1,)), ((), ())), preferred_element_type=F32
        )
        row = lax.broadcasted_iota(jnp.int32, (Q, Q), 0)
        col = lax.broadcasted_iota(jnp.int32, (Q, Q), 1)
        mask = row >= col if forward else row <= col
        for j in range(per_group):
            a_col = a_ref[0, :, j : j + 1]
            a_row = at_ref[0, j : j + 1, :]
            d_row = dt_ref[0, j : j + 1, :]
            differ = jnp.where(mask, a_col - a_row, 0.0)
            m = jnp.where(mask, jnp.exp(differ), 0.0) * d_row * inner
            x_j = x_ref[:, j * P_SIZE : (j + 1) * P_SIZE]
            m_hi = m.astype(BF16)
            m_lo = (m - m_hi.astype(F32)).astype(BF16)
            y_ref[:, j * P_SIZE : (j + 1) * P_SIZE] = jnp.dot(
                m_hi, x_j, preferred_element_type=F32
            ) + jnp.dot(m_lo, x_j, preferred_element_type=F32)

    return pl.pallas_call(
        kernel,
        grid=(blocks, groups),
        in_specs=[
            pl.BlockSpec((Q, N), lambda b, g: (b, 2 * g + 1)),
            pl.BlockSpec((Q, N), lambda b, g: (b, 2 * g)),
            pl.BlockSpec((Q, width_g), lambda b, g: (b, g)),
            pl.BlockSpec((1, Q, per_group), lambda b, g: (g, b, 0)),
            pl.BlockSpec((1, per_group, Q), lambda b, g: (g, 0, b)),
            pl.BlockSpec((1, per_group, Q), lambda b, g: (g, 0, b)),
        ],
        out_specs=pl.BlockSpec((Q, width_g), lambda b, g: (b, g)),
        out_shape=jax.ShapeDtypeStruct((rows, groups * width_g), F32),
        interpret=interpret,
    )(state_c, state_c, values_c, acc_g, acc_t, delta_t)


def conv_silu(padded, kernel, offset, count, forward):
    taps = kernel.shape[0]
    total = jnp.zeros((count, padded.shape[1]), F32) + offset[None, :]
    for index in range(taps):
        start = index if forward else taps - 1 - index
        total = total + kernel[index][None, :] * padded[start : start + count].astype(F32)
    return jax.nn.silu(total).astype(BF16)


def on_device(
    hidden,
    bases,
    w_gate,
    w_values,
    w_state_io,
    w_step,
    conv_values,
    conv_values_bias,
    conv_state_io,
    conv_state_bias,
    step_bias,
    decay_rate,
    skip_gain,
    norm_gain,
    w_out,
):
    rows, width = hidden.shape
    heads = w_step.shape[1]
    groups = w_state_io.shape[1] // (2 * N)
    per_group = heads // groups
    blocks = rows // Q
    known = jnp.where(bases == 4, 0.0, 1.0).astype(F32)

    lane_idx = jnp.arange(LANE)
    anti = (lane_idx[:, None] + lane_idx[None, :] == LANE - 1).astype(BF16)

    def lane_reverse(block):
        count = block.shape[0]
        flipped = jnp.einsum(
            "rki,ij->rkj", block.reshape(count, width // LANE, LANE), anti, preferred_element_type=F32
        ).astype(BF16)
        return jnp.flip(flipped, 1).reshape(count, width)

    hidden_rev = lane_reverse(hidden)

    taps = K - 1
    known_cols = jnp.broadcast_to(known.astype(BF16)[:, None], (rows, LANE))
    edge_first = jnp.concatenate([hidden[:taps], known_cols[:taps]], axis=1)
    edge_last = jnp.concatenate([hidden[rows - taps :], known_cols[rows - taps :]], axis=1)
    from_prev = shifted(edge_last, "seq", 1)
    from_next = shifted(edge_first, "seq", -1)
    rim_rows = jnp.concatenate([from_prev[:, :width], lane_reverse(from_next[:, :width])], axis=0)
    rim_known = jnp.concatenate([from_prev[:, width], from_next[:, width]], axis=0).astype(F32)
    rim_values = (
        jnp.dot(rim_rows, w_values, preferred_element_type=F32) * rim_known[:, None]
    ).astype(BF16)
    rim_state = jnp.dot(rim_rows, w_state_io, preferred_element_type=F32).astype(BF16)

    def project(source):
        gate_in = jnp.dot(source, w_gate, preferred_element_type=F32).astype(BF16)
        values = (jnp.dot(source, w_values, preferred_element_type=F32) * known[:, None]).astype(BF16)
        state_io = jnp.dot(source, w_state_io, preferred_element_type=F32).astype(BF16)
        step_raw = jnp.dot(source, w_step, preferred_element_type=F32).astype(BF16)
        return gate_in, values, state_io, step_raw

    t_idx = jnp.arange(Q)

    def local_scan(pieces, forward):
        gate_in, values, state_io, step_raw = pieces
        sign = 1 if forward else -1
        if forward:
            pv = jnp.concatenate([rim_values[:taps], values], axis=0)
            ps = jnp.concatenate([rim_state[:taps], state_io], axis=0)
        else:
            pv = jnp.concatenate([values, rim_values[taps:]], axis=0)
            ps = jnp.concatenate([state_io, rim_state[taps:]], axis=0)
        values_c = conv_silu(pv, conv_values, conv_values_bias, rows, forward)
        state_c = conv_silu(ps, conv_state_io, conv_state_bias, rows, forward)
        delta = jax.nn.softplus(step_raw.astype(F32) + step_bias[None, :])
        logdec = -decay_rate[None, :] * delta

        sb = state_c.reshape(blocks, Q, groups, 2, N)
        c_vec = sb[:, :, :, 1, :]
        ld = logdec.reshape(blocks, Q, heads)
        if forward:
            mask = t_idx[:, None] >= t_idx[None, :]
        else:
            mask = t_idx[:, None] <= t_idx[None, :]
        acc = jnp.einsum("ts,bsh->bth", mask.astype(F32), ld, precision=HIGHEST)
        blk = jnp.sum(ld, axis=1)
        acc_g, delta_g, acc_t, delta_t = group_layout(acc.reshape(rows, heads), delta, groups, per_group)
        states = block_states(state_c, values_c.T, acc_t, delta_t, forward)

        order = list(range(blocks)) if forward else list(range(blocks - 1, -1, -1))
        block_decay = jnp.exp(blk)
        running = jnp.zeros((heads, P_SIZE, N), F32)
        local_start = [None] * blocks
        entering = [None] * blocks
        log_before = jnp.zeros((heads,), F32)
        for index in order:
            local_start[index] = running
            entering[index] = jnp.exp(log_before)
            running = block_decay[index][:, None, None] * running + states[index]
            log_before = log_before + blk[index]
        total = log_before
        carried = exclusive_carry(total, running, sign)
        intra = block_intra(state_c, values_c, acc_g, acc_t, delta_t, forward)
        start = jnp.stack(
            [local_start[index] + entering[index][:, None, None] * carried for index in range(blocks)]
        )
        start = start.reshape(blocks, groups, per_group * P_SIZE, N)
        c_f32 = c_vec.astype(F32)
        inter = jnp.concatenate(
            [
                jnp.einsum("btn,bkn->btk", c_f32[:, :, group], start[:, group], precision=HIGHEST)
                for group in range(groups)
            ],
            axis=2,
        ).reshape(rows, heads, P_SIZE) * jnp.exp(acc).reshape(rows, heads)[:, :, None]
        x = values_c.astype(F32).reshape(rows, heads, P_SIZE)
        outputs = intra.reshape(rows, heads, P_SIZE) + inter + skip_gain[None, :, None] * x
        gated = outputs.reshape(rows, heads * P_SIZE) * jax.nn.silu(gate_in.astype(F32))
        grouped = gated.reshape(rows, groups, per_group * P_SIZE)
        scale = lax.rsqrt(jnp.mean(grouped * grouped, axis=-1, keepdims=True) + EPSILON)
        return ((grouped * scale).reshape(rows, heads * P_SIZE) * norm_gain[None, :]).astype(BF16)

    forward_out = local_scan(project(hidden), True)
    backward_out = local_scan(project(hidden_rev), False)
    combined = (forward_out.astype(F32) + backward_out.astype(F32)).astype(BF16)
    chan = lax.axis_size("chan")
    partial = jnp.dot(combined, w_out, preferred_element_type=F32).astype(BF16)
    partial = jnp.transpose(partial.reshape(rows, chan, width // chan), (1, 0, 2))
    summed = lax.psum_scatter(partial, "chan", scatter_dimension=0, tiled=True)
    return summed.reshape(rows, width // chan)


def solution(mesh):
    return jax.shard_map(
        on_device,
        mesh=mesh,
        in_specs=(
            P(("groups", "seq"), None),
            P(("groups", "seq")),
            P(None, "chan"),
            P(None, "chan"),
            P(None, "chan"),
            P(None, "chan"),
            P(None, "chan"),
            P("chan"),
            P(None, "chan"),
            P("chan"),
            P("chan"),
            P("chan"),
            P("chan"),
            P("chan"),
            P("chan", None),
        ),
        out_specs=P(("groups", "seq"), "chan"),
        check_vma=False,
    )
```

profile of v0, /device:TPU:0, one launch (start us, length us, event | category | flops | bytes accessed | tf_op | source)
XLA Modules:
  0.0 226.8 jit_solution(7383051570688756602)
XLA Ops:
  8.3 1.3 collective-permute-start.1
  9.7 3.0 %collective-permute-start = (bf16[3,2176]{1,0:T(4,128)(2,1)S(1)}, bf16[3,2176]{1,0:T(4,128)(2,1)S(1)}, u32[]{:S(2)}, u32[]{:S(2)}) collective-permute-start(bf16[3,2176]{1,0:T(4,128)(2,1)S(1)} %pad_maximum_fusion.15), channel_id=1, source_target_pairs={{0,4},{4,8},{8,12},{1,5},{5,9},{9,13},{2,6},{6,10},{10,14},{3,7},{... | collective-permute-start | bytes 39176 | tf_op jit(solution)/shard_map/ppermute | solution.py:25
  12.8 3.6 %convert_bitcast_fusion = bf16[512,16,128]{0,2,1:T(8,128)(2,1)} fusion(bf16[512,2048]{1,0:T(8,128)(2,1)} %param.15), kind=kOutput, calls=%fused_computation.38 | convolution fusion | flops 269516800 | bytes 4194304 | tf_op jit(solution)/shard_map/rki,ij->rkj/dot_general | solution.py:179
  16.4 3.1 %rev.9 = bf16[512,16,128]{0,2,1:T(8,128)(2,1)} reverse(bf16[512,16,128]{0,2,1:T(8,128)(2,1)} %convert_bitcast_fusion), dimensions={1} | reverse | bytes 4194304 | tf_op jit(solution)/shard_map/jit(_flip)/rev | solution.py:182
  19.5 6.3 %multiply_convert_fusion.3 = bf16[512,1024]{0,1:T(8,128)(2,1)} fusion(bf16[512,2048]{1,0:T(8,128)(2,1)} %param.15, bf16[2048,1024]{1,0:T(8,128)(2,1)} %param.18, f32[512]{0:T(512)S(1)} %get-tuple-element.55), kind=kOutput, calls=%fused_computation.40 | convolution fusion | flops 2148532224 | bytes 7342080 | tf_op jit(solution)/shard_map/dot_general | solution.py:201
  25.8 3.4 %multiply_convert_fusion.1 = bf16[512,1024]{0,1:T(8,128)(2,1)} fusion(bf16[512,2048]{0,1:T(8,128)(2,1)S(1)} %bitcast.295, bf16[2048,1024]{1,0:T(8,128)(2,1)S(1)} %copy-done.15, f32[512]{0:T(512)S(1)} %get-tuple-element.55), kind=kOutput, calls=%fused_computation.37 | convolution fusion | flops 2148532224 | bytes 7342080 | tf_op jit(solution)/shard_map/dot_general | solution.py:201
  29.2 2.1 convolution_convert_fusion.3
  31.3 2.1 convolution_convert_fusion.4
  33.9 1.3 broadcast_multiply_fusion.1
  40.0 1.0 copy.184.a_ref
  41.7 1.0 copy.169.a_ref
  43.7 4.0 %fusion.21 = bf16[6,1024]{0,1:T(8,128)(2,1)S(1)} fusion(bf16[2048,1024]{1,0:T(8,128)(2,1)} %param.18, f32[6]{0:T(128)S(1)} %maximum_convert_fusion, bf16[3,2048]{1,0:T(4,128)(2,1)S(1)} %bitcast.338, bf16[3,2048]{1,0:T(4,128)(2,1)S(1)} %slice.299), kind=kOutput, calls=%fused_computation.54 | convolution fusion | flops 25227264 | bytes 4231192 | tf_op jit(solution)/shard_map/dot_general | solution.py:195
  48.7 1.8 multiply_convert_fusion.5
  50.5 1.1 reshape.404
  51.7 8.9 %multiply_convert_fusion.2 = (bf16[512,1024]{0,1:T(8,128)(2,1)S(1)}, bf16[512,1024]{0,1:T(8,128)(2,1)S(1)}) fusion(bf16[512,1024]{0,1:T(8,128)(2,1)} %multiply_convert_fusion.3, bf16[3,1024]{0,1:T(8,128)(2,1)S(1)} %get-tuple-element.37, f32[1024]{0:T(1024)S(1)} %bitcast.342, f32[1024]{0:T(1024)S(1)} %bitcast.343, f32[1024]{0:T(1024)S(1)} %bitcast.341, ...), kind=kLoop, calls=%fused_computation.39 | loop fusion | flops 27262976 | bytes 4227072 | tf_op jit(solution)/shard_map/convert_element_type | solution.py:147
  60.7 1.7 copy.183.x_ref
  62.4 6.7 %shard_map.148 = f32[4,16,64,128]{3,2,1,0:T(8,128)} custom-call(bf16[512,512]{1,0:T(8,128)(2,1)} %copy-done.13, bf16[1024,512]{1,0:T(8,128)(2,1)} %bitcast.300, f32[2,8,512]{2,1,0:T(8,128)} %bitcast.333, f32[2,8,512]{2,1,0:T(8,128)} %bitcast.327), custom_call_target="tpu_custom_call" | custom-call | tf_op jit(solution)/shard_map/pallas_call | solution.py:83
  69.1 1.7 fusion.79
  70.8 1.2 bitcast_add_fusion
  72.9 1.3 collective-permute-start.4
  74.8 7.8 %shard_map.147 = f32[512,1024]{1,0:T(8,128)} custom-call(bf16[512,512]{1,0:T(8,128)(2,1)} %copy-done.13, bf16[512,512]{1,0:T(8,128)(2,1)} %copy-done.13, bf16[512,1024]{1,0:T(8,128)(2,1)} %copy.183.x_ref, f32[2,512,8]{2,1,0:T(8,128)} %copy.184.a_ref, f32[2,8,512]{2,1,0:T(8,128)} %bitcast.334, f32[2,8,512]{2,1,0:T(8,128)} %bitcast.328), custom_call_target="tpu_custom_call" | custom-call | tf_op jit(solution)/shard_map/pallas_call | solution.py:124
  82.6 3.0 %copy.192 = f32[512,1024]{0,1:T(8,128)} copy(f32[512,1024]{1,0:T(8,128)} %shard_map.147) | data formatting | bytes 4194304 | tf_op jit(solution)/shard_map/pallas_call | solution.py:124
  86.5 1.4 copy.168.x_ref
  87.9 6.7 %shard_map.146 = f32[4,16,64,128]{3,2,1,0:T(8,128)} custom-call(bf16[512,512]{1,0:T(8,128)(2,1)} %copy-done.12, bf16[1024,512]{1,0:T(8,128)(2,1)} %bitcast.299, f32[2,8,512]{2,1,0:T(8,128)} %bitcast.330, f32[2,8,512]{2,1,0:T(8,128)} %bitcast.335), custom_call_target="tpu_custom_call" | custom-call | tf_op jit(solution)/shard_map/pallas_call | solution.py:83
  94.6 1.7 fusion.78
  96.3 1.2 bitcast_add_fusion.4
  98.5 5.1 %collective-permute-start.2 = (f32[16,8320]{1,0:T(8,128)}, f32[16,8320]{1,0:T(8,128)S(1)}, u32[]{:S(2)}, u32[]{:S(2)}) collective-permute-start(f32[16,8320]{1,0:T(8,128)} %pad_maximum_fusion.6), channel_id=1, source_target_pairs={{0,4},{4,8},{8,12},{1,5},{5,9},{9,13},{2,6},{6,10},{10,14},{3,7},{... | collective-permute-start | bytes 1597448 | tf_op jit(solution)/shard_map/ppermute | solution.py:25
  105.0 7.8 %shard_map.145 = f32[512,1024]{1,0:T(8,128)} custom-call(bf16[512,512]{1,0:T(8,128)(2,1)} %copy-done.12, bf16[512,512]{1,0:T(8,128)(2,1)} %copy-done.12, bf16[512,1024]{1,0:T(8,128)(2,1)} %copy.168.x_ref, f32[2,512,8]{2,1,0:T(8,128)} %copy.169.a_ref, f32[2,8,512]{2,1,0:T(8,128)} %bitcast.331, f32[2,8,512]{2,1,0:T(8,128)} %bitcast.336), custom_call_target="tpu_custom_call" | custom-call | tf_op jit(solution)/shard_map/pallas_call | solution.py:124
  112.7 3.0 %copy.177 = f32[512,1024]{0,1:T(8,128)} copy(f32[512,1024]{1,0:T(8,128)} %shard_map.145) | data formatting | bytes 4194304 | tf_op jit(solution)/shard_map/pallas_call | solution.py:124
  116.9 1.3 collective-permute-start.5
  119.8 6.3 %collective-permute-start.3 = (f32[16,8320]{1,0:T(8,128)}, f32[16,8320]{1,0:T(8,128)}, u32[]{:S(2)}, u32[]{:S(2)}) collective-permute-start(f32[16,8320]{1,0:T(8,128)} %pad_maximum_fusion.7), channel_id=1, source_target_pairs={{0,8},{4,12},{1,9},{5,13},{2,10},{6,14},{3,11},{7,15},{16,24},{20,... | collective-permute-start | bytes 1597448 | tf_op jit(solution)/shard_map/ppermute | solution.py:25
  126.1 7.2 %collective-permute-done.5 = f32[16,8320]{1,0:T(8,128)} collective-permute-done((f32[16,8320]{1,0:T(8,128)}, f32[16,8320]{1,0:T(8,128)}, u32[]{:S(2)}, u32[]{:S(2)}) %collective-permute-start.5) | collective-permute-done | bytes 532512 | tf_op jit(solution)/shard_map/ppermute | solution.py:25
  133.4 1.2 fusion.50
  135.3 1.7 fusion.31
  137.0 1.6 fusion.30
  138.6 1.3 fusion.51
  141.6 1.6 fusion.33
  143.2 1.6 fusion.32
  144.9 1.4 pad_maximum_fusion.3
  146.3 3.1 %copy.203 = f32[512,1024]{0,1:T(8,128)} copy(f32[512,1024]{1,0:T(8,128)} %bitcast.302) | data formatting | bytes 4194304 | tf_op jit(solution)/shard_map/reshape | solution.py:259
  149.5 8.0 %bitcast_reduce_fusion = (f32[512,2]{0,1:T(2,128)S(1)}, f32[512,1024]{0,1:T(8,128)}) fusion(bf16[512,2048]{0,1:T(8,128)(2,1)S(1)} %bitcast.298, bf16[2048,1024]{1,0:T(8,128)(2,1)} %param.17, bf16[512,1024]{0,1:T(8,128)(2,1)S(1)} %copy-done.9, f32[1024]{0:T(1024)S(1)} %mul.591, f32[512,1024]{0,1:T(8,128)} %copy.192, f32[512,1024]{0,1:T(8,128)} %copy.203, ...), kind=kOutput, calls=%fused_computation.24 | convolution fusion | flops 2154822656 | bytes 13672448 | tf_op jit(solution)/shard_map/dot_general | solution.py:200
  157.4 1.5 pad_maximum_fusion.1
  159.0 3.1 %copy.202 = f32[512,1024]{0,1:T(8,128)} copy(f32[512,1024]{1,0:T(8,128)} %bitcast.303) | data formatting | bytes 4194304 | tf_op jit(solution)/shard_map/reshape | solution.py:259
  162.0 6.6 %bitcast_reduce_fusion.1 = (f32[512,2]{0,1:T(2,128)S(1)}, f32[512,1024]{0,1:T(8,128)S(1)}) fusion(bf16[512,2048]{1,0:T(8,128)(2,1)S(1)} %copy-done.5, bf16[2048,1024]{1,0:T(8,128)(2,1)} %param.17, bf16[512,1024]{0,1:T(8,128)(2,1)S(1)} %copy-done.7, f32[1024]{0:T(1024)S(1)} %mul.591, f32[512,1024]{0,1:T(8,128)} %copy.177, f32[512,1024]{0,1:T(8,128)} %copy.202, ...), kind=kOutput, calls=%fused_computation.31 | convolution fusion | flops 2154822656 | bytes 13672448 | tf_op jit(solution)/shard_map/dot_general | solution.py:200
  169.1 1.8 copy-done.66
  170.9 2.5 %convolution_convert_fusion = bf16[512,2048]{1,0:T(8,128)(2,1)S(1)} fusion(bf16[1024,2048]{1,0:T(8,128)(2,1)S(1)} %copy-done.66, bf16[512,1024]{0,1:T(8,128)(2,1)S(1)} %get-tuple-element.54, bf16[512,1024]{0,1:T(8,128)(2,1)S(1)} %get-tuple-element.53), kind=kOutput, calls=%fused_computation | convolution fusion | flops 2150629376 | bytes 8388608 | tf_op jit(solution)/shard_map/dot_general | solution.py:271
  173.4 1.5 copy.258
  174.9 45.1 %reduce-scatter.2.cloned.1.call-done = bf16[1,512,512]{2,1,0:T(8,128)(2,1)} async-done(((bf16[4,512,512]{2,1,0:T(8,128)(2,1)}), bf16[1,512,512]{2,1,0:T(8,128)(2,1)}) %reduce-scatter.2.cloned.1.call-update) | async-done | bytes 524304 | tf_op jit(solution)/shard_map/reduce_scatter | solution.py:273
  (216 shorter events, 20.0 us)
Async XLA Ops:
  6.5 22.7 %copy-start = (bf16[2048,512]{1,0:T(8,128)(2,1)S(1)}, bf16[2048,512]{1,0:T(8,128)(2,1)}, u32[]{:S(2)}) copy-start(bf16[2048,512]{1,0:T(8,128)(2,1)} %param.19) | copy-start | bytes 6291460
  6.5 213.4 %reduce-scatter.2.cloned.1.call-start = ((), (), s32[]{:S(2)}) async-start(), calls=%async_computation.1 | async-start | bytes 2621440 | tf_op jit(solution)/shard_map/reduce_scatter | solution.py:273
  8.3 34.4 %collective-permute-start.1 = (bf16[3,2176]{1,0:T(4,128)(2,1)S(1)}, bf16[3,2176]{1,0:T(4,128)(2,1)S(1)}, u32[]{:S(2)}, u32[]{:S(2)}) collective-permute-start(bf16[3,2176]{1,0:T(4,128)(2,1)S(1)} %pad_maximum_fusion.16), channel_id=1, source_target_pairs={{4,0},{8,4},{12,8},{5,1},{9,5},{13,9},{6,2},{10,6},{14,10},{7,3},{... | collective-permute-start | bytes 39176 | tf_op jit(solution)/shard_map/ppermute | solution.py:25
  9.7 33.4 %collective-permute-start = (bf16[3,2176]{1,0:T(4,128)(2,1)S(1)}, bf16[3,2176]{1,0:T(4,128)(2,1)S(1)}, u32[]{:S(2)}, u32[]{:S(2)}) collective-permute-start(bf16[3,2176]{1,0:T(4,128)(2,1)S(1)} %pad_maximum_fusion.15), channel_id=1, source_target_pairs={{0,4},{4,8},{8,12},{1,5},{5,9},{9,13},{2,6},{6,10},{10,14},{3,7},{... | collective-permute-start | bytes 39176 | tf_op jit(solution)/shard_map/ppermute | solution.py:25
  19.5 6.4 %copy-start.2 = (bf16[512,16,128]{0,2,1:T(8,128)(2,1)S(1)}, bf16[512,16,128]{0,2,1:T(8,128)(2,1)}, u32[]{:S(2)}) copy-start(bf16[512,16,128]{0,2,1:T(8,128)(2,1)} %rev.9) | copy-start | bytes 6291460
  19.5 6.4 %copy-start.15 = (bf16[2048,1024]{1,0:T(8,128)(2,1)S(1)}, bf16[2048,1024]{1,0:T(8,128)(2,1)}, u32[]{:S(2)}) copy-start(bf16[2048,1024]{1,0:T(8,128)(2,1)} %param.18) | copy-start | bytes 12582916
  33.8 8.9 %copy-start.26 = (f32[512,16]{0,1:T(8,128)}, f32[512,16]{0,1:T(8,128)S(1)}, u32[]{:S(2)}) copy-start(f32[512,16]{0,1:T(8,128)S(1)} %compare_select_fusion) | copy-start | bytes 98308
  33.9 7.2 %copy-start.65 = (f32[16]{0:T(128)S(1)}, f32[16]{0:T(128)}, u32[]{:S(2)}) copy-start(f32[16]{0:T(128)} %param.27) | copy-start | bytes 196
  37.8 3.2 %copy-start.43 = (f32[16]{0:T(128)}, f32[16]{0:T(128)S(1)}, u32[]{:S(2)}) copy-start(f32[16]{0:T(128)S(1)} %get-tuple-element.76) | copy-start | bytes 196
  39.4 3.3 %copy-start.41 = (f32[16]{0:T(128)}, f32[16]{0:T(128)S(1)}, u32[]{:S(2)}) copy-start(f32[16]{0:T(128)S(1)} %get-tuple-element.72) | copy-start | bytes 196
  39.5 8.3 %copy-start.28 = (f32[512,2,8]{0,2,1:T(8,128)}, f32[512,2,8]{0,2,1:T(8,128)S(1)}, u32[]{:S(2)}) copy-start(f32[512,2,8]{0,2,1:T(8,128)S(1)} %reshape_reshape.7) | copy-start | bytes 98308
  41.2 6.6 %copy-start.27 = (f32[512,2,8]{0,2,1:T(8,128)}, f32[512,2,8]{0,2,1:T(8,128)S(1)}, u32[]{:S(2)}) copy-start(f32[512,2,8]{0,2,1:T(8,128)S(1)} %reshape_reshape.6) | copy-start | bytes 98308
  43.7 5.0 %copy-start.22 = (bf16[512,512]{1,0:T(8,128)(2,1)S(1)}, bf16[512,512]{1,0:T(8,128)(2,1)}, u32[]{:S(2)}) copy-start(bf16[512,512]{1,0:T(8,128)(2,1)} %convolution_convert_fusion.3) | copy-start | bytes 1572868
  43.7 5.0 %copy-start.29 = (bf16[512,512]{1,0:T(8,128)(2,1)S(1)}, bf16[512,512]{1,0:T(8,128)(2,1)}, u32[]{:S(2)}) copy-start(bf16[512,512]{1,0:T(8,128)(2,1)} %convolution_convert_fusion.4) | copy-start | bytes 1572868
  43.7 5.0 %copy-start.36 = (f32[1,512]{1,0:T(1,128)S(1)}, f32[1,512]{1,0:T(1,128)}, u32[]{:S(2)}) copy-start(f32[1,512]{1,0:T(1,128)} %get-tuple-element.49) | copy-start | bytes 6148
  43.7 5.0 %copy-start.37 = (f32[1,512]{1,0:T(1,128)S(1)}, f32[1,512]{1,0:T(1,128)}, u32[]{:S(2)}) copy-start(f32[1,512]{1,0:T(1,128)} %get-tuple-element.50) | copy-start | bytes 6148
  43.7 5.0 %copy-start.38 = (f32[1,512]{1,0:T(1,128)S(1)}, f32[1,512]{1,0:T(1,128)}, u32[]{:S(2)}) copy-start(f32[1,512]{1,0:T(1,128)} %get-tuple-element.51) | copy-start | bytes 6148
  43.7 5.0 %copy-start.39 = (f32[1,512]{1,0:T(1,128)S(1)}, f32[1,512]{1,0:T(1,128)}, u32[]{:S(2)}) copy-start(f32[1,512]{1,0:T(1,128)} %get-tuple-element.52) | copy-start | bytes 6148
  43.7 5.0 %copy-start.53 = (f32[512]{0:T(512)S(1)}, f32[512]{0:T(512)}, u32[]{:S(2)}) copy-start(f32[512]{0:T(512)} %param.24) | copy-start | bytes 6148
  47.8 3.9 %copy-start.33 = (f32[1,1024]{1,0:T(1,128)S(1)}, f32[1,1024]{1,0:T(1,128)}, u32[]{:S(2)}) copy-start(f32[1,1024]{1,0:T(1,128)} %get-tuple-element.42) | copy-start | bytes 12292
  47.8 3.9 %copy-start.34 = (f32[1,1024]{1,0:T(1,128)S(1)}, f32[1,1024]{1,0:T(1,128)}, u32[]{:S(2)}) copy-start(f32[1,1024]{1,0:T(1,128)} %get-tuple-element.43) | copy-start | bytes 12292
  47.8 3.9 %copy-start.35 = (f32[1,1024]{1,0:T(1,128)S(1)}, f32[1,1024]{1,0:T(1,128)}, u32[]{:S(2)}) copy-start(f32[1,1024]{1,0:T(1,128)} %get-tuple-element.44) | copy-start | bytes 12292
  50.5 10.1 %copy-start.13 = (bf16[512,512]{1,0:T(8,128)(2,1)}, bf16[512,512]{1,0:T(8,128)(2,1)S(1)}, u32[]{:S(2)}) copy-start(bf16[512,512]{1,0:T(8,128)(2,1)S(1)} %get-tuple-element.46.c_ref.b_ref) | copy-start | bytes 1572868
  50.5 35.1 %copy-start.12 = (bf16[512,512]{1,0:T(8,128)(2,1)}, bf16[512,512]{1,0:T(8,128)(2,1)S(1)}, u32[]{:S(2)}) copy-start(bf16[512,512]{1,0:T(8,128)(2,1)S(1)} %get-tuple-element.45.c_ref.b_ref) | copy-start | bytes 1572868
  60.6 25.9 %copy-start.6 = (bf16[512,1024]{0,1:T(8,128)(2,1)}, bf16[512,1024]{0,1:T(8,128)(2,1)S(1)}, u32[]{:S(2)}) copy-start(bf16[512,1024]{0,1:T(8,128)(2,1)S(1)} %get-tuple-element.39) | copy-start | bytes 3145732
  70.7 3.5 %copy-start.23 = (bf16[4,128,2,2,128]{4,3,2,1,0:T(2,128)(2,1)S(1)}, bf16[4,128,2,2,128]{4,3,2,1,0:T(2,128)(2,1)}, u32[]{:S(2)}) copy-start(bf16[4,128,2,2,128]{4,3,2,1,0:T(2,128)(2,1)} %reshape.404) | copy-start | bytes 1572868
  72.9 42.8 %collective-permute-start.4 = (f32[16,8320]{1,0:T(8,128)}, f32[16,8320]{1,0:T(8,128)S(1)}, u32[]{:S(2)}, u32[]{:S(2)}) collective-permute-start(f32[16,8320]{1,0:T(8,128)} %pad_maximum_fusion.8), channel_id=1, source_target_pairs={{4,0},{8,4},{12,8},{5,1},{9,5},{13,9},{6,2},{10,6},{14,10},{7,3},{... | collective-permute-start | bytes 1597448 | tf_op jit(solution)/shard_map/ppermute | solution.py:25
  96.3 7.3 %copy-start.24 = (bf16[4,128,2,2,128]{4,3,2,1,0:T(2,128)(2,1)S(1)}, bf16[4,128,2,2,128]{4,3,2,1,0:T(2,128)(2,1)}, u32[]{:S(2)}) copy-start(bf16[4,128,2,2,128]{4,3,2,1,0:T(2,128)(2,1)} %reshape.397) | copy-start | bytes 1572868
  98.5 19.7 %collective-permute-start.2 = (f32[16,8320]{1,0:T(8,128)}, f32[16,8320]{1,0:T(8,128)S(1)}, u32[]{:S(2)}, u32[]{:S(2)}) collective-permute-start(f32[16,8320]{1,0:T(8,128)} %pad_maximum_fusion.6), channel_id=1, source_target_pairs={{0,4},{4,8},{8,12},{1,5},{5,9},{9,13},{2,6},{6,10},{10,14},{3,7},{... | collective-permute-start | bytes 1597448 | tf_op jit(solution)/shard_map/ppermute | solution.py:25
  112.7 3.1 %copy-start.64 = (f32[16]{0:T(128)S(1)}, f32[16]{0:T(128)}, u32[]{:S(2)}) copy-start(f32[16]{0:T(128)} %exp.142) | copy-start | bytes 196
  116.9 16.5 %collective-permute-start.5 = (f32[16,8320]{1,0:T(8,128)}, f32[16,8320]{1,0:T(8,128)}, u32[]{:S(2)}, u32[]{:S(2)}) collective-permute-start(f32[16,8320]{1,0:T(8,128)} %pad_maximum_fusion.9), channel_id=1, source_target_pairs={{8,0},{12,4},{9,1},{13,5},{10,2},{14,6},{11,3},{15,7},{24,16},{28,... | collective-permute-start | bytes 1597448 | tf_op jit(solution)/shard_map/ppermute | solution.py:25
  119.8 14.9 %copy-start.10 = (f32[4,16,64,128]{3,2,1,0:T(8,128)S(1)}, f32[4,16,64,128]{3,2,1,0:T(8,128)}, u32[]{:S(2)}) copy-start(f32[4,16,64,128]{3,2,1,0:T(8,128)} %shard_map.148) | copy-start | bytes 6291460
  119.8 14.9 %copy-start.60 = (f32[16]{0:T(128)S(1)}, f32[16]{0:T(128)}, u32[]{:S(2)}) copy-start(f32[16]{0:T(128)} %get-tuple-element.74) | copy-start | bytes 196
  119.8 14.9 %copy-start.61 = (f32[16]{0:T(128)S(1)}, f32[16]{0:T(128)}, u32[]{:S(2)}) copy-start(f32[16]{0:T(128)} %get-tuple-element.75) | copy-start | bytes 196
  119.8 14.9 %copy-start.62 = (f32[16]{0:T(128)S(1)}, f32[16]{0:T(128)}, u32[]{:S(2)}) copy-start(f32[16]{0:T(128)} %get-tuple-element.77) | copy-start | bytes 196
  119.8 18.8 %collective-permute-start.3 = (f32[16,8320]{1,0:T(8,128)}, f32[16,8320]{1,0:T(8,128)}, u32[]{:S(2)}, u32[]{:S(2)}) collective-permute-start(f32[16,8320]{1,0:T(8,128)} %pad_maximum_fusion.7), channel_id=1, source_target_pairs={{0,8},{4,12},{1,9},{5,13},{2,10},{6,14},{3,11},{7,15},{16,24},{20,... | collective-permute-start | bytes 1597448 | tf_op jit(solution)/shard_map/ppermute | solution.py:25
  135.3 3.3 %copy-start.21 = (f32[16,8320]{1,0:T(8,128)S(1)}, f32[16,8320]{1,0:T(8,128)}, u32[]{:S(2)}) copy-start(f32[16,8320]{1,0:T(8,128)} %copy-done.20) | copy-start | bytes 1597444
  141.6 3.3 %copy-start.16 = (f32[4,128,512]{2,1,0:T(8,128)S(1)}, f32[4,128,512]{2,1,0:T(8,128)}, u32[]{:S(2)}) copy-start(f32[4,128,512]{2,1,0:T(8,128)} %fusion.31) | copy-start | bytes 3145732
  141.6 3.3 %copy-start.17 = (f32[4,128,512]{2,1,0:T(8,128)S(1)}, f32[4,128,512]{2,1,0:T(8,128)}, u32[]{:S(2)}) copy-start(f32[4,128,512]{2,1,0:T(8,128)} %fusion.30) | copy-start | bytes 3145732
  146.3 3.1 %copy-start.3 = (bf16[512,16,128]{0,2,1:T(8,128)(2,1)S(1)}, bf16[512,16,128]{0,2,1:T(8,128)(2,1)}, u32[]{:S(2)}) copy-start(bf16[512,16,128]{0,2,1:T(8,128)(2,1)} %rev.9) | copy-start | bytes 6291460
  146.3 3.1 %copy-start.9 = (bf16[512,1024]{0,1:T(8,128)(2,1)S(1)}, bf16[512,1024]{0,1:T(8,128)(2,1)}, u32[]{:S(2)}) copy-start(bf16[512,1024]{0,1:T(8,128)(2,1)} %copy-done.8) | copy-start | bytes 3145732
  146.3 3.1 %copy-start.31 = (f32[512,16]{0,1:T(8,128)S(1)}, f32[512,16]{0,1:T(8,128)}, u32[]{:S(2)}) copy-start(f32[512,16]{0,1:T(8,128)} %copy_bitcast_fusion.2) | copy-start | bytes 98308
  149.4 8.0 %copy-start.18 = (f32[4,128,512]{2,1,0:T(8,128)S(1)}, f32[4,128,512]{2,1,0:T(8,128)}, u32[]{:S(2)}) copy-start(f32[4,128,512]{2,1,0:T(8,128)} %fusion.33) | copy-start | bytes 3145732
  149.4 8.0 %copy-start.19 = (f32[4,128,512]{2,1,0:T(8,128)S(1)}, f32[4,128,512]{2,1,0:T(8,128)}, u32[]{:S(2)}) copy-start(f32[4,128,512]{2,1,0:T(8,128)} %fusion.32) | copy-start | bytes 3145732
  159.0 3.1 %copy-start.7 = (bf16[512,1024]{0,1:T(8,128)(2,1)S(1)}, bf16[512,1024]{0,1:T(8,128)(2,1)}, u32[]{:S(2)}) copy-start(bf16[512,1024]{0,1:T(8,128)(2,1)} %copy-done.6) | copy-start | bytes 3145732
  162.0 6.6 %copy-start.14 = (f32[512,1024]{0,1:T(8,128)S(1)}, f32[512,1024]{0,1:T(8,128)}, u32[]{:S(2)}) copy-start(f32[512,1024]{0,1:T(8,128)} %get-tuple-element.69) | copy-start | bytes 6291460
  162.0 6.6 %copy-start.52 = (f32[1024]{0:T(1024)S(1)}, f32[1024]{0:T(1024)}, u32[]{:S(2)}) copy-start(f32[1024]{0:T(1024)} %param.28) | copy-start | bytes 12292
  173.4 46.6 %copy-start.1 = (bf16[2048,512]{1,0:T(8,128)(2,1)S(1)}, bf16[2048,512]{1,0:T(8,128)(2,1)}, u32[]{:S(2)}) copy-start(bf16[2048,512]{1,0:T(8,128)(2,1)} %param.19) | copy-start | bytes 6291460
  (27 other events, 51.1 us)
Sparse Core Ops, SparseCore 0:
  175.0 44.9 reduce-scatter.1
where the time goes:
time: 228 us; the launch traced here: 227 us
  waiting for transfers between devices  52.3 us (23%)
  matrix products  47.7 us (21%)
  local copies, waits for them, and re-layouts  38.9 us (17%)
  Pallas kernels  28.9 us (13%)
  other arithmetic  26.3 us (12%)
  starting transfers between devices  18.3 us (8%)
  between operations  14.3 us (6%)
    reduce_scatter x1, waiting for transfers between devices, on_device(): summed = lax.psum_scatter(partial, 'chan', scatter_dimension=0, tiled=True)  45.1 us
    ppermute x6, starting transfers between devices, shifted(): return lax.ppermute(value, axis, pairs)  18.3 us
    pallas_call x2, Pallas kernels, block_intra(): pl.pallas_call(kernel, grid=(blocks, groups), in_specs=[pl.BlockSpec((Q,...  15.6 us
    dot_general x2, matrix products, project(): gate_in = jnp.dot(source, w_gate, preferred_element_type=F32).astype(BF16)  14.6 us
    pallas_call x2, Pallas kernels, block_states(): pl.pallas_call(kernel, grid=(blocks, groups), in_specs=[pl.BlockSpec((Q,...  13.3 us
    convert_element_type x2, other arithmetic, conv_silu(): return jax.nn.silu(total).astype(BF16)  10.7 us
    dot_general x2, matrix products, project(): jnp.dot(source, w_values, preferred_element_type=F32) * known[:, None]  9.72 us
    ppermute x6, waiting for transfers between devices, shifted(): return lax.ppermute(value, axis, pairs)  7.24 us
  transfers between devices with their start and end apart: 7, of which 2 were waited for; matrix products, arithmetic and copies ran while one was open for 23% of the time, Pallas kernels for 10%

commit v1 on v0

--- a/solution.py
+++ b/solution.py
@@ -32,9 +32,19 @@
     size = flat.shape[1]
 
     def send(log, st, distance):
-        packed = jnp.concatenate([st, jnp.broadcast_to(log[:, None], (heads, LANE))], axis=1)
+        log_hi = log.astype(BF16)
+        log_lo = (log - log_hi.astype(F32)).astype(BF16)
+        packed = jnp.concatenate(
+            [
+                st.astype(BF16),
+                jnp.broadcast_to(log_hi[:, None], (heads, LANE)),
+                jnp.broadcast_to(log_lo[:, None], (heads, LANE)),
+            ],
+            axis=1,
+        )
         got = shifted(packed, "seq", sign * distance)
-        return got[:, size], got[:, :size]
+        got_log = got[:, size].astype(F32) + got[:, size + LANE].astype(F32)
+        return got_log, got[:, :size].astype(F32)
 
     got_log, got_state = send(total_log, flat, 1)
     x_log, x_state = got_log, got_state

time: 228 us -> 227 us (level)
  waiting for transfers between devices: 52.3 us -> 46.3 us
  local copies, waits for them, and re-layouts: 38.9 us -> 43.9 us
    ppermute x6, waiting for transfers between devices: 7.24 us -> 1.77 us  [shifted(): return lax.ppermute(value, axis, pairs)]
    unnamed x144 -> x140, local copies, waits for them, and re-layouts: 4.75 us -> 10 us
    convert_element_type x0 -> x4, other arithmetic: none -> 4.42 us  [send(): st.astype(BF16)]
    another operation x2, local copies, waits for them, and re-layouts: 0.17 us -> 3.85 us  [local_scan(): jnp.stack([local_start[index] + entering[index][:, None, None] * carried...]
    convert_element_type x2, other arithmetic: 10.7 us -> 7.99 us  [conv_silu(): return jax.nn.silu(total).astype(BF16)]
    add x4 -> x0, other arithmetic: 2.64 us -> none  [the longest x2 2.4 us: local_scan(): running = block_decay[index][:, None, None] * running + states[index]]
  transfers between devices with their start and end apart: 7 -> 7, of which waited for: 2 -> 2; matrix products, arithmetic and copies ran while one was open for 23% -> 25% of each run, Pallas kernels for 10% -> 10%
where the time goes in v1:
time: 227 us; the launch traced here: 225 us
  matrix products  46.4 us (20%)
  waiting for transfers between devices  46.3 us (20%)
  local copies, waits for them, and re-layouts  43.9 us (19%)
  Pallas kernels  29 us (13%)
  other arithmetic  27.5 us (12%)
  starting transfers between devices  18 us (8%)
  between operations  14.3 us (6%)
    reduce_scatter x1, waiting for transfers between devices, on_device(): summed = lax.psum_scatter(partial, 'chan', scatter_dimension=0, tiled=True)  44.5 us
    ppermute x6, starting transfers between devices, shifted(): return lax.ppermute(value, axis, pairs)  18 us
    pallas_call x2, Pallas kernels, block_intra(): pl.pallas_call(kernel, grid=(blocks, groups), in_specs=[pl.BlockSpec((Q,...  15.6 us
    dot_general x2, matrix products, project(): gate_in = jnp.dot(source, w_gate, preferred_element_type=F32).astype(BF16)  14.8 us
    pallas_call x2, Pallas kernels, block_states(): pl.pallas_call(kernel, grid=(blocks, groups), in_specs=[pl.BlockSpec((Q,...  13.3 us
    unnamed x140, local copies, waits for them, and re-layouts  10 us
    dot_general x2, matrix products, project(): jnp.dot(source, w_values, preferred_element_type=F32) * known[:, None]  9.72 us
    convert_element_type x2, other arithmetic, conv_silu(): return jax.nn.silu(total).astype(BF16)  7.99 us
  transfers between devices with their start and end apart: 7, of which 2 were waited for; matrix products, arithmetic and copies ran while one was open for 25% of the time, Pallas kernels for 10%

profile of v1, /device:TPU:0, one launch (start us, length us, event | category | flops | bytes accessed | tf_op | source)
XLA Modules:
  0.0 225.4 jit_solution(17541947474698325931)
XLA Ops:
  8.3 1.3 collective-permute-start.1
  9.7 3.0 %collective-permute-start = (bf16[3,2176]{1,0:T(4,128)(2,1)S(1)}, bf16[3,2176]{1,0:T(4,128)(2,1)S(1)}, u32[]{:S(2)}, u32[]{:S(2)}) collective-permute-start(bf16[3,2176]{1,0:T(4,128)(2,1)S(1)} %pad_maximum_fusion.15), channel_id=1, source_target_pairs={{0,4},{4,8},{8,12},{1,5},{5,9},{9,13},{2,6},{6,10},{10,14},{3,7},{... | collective-permute-start | bytes 39176 | tf_op jit(solution)/shard_map/ppermute | solution.py:25
  12.8 3.6 %convert_bitcast_fusion = bf16[512,16,128]{0,2,1:T(8,128)(2,1)} fusion(bf16[512,2048]{1,0:T(8,128)(2,1)} %param.15), kind=kOutput, calls=%fused_computation.38 | convolution fusion | flops 269516800 | bytes 4194304 | tf_op jit(solution)/shard_map/rki,ij->rkj/dot_general | solution.py:189
  16.4 3.1 %rev.9 = bf16[512,16,128]{0,2,1:T(8,128)(2,1)} reverse(bf16[512,16,128]{0,2,1:T(8,128)(2,1)} %convert_bitcast_fusion), dimensions={1} | reverse | bytes 4194304 | tf_op jit(solution)/shard_map/jit(_flip)/rev | solution.py:192
  19.5 6.3 %multiply_convert_fusion.3 = bf16[512,1024]{0,1:T(8,128)(2,1)} fusion(bf16[512,2048]{1,0:T(8,128)(2,1)} %param.15, bf16[2048,1024]{1,0:T(8,128)(2,1)} %param.18, f32[512]{0:T(512)S(1)} %get-tuple-element.63), kind=kOutput, calls=%fused_computation.40 | convolution fusion | flops 2148532224 | bytes 7342080 | tf_op jit(solution)/shard_map/dot_general | solution.py:211
  25.9 3.4 %multiply_convert_fusion.1 = bf16[512,1024]{0,1:T(8,128)(2,1)} fusion(bf16[512,2048]{0,1:T(8,128)(2,1)S(1)} %bitcast.311, bf16[2048,1024]{1,0:T(8,128)(2,1)S(1)} %copy-done.13, f32[512]{0:T(512)S(1)} %get-tuple-element.63), kind=kOutput, calls=%fused_computation.37 | convolution fusion | flops 2148532224 | bytes 7342080 | tf_op jit(solution)/shard_map/dot_general | solution.py:211
  29.3 1.3 convolution_convert_fusion.3
  30.9 1.3 convolution_convert_fusion.4
  32.6 1.3 broadcast_multiply_fusion.1
  41.5 4.1 %fusion.21 = bf16[6,1024]{0,1:T(8,128)(2,1)S(1)} fusion(bf16[2048,1024]{1,0:T(8,128)(2,1)} %param.18, f32[6]{0:T(128)S(1)} %maximum_convert_fusion, bf16[3,2048]{1,0:T(4,128)(2,1)S(1)} %bitcast.354, bf16[3,2048]{1,0:T(4,128)(2,1)S(1)} %slice.307), kind=kOutput, calls=%fused_computation.54 | convolution fusion | flops 25227264 | bytes 4231192 | tf_op jit(solution)/shard_map/dot_general | solution.py:205
  45.8 5.6 %multiply_convert_fusion.2 = (bf16[512,1024]{0,1:T(8,128)(2,1)}, bf16[512,1024]{0,1:T(8,128)(2,1)}) fusion(bf16[512,1024]{0,1:T(8,128)(2,1)S(1)} %copy-done.27, bf16[3,1024]{0,1:T(8,128)(2,1)S(1)} %get-tuple-element.45, f32[1024]{0:T(1024)S(1)} %bitcast.358, f32[1024]{0:T(1024)S(1)} %bitcast.359, f32[1024]{0:T(1024)S(1)} %bitcast.357, ...), kind=kLoop, calls=%fused_computation.39 | loop fusion | flops 27262976 | bytes 4227072 | tf_op jit(solution)/shard_map/convert_element_type | solution.py:157
  51.4 2.4 %multiply_convert_fusion.5 = (bf16[512,512]{1,0:T(8,128)(2,1)}, bf16[512,512]{1,0:T(8,128)(2,1)}) fusion(bf16[512,512]{1,0:T(8,128)(2,1)S(1)} %convolution_convert_fusion.4, bf16[3,512]{1,0:T(4,128)(2,1)S(1)} %get-tuple-element.55, f32[512]{0:T(512)S(1)} %bitcast.362, f32[512]{0:T(512)S(1)} %bitcast.363, f32[512]{0:T(512)S(1)} %bitcast.361, ...), kind=kLoop, calls=%fused_computation.80 | loop fusion | flops 13631488 | bytes 2113536 | tf_op jit(solution)/shard_map/convert_element_type | solution.py:157
  53.8 6.7 %shard_map.148 = f32[4,16,64,128]{3,2,1,0:T(8,128)} custom-call(bf16[512,512]{1,0:T(8,128)(2,1)} %get-tuple-element.54.c_ref.b_ref, bf16[1024,512]{1,0:T(8,128)(2,1)} %bitcast.316, f32[2,8,512]{2,1,0:T(8,128)} %bitcast.349, f32[2,8,512]{2,1,0:T(8,128)} %bitcast.343), custom_call_target="tpu_custom_call" | custom-call | tf_op jit(solution)/shard_map/pallas_call | solution.py:93
  60.5 1.8 fusion.81
  62.3 2.1 fusion.79
  65.2 1.3 collective-permute-start.4
  66.5 6.7 %shard_map.146 = f32[4,16,64,128]{3,2,1,0:T(8,128)} custom-call(bf16[512,512]{1,0:T(8,128)(2,1)} %get-tuple-element.53.c_ref.b_ref, bf16[1024,512]{1,0:T(8,128)(2,1)} %bitcast.315, f32[2,8,512]{2,1,0:T(8,128)} %bitcast.346, f32[2,8,512]{2,1,0:T(8,128)} %bitcast.351), custom_call_target="tpu_custom_call" | custom-call | tf_op jit(solution)/shard_map/pallas_call | solution.py:93
  73.2 1.7 fusion.80
  75.0 2.1 fusion.78
  78.9 1.3 copy.188.x_ref
  80.4 1.3 copy.172.x_ref
  83.0 7.8 %shard_map.147 = f32[512,1024]{1,0:T(8,128)} custom-call(bf16[512,512]{1,0:T(8,128)(2,1)} %get-tuple-element.54.c_ref.b_ref, bf16[512,512]{1,0:T(8,128)(2,1)} %get-tuple-element.54.c_ref.b_ref, bf16[512,1024]{1,0:T(8,128)(2,1)} %copy.188.x_ref, f32[2,512,8]{2,1,0:T(8,128)} %copy.189.a_ref, f32[2,8,512]{2,1,0:T(8,128)} %bitcast.350, f32[2,8,512]{2,1,0:T(8,128)} %bitcast.344), custom_call_target="tpu_custom_call" | custom-call | tf_op jit(solution)/shard_map/pallas_call | solution.py:134
  90.8 2.9 %copy.198 = f32[512,1024]{0,1:T(8,128)} copy(f32[512,1024]{1,0:T(8,128)} %shard_map.147) | data formatting | bytes 4194304 | tf_op jit(solution)/shard_map/pallas_call | solution.py:134
  93.7 5.1 %collective-permute-start.2 = (bf16[16,8448]{1,0:T(8,128)(2,1)}, bf16[16,8448]{1,0:T(8,128)(2,1)S(1)}, u32[]{:S(2)}, u32[]{:S(2)}) collective-permute-start(bf16[16,8448]{1,0:T(8,128)(2,1)} %pad_maximum_fusion.8), channel_id=1, source_target_pairs={{0,4},{4,8},{8,12},{1,5},{5,9},{9,13},{2,6},{6,10},{10,14},{3,7},{... | collective-permute-start | bytes 811016 | tf_op jit(solution)/shard_map/ppermute | solution.py:25
  100.2 7.8 %shard_map.145 = f32[512,1024]{1,0:T(8,128)} custom-call(bf16[512,512]{1,0:T(8,128)(2,1)} %get-tuple-element.53.c_ref.b_ref, bf16[512,512]{1,0:T(8,128)(2,1)} %get-tuple-element.53.c_ref.b_ref, bf16[512,1024]{1,0:T(8,128)(2,1)} %copy.172.x_ref, f32[2,512,8]{2,1,0:T(8,128)} %copy.173.a_ref, f32[2,8,512]{2,1,0:T(8,128)} %bitcast.347, f32[2,8,512]{2,1,0:T(8,128)} %bitcast.352), custom_call_target="tpu_custom_call" | custom-call | tf_op jit(solution)/shard_map/pallas_call | solution.py:134
  108.0 3.0 %copy.182 = f32[512,1024]{0,1:T(8,128)} copy(f32[512,1024]{1,0:T(8,128)} %shard_map.145) | data formatting | bytes 4194304 | tf_op jit(solution)/shard_map/pallas_call | solution.py:134
  112.3 1.3 collective-permute-start.5
  115.4 6.0 %collective-permute-start.3 = (bf16[16,8448]{1,0:T(8,128)(2,1)}, bf16[16,8448]{1,0:T(8,128)(2,1)}, u32[]{:S(2)}, u32[]{:S(2)}) collective-permute-start(bf16[16,8448]{1,0:T(8,128)(2,1)} %pad_maximum_fusion.9), channel_id=1, source_target_pairs={{0,8},{4,12},{1,9},{5,13},{2,10},{6,14},{3,11},{7,15},{16,24},{20,... | collective-permute-start | bytes 811016 | tf_op jit(solution)/shard_map/ppermute | solution.py:25
  121.4 1.8 collective-permute-done.5
  123.1 1.9 convert_add_fusion
  125.0 1.9 stack.36
  126.9 1.1 copy.233
  130.1 1.6 fusion.31
  131.7 1.6 fusion.30
  133.3 2.0 convert_add_fusion.1
  135.4 2.0 stack.28
  140.5 1.6 fusion.33
  142.1 1.6 fusion.32
  143.8 1.5 pad_maximum_fusion.3
  145.2 3.0 %copy.209 = f32[512,1024]{0,1:T(8,128)} copy(f32[512,1024]{1,0:T(8,128)} %bitcast.318) | data formatting | bytes 4194304 | tf_op jit(solution)/shard_map/reshape | solution.py:269
  148.3 8.2 %bitcast_reduce_fusion = (f32[512,2]{0,1:T(2,128)S(1)}, f32[512,1024]{0,1:T(8,128)}) fusion(bf16[512,2048]{0,1:T(8,128)(2,1)S(1)} %bitcast.314, bf16[2048,1024]{1,0:T(8,128)(2,1)} %param.17, bf16[512,1024]{0,1:T(8,128)(2,1)} %get-tuple-element.48, f32[1024]{0:T(1024)S(1)} %mul.591, f32[512,1024]{0,1:T(8,128)} %copy.198, f32[512,1024]{0,1:T(8,128)} %copy.209, ...), kind=kOutput, calls=%fused_computation.24 | convolution fusion | flops 2154822656 | bytes 13672448 | tf_op jit(solution)/shard_map/dot_general | solution.py:210
  156.6 1.5 pad_maximum_fusion.1
  158.0 3.1 %copy.208 = f32[512,1024]{0,1:T(8,128)} copy(f32[512,1024]{1,0:T(8,128)} %bitcast.319) | data formatting | bytes 4194304 | tf_op jit(solution)/shard_map/reshape | solution.py:269
  161.1 6.6 %bitcast_reduce_fusion.1 = (f32[512,2]{0,1:T(2,128)S(1)}, f32[512,1024]{0,1:T(8,128)S(1)}) fusion(bf16[512,2048]{1,0:T(8,128)(2,1)S(1)} %copy-done.5, bf16[2048,1024]{1,0:T(8,128)(2,1)} %param.17, bf16[512,1024]{0,1:T(8,128)(2,1)S(1)} %copy-done.6, f32[1024]{0:T(1024)S(1)} %mul.591, f32[512,1024]{0,1:T(8,128)} %copy.182, f32[512,1024]{0,1:T(8,128)} %copy.208, ...), kind=kOutput, calls=%fused_computation.31 | convolution fusion | flops 2154822656 | bytes 13672448 | tf_op jit(solution)/shard_map/dot_general | solution.py:210
  168.2 1.8 copy-done.63
  169.9 2.5 %convolution_convert_fusion = bf16[512,2048]{1,0:T(8,128)(2,1)S(1)} fusion(bf16[1024,2048]{1,0:T(8,128)(2,1)S(1)} %copy-done.63, bf16[512,1024]{0,1:T(8,128)(2,1)S(1)} %get-tuple-element.62, bf16[512,1024]{0,1:T(8,128)(2,1)S(1)} %get-tuple-element.61), kind=kOutput, calls=%fused_computation | convolution fusion | flops 2150629376 | bytes 8388608 | tf_op jit(solution)/shard_map/dot_general | solution.py:281
  172.4 1.5 copy.274
  174.0 44.5 %reduce-scatter.2.cloned.1.call-done = bf16[1,512,512]{2,1,0:T(8,128)(2,1)} async-done(((bf16[4,512,512]{2,1,0:T(8,128)(2,1)}), bf16[1,512,512]{2,1,0:T(8,128)(2,1)}) %reduce-scatter.2.cloned.1.call-update) | async-done | bytes 524304 | tf_op jit(solution)/shard_map/reduce_scatter | solution.py:283
  (216 shorter events, 24.2 us)
Async XLA Ops:
  6.5 22.7 %copy-start = (bf16[2048,512]{1,0:T(8,128)(2,1)S(1)}, bf16[2048,512]{1,0:T(8,128)(2,1)}, u32[]{:S(2)}) copy-start(bf16[2048,512]{1,0:T(8,128)(2,1)} %param.19) | copy-start | bytes 6291460
  6.5 212.0 %reduce-scatter.2.cloned.1.call-start = ((), (), s32[]{:S(2)}) async-start(), calls=%async_computation.1 | async-start | bytes 2621440 | tf_op jit(solution)/shard_map/reduce_scatter | solution.py:283
  8.3 32.3 %collective-permute-start.1 = (bf16[3,2176]{1,0:T(4,128)(2,1)S(1)}, bf16[3,2176]{1,0:T(4,128)(2,1)S(1)}, u32[]{:S(2)}, u32[]{:S(2)}) collective-permute-start(bf16[3,2176]{1,0:T(4,128)(2,1)S(1)} %pad_maximum_fusion.16), channel_id=1, source_target_pairs={{4,0},{8,4},{12,8},{5,1},{9,5},{13,9},{6,2},{10,6},{14,10},{7,3},{... | collective-permute-start | bytes 39176 | tf_op jit(solution)/shard_map/ppermute | solution.py:25
  9.7 31.2 %collective-permute-start = (bf16[3,2176]{1,0:T(4,128)(2,1)S(1)}, bf16[3,2176]{1,0:T(4,128)(2,1)S(1)}, u32[]{:S(2)}, u32[]{:S(2)}) collective-permute-start(bf16[3,2176]{1,0:T(4,128)(2,1)S(1)} %pad_maximum_fusion.15), channel_id=1, source_target_pairs={{0,4},{4,8},{8,12},{1,5},{5,9},{9,13},{2,6},{6,10},{10,14},{3,7},{... | collective-permute-start | bytes 39176 | tf_op jit(solution)/shard_map/ppermute | solution.py:25
  19.5 6.4 %copy-start.2 = (bf16[512,16,128]{0,2,1:T(8,128)(2,1)S(1)}, bf16[512,16,128]{0,2,1:T(8,128)(2,1)}, u32[]{:S(2)}) copy-start(bf16[512,16,128]{0,2,1:T(8,128)(2,1)} %rev.9) | copy-start | bytes 6291460
  19.5 6.4 %copy-start.13 = (bf16[2048,1024]{1,0:T(8,128)(2,1)S(1)}, bf16[2048,1024]{1,0:T(8,128)(2,1)}, u32[]{:S(2)}) copy-start(bf16[2048,1024]{1,0:T(8,128)(2,1)} %param.18) | copy-start | bytes 12582916
  32.6 8.0 %copy-start.29 = (f32[512,16]{0,1:T(8,128)}, f32[512,16]{0,1:T(8,128)S(1)}, u32[]{:S(2)}) copy-start(f32[512,16]{0,1:T(8,128)S(1)} %compare_select_fusion) | copy-start | bytes 98308
  32.6 6.7 %copy-start.62 = (f32[16]{0:T(128)S(1)}, f32[16]{0:T(128)}, u32[]{:S(2)}) copy-start(f32[16]{0:T(128)} %param.27) | copy-start | bytes 196
  35.4 26.9 %copy-start.41 = (f32[16]{0:T(128)}, f32[16]{0:T(128)S(1)}, u32[]{:S(2)}) copy-start(f32[16]{0:T(128)S(1)} %get-tuple-element.18) | copy-start | bytes 196
  35.4 26.9 %copy-start.43 = (f32[16]{0:T(128)}, f32[16]{0:T(128)S(1)}, u32[]{:S(2)}) copy-start(f32[16]{0:T(128)S(1)} %get-tuple-element.19) | copy-start | bytes 196
  35.4 26.9 %copy-start.45 = (f32[16]{0:T(128)}, f32[16]{0:T(128)S(1)}, u32[]{:S(2)}) copy-start(f32[16]{0:T(128)S(1)} %get-tuple-element.20) | copy-start | bytes 196
  38.3 7.3 %copy-start.31 = (f32[512,2,8]{0,2,1:T(8,128)}, f32[512,2,8]{0,2,1:T(8,128)S(1)}, u32[]{:S(2)}) copy-start(f32[512,2,8]{0,2,1:T(8,128)S(1)} %reshape_reshape.7) | copy-start | bytes 98308
  39.5 6.1 %copy-start.30 = (f32[512,2,8]{0,2,1:T(8,128)}, f32[512,2,8]{0,2,1:T(8,128)S(1)}, u32[]{:S(2)}) copy-start(f32[512,2,8]{0,2,1:T(8,128)S(1)} %reshape_reshape.6) | copy-start | bytes 98308
  41.5 4.3 %copy-start.27 = (bf16[512,1024]{0,1:T(8,128)(2,1)S(1)}, bf16[512,1024]{0,1:T(8,128)(2,1)}, u32[]{:S(2)}) copy-start(bf16[512,1024]{0,1:T(8,128)(2,1)} %multiply_convert_fusion.3) | copy-start | bytes 3145732
  41.5 4.3 %copy-start.28 = (bf16[512,1024]{0,1:T(8,128)(2,1)S(1)}, bf16[512,1024]{0,1:T(8,128)(2,1)}, u32[]{:S(2)}) copy-start(bf16[512,1024]{0,1:T(8,128)(2,1)} %multiply_convert_fusion.1) | copy-start | bytes 3145732
  41.5 4.3 %copy-start.47 = (f32[1024]{0:T(1024)S(1)}, f32[1024]{0:T(1024)}, u32[]{:S(2)}) copy-start(f32[1024]{0:T(1024)} %param.22) | copy-start | bytes 12292
  45.8 5.6 %copy-start.49 = (f32[512]{0:T(512)S(1)}, f32[512]{0:T(512)}, u32[]{:S(2)}) copy-start(f32[512]{0:T(512)} %param.24) | copy-start | bytes 6148
  65.2 45.8 %collective-permute-start.4 = (bf16[16,8448]{1,0:T(8,128)(2,1)}, bf16[16,8448]{1,0:T(8,128)(2,1)S(1)}, u32[]{:S(2)}, u32[]{:S(2)}) collective-permute-start(bf16[16,8448]{1,0:T(8,128)(2,1)} %pad_maximum_fusion.10), channel_id=1, source_target_pairs={{4,0},{8,4},{12,8},{5,1},{9,5},{13,9},{6,2},{10,6},{14,10},{7,3},{... | collective-permute-start | bytes 811016 | tf_op jit(solution)/shard_map/ppermute | solution.py:25
  75.0 3.9 %copy-start.7 = (bf16[512,1024]{0,1:T(8,128)(2,1)S(1)}, bf16[512,1024]{0,1:T(8,128)(2,1)}, u32[]{:S(2)}) copy-start(bf16[512,1024]{0,1:T(8,128)(2,1)} %get-tuple-element.48) | copy-start | bytes 3145732
  77.0 3.2 %copy-start.10 = (bf16[512,512]{1,0:T(8,128)(2,1)S(1)}, bf16[512,512]{1,0:T(8,128)(2,1)}, u32[]{:S(2)}) copy-start(bf16[512,512]{1,0:T(8,128)(2,1)} %get-tuple-element.53.c_ref.b_ref) | copy-start | bytes 1572868
  93.7 19.9 %collective-permute-start.2 = (bf16[16,8448]{1,0:T(8,128)(2,1)}, bf16[16,8448]{1,0:T(8,128)(2,1)S(1)}, u32[]{:S(2)}, u32[]{:S(2)}) collective-permute-start(bf16[16,8448]{1,0:T(8,128)(2,1)} %pad_maximum_fusion.8), channel_id=1, source_target_pairs={{0,4},{4,8},{8,12},{1,5},{5,9},{9,13},{2,6},{6,10},{10,14},{3,7},{... | collective-permute-start | bytes 811016 | tf_op jit(solution)/shard_map/ppermute | solution.py:25
  108.0 3.3 %copy-start.37 = (f32[16]{0:T(128)S(1)}, f32[16]{0:T(128)}, u32[]{:S(2)}) copy-start(f32[16]{0:T(128)} %copy-done.36) | copy-start | bytes 196
  108.0 3.3 %copy-start.19 = (f32[16,8192]{1,0:T(8,128)S(1)}, f32[16,8192]{1,0:T(8,128)}, u32[]{:S(2)}) copy-start(f32[16,8192]{1,0:T(8,128)} %get-tuple-element.24) | copy-start | bytes 1572868
  108.0 3.3 %copy-start.52 = (f32[16]{0:T(128)S(1)}, f32[16]{0:T(128)}, u32[]{:S(2)}) copy-start(f32[16]{0:T(128)} %get-tuple-element.78) | copy-start | bytes 196
  108.0 6.3 %copy-start.18 = (f32[16,8192]{1,0:T(8,128)S(1)}, f32[16,8192]{1,0:T(8,128)}, u32[]{:S(2)}) copy-start(f32[16,8192]{1,0:T(8,128)} %get-tuple-element.22) | copy-start | bytes 1572868
  108.0 6.3 %copy-start.51 = (f32[16]{0:T(128)S(1)}, f32[16]{0:T(128)}, u32[]{:S(2)}) copy-start(f32[16]{0:T(128)} %get-tuple-element.73) | copy-start | bytes 196
  112.3 10.8 %collective-permute-start.5 = (bf16[16,8448]{1,0:T(8,128)(2,1)}, bf16[16,8448]{1,0:T(8,128)(2,1)}, u32[]{:S(2)}, u32[]{:S(2)}) collective-permute-start(bf16[16,8448]{1,0:T(8,128)(2,1)} %pad_maximum_fusion.11), channel_id=1, source_target_pairs={{8,0},{12,4},{9,1},{13,5},{10,2},{14,6},{11,3},{15,7},{24,16},{28,... | collective-permute-start | bytes 811016 | tf_op jit(solution)/shard_map/ppermute | solution.py:25
  114.5 13.6 %copy-start.9 = (f32[4,16,64,128]{3,2,1,0:T(8,128)S(1)}, f32[4,16,64,128]{3,2,1,0:T(8,128)}, u32[]{:S(2)}) copy-start(f32[4,16,64,128]{3,2,1,0:T(8,128)} %shard_map.148) | copy-start | bytes 6291460
  114.5 13.6 %copy-start.42 = (f32[16]{0:T(128)S(1)}, f32[16]{0:T(128)}, u32[]{:S(2)}) copy-start(f32[16]{0:T(128)} %copy-done.41) | copy-start | bytes 196
  114.5 13.6 %copy-start.44 = (f32[16]{0:T(128)S(1)}, f32[16]{0:T(128)}, u32[]{:S(2)}) copy-start(f32[16]{0:T(128)} %copy-done.43) | copy-start | bytes 196
  114.5 13.6 %copy-start.46 = (f32[16]{0:T(128)S(1)}, f32[16]{0:T(128)}, u32[]{:S(2)}) copy-start(f32[16]{0:T(128)} %copy-done.45) | copy-start | bytes 196
  114.5 13.6 %copy-start.59 = (f32[16]{0:T(128)S(1)}, f32[16]{0:T(128)}, u32[]{:S(2)}) copy-start(f32[16]{0:T(128)} %get-tuple-element.90) | copy-start | bytes 196
  114.5 13.6 %copy-start.60 = (f32[16]{0:T(128)S(1)}, f32[16]{0:T(128)}, u32[]{:S(2)}) copy-start(f32[16]{0:T(128)} %get-tuple-element.91) | copy-start | bytes 196
  114.5 13.6 %copy-start.61 = (f32[16]{0:T(128)S(1)}, f32[16]{0:T(128)}, u32[]{:S(2)}) copy-start(f32[16]{0:T(128)} %get-tuple-element.93) | copy-start | bytes 196
  115.4 17.9 %collective-permute-start.3 = (bf16[16,8448]{1,0:T(8,128)(2,1)}, bf16[16,8448]{1,0:T(8,128)(2,1)}, u32[]{:S(2)}, u32[]{:S(2)}) collective-permute-start(bf16[16,8448]{1,0:T(8,128)(2,1)} %pad_maximum_fusion.9), channel_id=1, source_target_pairs={{0,8},{4,12},{1,9},{5,13},{2,10},{6,14},{3,11},{7,15},{16,24},{20,... | collective-permute-start | bytes 811016 | tf_op jit(solution)/shard_map/ppermute | solution.py:25
  130.1 3.3 %copy-start.24 = (bf16[16,8448]{1,0:T(8,128)(2,1)S(1)}, bf16[16,8448]{1,0:T(8,128)(2,1)}, u32[]{:S(2)}) copy-start(bf16[16,8448]{1,0:T(8,128)(2,1)} %copy-done.23) | copy-start | bytes 811012
  133.3 5.2 %copy-start.8 = (f32[4,16,64,128]{3,2,1,0:T(8,128)S(1)}, f32[4,16,64,128]{3,2,1,0:T(8,128)}, u32[]{:S(2)}) copy-start(f32[4,16,64,128]{3,2,1,0:T(8,128)} %shard_map.146) | copy-start | bytes 6291460
  133.3 5.2 %copy-start.56 = (f32[16]{0:T(128)S(1)}, f32[16]{0:T(128)}, u32[]{:S(2)}) copy-start(f32[16]{0:T(128)} %get-tuple-element.86) | copy-start | bytes 196
  133.3 5.2 %copy-start.57 = (f32[16]{0:T(128)S(1)}, f32[16]{0:T(128)}, u32[]{:S(2)}) copy-start(f32[16]{0:T(128)} %get-tuple-element.87) | copy-start | bytes 196
  133.3 5.2 %copy-start.58 = (f32[16]{0:T(128)S(1)}, f32[16]{0:T(128)}, u32[]{:S(2)}) copy-start(f32[16]{0:T(128)} %get-tuple-element.89) | copy-start | bytes 196
  140.5 3.3 %copy-start.14 = (f32[4,128,512]{2,1,0:T(8,128)S(1)}, f32[4,128,512]{2,1,0:T(8,128)}, u32[]{:S(2)}) copy-start(f32[4,128,512]{2,1,0:T(8,128)} %fusion.31) | copy-start | bytes 3145732
  140.5 3.3 %copy-start.15 = (f32[4,128,512]{2,1,0:T(8,128)S(1)}, f32[4,128,512]{2,1,0:T(8,128)}, u32[]{:S(2)}) copy-start(f32[4,128,512]{2,1,0:T(8,128)} %fusion.30) | copy-start | bytes 3145732
  148.3 8.3 %copy-start.16 = (f32[4,128,512]{2,1,0:T(8,128)S(1)}, f32[4,128,512]{2,1,0:T(8,128)}, u32[]{:S(2)}) copy-start(f32[4,128,512]{2,1,0:T(8,128)} %fusion.33) | copy-start | bytes 3145732
  148.3 8.3 %copy-start.17 = (f32[4,128,512]{2,1,0:T(8,128)S(1)}, f32[4,128,512]{2,1,0:T(8,128)}, u32[]{:S(2)}) copy-start(f32[4,128,512]{2,1,0:T(8,128)} %fusion.32) | copy-start | bytes 3145732
  158.0 3.1 %copy-start.33 = (f32[512,16]{0,1:T(8,128)S(1)}, f32[512,16]{0,1:T(8,128)}, u32[]{:S(2)}) copy-start(f32[512,16]{0,1:T(8,128)} %copy_bitcast_fusion.3) | copy-start | bytes 98308
  161.1 6.6 %copy-start.12 = (f32[512,1024]{0,1:T(8,128)S(1)}, f32[512,1024]{0,1:T(8,128)}, u32[]{:S(2)}) copy-start(f32[512,1024]{0,1:T(8,128)} %get-tuple-element.85) | copy-start | bytes 6291460
  161.1 6.6 %copy-start.48 = (f32[1024]{0:T(1024)S(1)}, f32[1024]{0:T(1024)}, u32[]{:S(2)}) copy-start(f32[1024]{0:T(1024)} %param.28) | copy-start | bytes 12292
  172.4 46.1 %copy-start.1 = (bf16[2048,512]{1,0:T(8,128)(2,1)S(1)}, bf16[2048,512]{1,0:T(8,128)(2,1)}, u32[]{:S(2)}) copy-start(bf16[2048,512]{1,0:T(8,128)(2,1)} %param.19) | copy-start | bytes 6291460
  (24 other events, 44.0 us)
Sparse Core Ops, SparseCore 0:
  174.1 44.3 reduce-scatter.1

commit v2 on v1

--- a/solution.py
+++ b/solution.py
@@ -125,11 +125,9 @@
             differ = jnp.where(mask, a_col - a_row, 0.0)
             m = jnp.where(mask, jnp.exp(differ), 0.0) * d_row * inner
             x_j = x_ref[:, j * P_SIZE : (j + 1) * P_SIZE]
-            m_hi = m.astype(BF16)
-            m_lo = (m - m_hi.astype(F32)).astype(BF16)
             y_ref[:, j * P_SIZE : (j + 1) * P_SIZE] = jnp.dot(
-                m_hi, x_j, preferred_element_type=F32
-            ) + jnp.dot(m_lo, x_j, preferred_element_type=F32)
+                m.astype(BF16), x_j, preferred_element_type=F32
+            )
 
     return pl.pallas_call(
         kernel,

time: 227 us -> 226 us (level)
  no operation moved by 1% of the time
where the time goes in v2:
time: 226 us; the launch traced here: 225 us
  matrix products  46.4 us (21%)
  waiting for transfers between devices  46.3 us (20%)
  local copies, waits for them, and re-layouts  43.9 us (19%)
  Pallas kernels  28.3 us (13%)
  other arithmetic  27.5 us (12%)
  starting transfers between devices  18 us (8%)
  between operations  14.3 us (6%)
    reduce_scatter x1, waiting for transfers between devices, on_device(): summed = lax.psum_scatter(partial, 'chan', scatter_dimension=0, tiled=True)  44.5 us
    ppermute x6, starting transfers between devices, shifted(): return lax.ppermute(value, axis, pairs)  18 us
    pallas_call x2, Pallas kernels, block_intra(): pl.pallas_call(kernel, grid=(blocks, groups), in_specs=[pl.BlockSpec((Q,...  15 us
    dot_general x2, matrix products, project(): gate_in = jnp.dot(source, w_gate, preferred_element_type=F32).astype(BF16)  14.8 us
    pallas_call x2, Pallas kernels, block_states(): pl.pallas_call(kernel, grid=(blocks, groups), in_specs=[pl.BlockSpec((Q,...  13.3 us
    unnamed x140, local copies, waits for them, and re-layouts  10 us
    dot_general x2, matrix products, project(): jnp.dot(source, w_values, preferred_element_type=F32) * known[:, None]  9.72 us
    convert_element_type x2, other arithmetic, conv_silu(): return jax.nn.silu(total).astype(BF16)  7.99 us
  transfers between devices with their start and end apart: 7, of which 2 were waited for; matrix products, arithmetic and copies ran while one was open for 25% of the time, Pallas kernels for 10%

profile of v2, /device:TPU:0, one launch (start us, length us, event | category | flops | bytes accessed | tf_op | source)
XLA Modules:
  0.0 224.7 jit_solution(18267047582924654052)
XLA Ops:
  8.3 1.3 collective-permute-start.1
  9.7 3.0 %collective-permute-start = (bf16[3,2176]{1,0:T(4,128)(2,1)S(1)}, bf16[3,2176]{1,0:T(4,128)(2,1)S(1)}, u32[]{:S(2)}, u32[]{:S(2)}) collective-permute-start(bf16[3,2176]{1,0:T(4,128)(2,1)S(1)} %pad_maximum_fusion.15), channel_id=1, source_target_pairs={{0,4},{4,8},{8,12},{1,5},{5,9},{9,13},{2,6},{6,10},{10,14},{3,7},{... | collective-permute-start | bytes 39176 | tf_op jit(solution)/shard_map/ppermute | solution.py:25
  12.8 3.6 %convert_bitcast_fusion = bf16[512,16,128]{0,2,1:T(8,128)(2,1)} fusion(bf16[512,2048]{1,0:T(8,128)(2,1)} %param.15), kind=kOutput, calls=%fused_computation.38 | convolution fusion | flops 269516800 | bytes 4194304 | tf_op jit(solution)/shard_map/rki,ij->rkj/dot_general | solution.py:187
  16.4 3.1 %rev.9 = bf16[512,16,128]{0,2,1:T(8,128)(2,1)} reverse(bf16[512,16,128]{0,2,1:T(8,128)(2,1)} %convert_bitcast_fusion), dimensions={1} | reverse | bytes 4194304 | tf_op jit(solution)/shard_map/jit(_flip)/rev | solution.py:190
  19.5 6.3 %multiply_convert_fusion.3 = bf16[512,1024]{0,1:T(8,128)(2,1)} fusion(bf16[512,2048]{1,0:T(8,128)(2,1)} %param.15, bf16[2048,1024]{1,0:T(8,128)(2,1)} %param.18, f32[512]{0:T(512)S(1)} %get-tuple-element.63), kind=kOutput, calls=%fused_computation.40 | convolution fusion | flops 2148532224 | bytes 7342080 | tf_op jit(solution)/shard_map/dot_general | solution.py:209
  25.9 3.4 %multiply_convert_fusion.1 = bf16[512,1024]{0,1:T(8,128)(2,1)} fusion(bf16[512,2048]{0,1:T(8,128)(2,1)S(1)} %bitcast.311, bf16[2048,1024]{1,0:T(8,128)(2,1)S(1)} %copy-done.13, f32[512]{0:T(512)S(1)} %get-tuple-element.63), kind=kOutput, calls=%fused_computation.37 | convolution fusion | flops 2148532224 | bytes 7342080 | tf_op jit(solution)/shard_map/dot_general | solution.py:209
  29.3 1.3 convolution_convert_fusion.3
  30.9 1.3 convolution_convert_fusion.4
  32.6 1.3 broadcast_multiply_fusion.1
  41.5 4.1 %fusion.21 = bf16[6,1024]{0,1:T(8,128)(2,1)S(1)} fusion(bf16[2048,1024]{1,0:T(8,128)(2,1)} %param.18, f32[6]{0:T(128)S(1)} %maximum_convert_fusion, bf16[3,2048]{1,0:T(4,128)(2,1)S(1)} %bitcast.354, bf16[3,2048]{1,0:T(4,128)(2,1)S(1)} %slice.307), kind=kOutput, calls=%fused_computation.54 | convolution fusion | flops 25227264 | bytes 4231192 | tf_op jit(solution)/shard_map/dot_general | solution.py:203
  45.8 5.6 %multiply_convert_fusion.2 = (bf16[512,1024]{0,1:T(8,128)(2,1)}, bf16[512,1024]{0,1:T(8,128)(2,1)}) fusion(bf16[512,1024]{0,1:T(8,128)(2,1)S(1)} %copy-done.27, bf16[3,1024]{0,1:T(8,128)(2,1)S(1)} %get-tuple-element.45, f32[1024]{0:T(1024)S(1)} %bitcast.358, f32[1024]{0:T(1024)S(1)} %bitcast.359, f32[1024]{0:T(1024)S(1)} %bitcast.357, ...), kind=kLoop, calls=%fused_computation.39 | loop fusion | flops 27262976 | bytes 4227072 | tf_op jit(solution)/shard_map/convert_element_type | solution.py:155
  51.4 2.4 %multiply_convert_fusion.5 = (bf16[512,512]{1,0:T(8,128)(2,1)}, bf16[512,512]{1,0:T(8,128)(2,1)}) fusion(bf16[512,512]{1,0:T(8,128)(2,1)S(1)} %convolution_convert_fusion.4, bf16[3,512]{1,0:T(4,128)(2,1)S(1)} %get-tuple-element.55, f32[512]{0:T(512)S(1)} %bitcast.362, f32[512]{0:T(512)S(1)} %bitcast.363, f32[512]{0:T(512)S(1)} %bitcast.361, ...), kind=kLoop, calls=%fused_computation.80 | loop fusion | flops 13631488 | bytes 2113536 | tf_op jit(solution)/shard_map/convert_element_type | solution.py:155
  53.8 6.7 %shard_map.148 = f32[4,16,64,128]{3,2,1,0:T(8,128)} custom-call(bf16[512,512]{1,0:T(8,128)(2,1)} %get-tuple-element.54.c_ref.b_ref, bf16[1024,512]{1,0:T(8,128)(2,1)} %bitcast.316, f32[2,8,512]{2,1,0:T(8,128)} %bitcast.349, f32[2,8,512]{2,1,0:T(8,128)} %bitcast.343), custom_call_target="tpu_custom_call" | custom-call | tf_op jit(solution)/shard_map/pallas_call | solution.py:93
  60.5 1.8 fusion.81
  62.3 2.1 fusion.79
  65.2 1.3 collective-permute-start.4
  66.5 6.7 %shard_map.146 = f32[4,16,64,128]{3,2,1,0:T(8,128)} custom-call(bf16[512,512]{1,0:T(8,128)(2,1)} %get-tuple-element.53.c_ref.b_ref, bf16[1024,512]{1,0:T(8,128)(2,1)} %bitcast.315, f32[2,8,512]{2,1,0:T(8,128)} %bitcast.346, f32[2,8,512]{2,1,0:T(8,128)} %bitcast.351), custom_call_target="tpu_custom_call" | custom-call | tf_op jit(solution)/shard_map/pallas_call | solution.py:93
  73.2 1.7 fusion.80
  75.0 2.1 fusion.78
  78.9 1.3 copy.188.x_ref
  80.4 1.3 copy.172.x_ref
  83.0 7.5 %shard_map.147 = f32[512,1024]{1,0:T(8,128)} custom-call(bf16[512,512]{1,0:T(8,128)(2,1)} %get-tuple-element.54.c_ref.b_ref, bf16[512,512]{1,0:T(8,128)(2,1)} %get-tuple-element.54.c_ref.b_ref, bf16[512,1024]{1,0:T(8,128)(2,1)} %copy.188.x_ref, f32[2,512,8]{2,1,0:T(8,128)} %copy.189.a_ref, f32[2,8,512]{2,1,0:T(8,128)} %bitcast.350, f32[2,8,512]{2,1,0:T(8,128)} %bitcast.344), custom_call_target="tpu_custom_call" | custom-call | tf_op jit(solution)/shard_map/pallas_call | solution.py:132
  90.5 2.9 %copy.198 = f32[512,1024]{0,1:T(8,128)} copy(f32[512,1024]{1,0:T(8,128)} %shard_map.147) | data formatting | bytes 4194304 | tf_op jit(solution)/shard_map/pallas_call | solution.py:132
  93.4 5.1 %collective-permute-start.2 = (bf16[16,8448]{1,0:T(8,128)(2,1)}, bf16[16,8448]{1,0:T(8,128)(2,1)S(1)}, u32[]{:S(2)}, u32[]{:S(2)}) collective-permute-start(bf16[16,8448]{1,0:T(8,128)(2,1)} %pad_maximum_fusion.8), channel_id=1, source_target_pairs={{0,4},{4,8},{8,12},{1,5},{5,9},{9,13},{2,6},{6,10},{10,14},{3,7},{... | collective-permute-start | bytes 811016 | tf_op jit(solution)/shard_map/ppermute | solution.py:25
  99.8 7.5 %shard_map.145 = f32[512,1024]{1,0:T(8,128)} custom-call(bf16[512,512]{1,0:T(8,128)(2,1)} %get-tuple-element.53.c_ref.b_ref, bf16[512,512]{1,0:T(8,128)(2,1)} %get-tuple-element.53.c_ref.b_ref, bf16[512,1024]{1,0:T(8,128)(2,1)} %copy.172.x_ref, f32[2,512,8]{2,1,0:T(8,128)} %copy.173.a_ref, f32[2,8,512]{2,1,0:T(8,128)} %bitcast.347, f32[2,8,512]{2,1,0:T(8,128)} %bitcast.352), custom_call_target="tpu_custom_call" | custom-call | tf_op jit(solution)/shard_map/pallas_call | solution.py:132
  107.4 3.0 %copy.182 = f32[512,1024]{0,1:T(8,128)} copy(f32[512,1024]{1,0:T(8,128)} %shard_map.145) | data formatting | bytes 4194304 | tf_op jit(solution)/shard_map/pallas_call | solution.py:132
  111.6 1.3 collective-permute-start.5
  114.8 6.0 %collective-permute-start.3 = (bf16[16,8448]{1,0:T(8,128)(2,1)}, bf16[16,8448]{1,0:T(8,128)(2,1)}, u32[]{:S(2)}, u32[]{:S(2)}) collective-permute-start(bf16[16,8448]{1,0:T(8,128)(2,1)} %pad_maximum_fusion.9), channel_id=1, source_target_pairs={{0,8},{4,12},{1,9},{5,13},{2,10},{6,14},{3,11},{7,15},{16,24},{20,... | collective-permute-start | bytes 811016 | tf_op jit(solution)/shard_map/ppermute | solution.py:25
  120.7 1.8 collective-permute-done.5
  122.5 1.9 convert_add_fusion
  124.4 1.9 stack.36
  126.3 1.1 copy.233
  129.4 1.6 fusion.31
  131.0 1.6 fusion.30
  132.7 2.0 convert_add_fusion.1
  134.7 2.0 stack.28
  139.8 1.6 fusion.33
  141.4 1.6 fusion.32
  143.1 1.5 pad_maximum_fusion.3
  144.6 3.0 %copy.209 = f32[512,1024]{0,1:T(8,128)} copy(f32[512,1024]{1,0:T(8,128)} %bitcast.318) | data formatting | bytes 4194304 | tf_op jit(solution)/shard_map/reshape | solution.py:267
  147.6 8.2 %bitcast_reduce_fusion = (f32[512,2]{0,1:T(2,128)S(1)}, f32[512,1024]{0,1:T(8,128)}) fusion(bf16[512,2048]{0,1:T(8,128)(2,1)S(1)} %bitcast.314, bf16[2048,1024]{1,0:T(8,128)(2,1)} %param.17, bf16[512,1024]{0,1:T(8,128)(2,1)} %get-tuple-element.48, f32[1024]{0:T(1024)S(1)} %mul.591, f32[512,1024]{0,1:T(8,128)} %copy.198, f32[512,1024]{0,1:T(8,128)} %copy.209, ...), kind=kOutput, calls=%fused_computation.24 | convolution fusion | flops 2154822656 | bytes 13672448 | tf_op jit(solution)/shard_map/dot_general | solution.py:208
  155.9 1.5 pad_maximum_fusion.1
  157.4 3.1 %copy.208 = f32[512,1024]{0,1:T(8,128)} copy(f32[512,1024]{1,0:T(8,128)} %bitcast.319) | data formatting | bytes 4194304 | tf_op jit(solution)/shard_map/reshape | solution.py:267
  160.5 6.6 %bitcast_reduce_fusion.1 = (f32[512,2]{0,1:T(2,128)S(1)}, f32[512,1024]{0,1:T(8,128)S(1)}) fusion(bf16[512,2048]{1,0:T(8,128)(2,1)S(1)} %copy-done.5, bf16[2048,1024]{1,0:T(8,128)(2,1)} %param.17, bf16[512,1024]{0,1:T(8,128)(2,1)S(1)} %copy-done.6, f32[1024]{0:T(1024)S(1)} %mul.591, f32[512,1024]{0,1:T(8,128)} %copy.182, f32[512,1024]{0,1:T(8,128)} %copy.208, ...), kind=kOutput, calls=%fused_computation.31 | convolution fusion | flops 2154822656 | bytes 13672448 | tf_op jit(solution)/shard_map/dot_general | solution.py:208
  167.5 1.8 copy-done.63
  169.3 2.5 %convolution_convert_fusion = bf16[512,2048]{1,0:T(8,128)(2,1)S(1)} fusion(bf16[1024,2048]{1,0:T(8,128)(2,1)S(1)} %copy-done.63, bf16[512,1024]{0,1:T(8,128)(2,1)S(1)} %get-tuple-element.62, bf16[512,1024]{0,1:T(8,128)(2,1)S(1)} %get-tuple-element.61), kind=kOutput, calls=%fused_computation | convolution fusion | flops 2150629376 | bytes 8388608 | tf_op jit(solution)/shard_map/dot_general | solution.py:279
  171.8 1.5 copy.274
  173.3 44.5 %reduce-scatter.2.cloned.1.call-done = bf16[1,512,512]{2,1,0:T(8,128)(2,1)} async-done(((bf16[4,512,512]{2,1,0:T(8,128)(2,1)}), bf16[1,512,512]{2,1,0:T(8,128)(2,1)}) %reduce-scatter.2.cloned.1.call-update) | async-done | bytes 524304 | tf_op jit(solution)/shard_map/reduce_scatter | solution.py:281
  (216 shorter events, 24.2 us)
Async XLA Ops:
  6.5 22.7 %copy-start = (bf16[2048,512]{1,0:T(8,128)(2,1)S(1)}, bf16[2048,512]{1,0:T(8,128)(2,1)}, u32[]{:S(2)}) copy-start(bf16[2048,512]{1,0:T(8,128)(2,1)} %param.19) | copy-start | bytes 6291460
  6.5 211.3 %reduce-scatter.2.cloned.1.call-start = ((), (), s32[]{:S(2)}) async-start(), calls=%async_computation.1 | async-start | bytes 2621440 | tf_op jit(solution)/shard_map/reduce_scatter | solution.py:281
  8.3 32.3 %collective-permute-start.1 = (bf16[3,2176]{1,0:T(4,128)(2,1)S(1)}, bf16[3,2176]{1,0:T(4,128)(2,1)S(1)}, u32[]{:S(2)}, u32[]{:S(2)}) collective-permute-start(bf16[3,2176]{1,0:T(4,128)(2,1)S(1)} %pad_maximum_fusion.16), channel_id=1, source_target_pairs={{4,0},{8,4},{12,8},{5,1},{9,5},{13,9},{6,2},{10,6},{14,10},{7,3},{... | collective-permute-start | bytes 39176 | tf_op jit(solution)/shard_map/ppermute | solution.py:25
  9.7 31.2 %collective-permute-start = (bf16[3,2176]{1,0:T(4,128)(2,1)S(1)}, bf16[3,2176]{1,0:T(4,128)(2,1)S(1)}, u32[]{:S(2)}, u32[]{:S(2)}) collective-permute-start(bf16[3,2176]{1,0:T(4,128)(2,1)S(1)} %pad_maximum_fusion.15), channel_id=1, source_target_pairs={{0,4},{4,8},{8,12},{1,5},{5,9},{9,13},{2,6},{6,10},{10,14},{3,7},{... | collective-permute-start | bytes 39176 | tf_op jit(solution)/shard_map/ppermute | solution.py:25
  19.5 6.4 %copy-start.2 = (bf16[512,16,128]{0,2,1:T(8,128)(2,1)S(1)}, bf16[512,16,128]{0,2,1:T(8,128)(2,1)}, u32[]{:S(2)}) copy-start(bf16[512,16,128]{0,2,1:T(8,128)(2,1)} %rev.9) | copy-start | bytes 6291460
  19.5 6.4 %copy-start.13 = (bf16[2048,1024]{1,0:T(8,128)(2,1)S(1)}, bf16[2048,1024]{1,0:T(8,128)(2,1)}, u32[]{:S(2)}) copy-start(bf16[2048,1024]{1,0:T(8,128)(2,1)} %param.18) | copy-start | bytes 12582916
  32.6 8.0 %copy-start.29 = (f32[512,16]{0,1:T(8,128)}, f32[512,16]{0,1:T(8,128)S(1)}, u32[]{:S(2)}) copy-start(f32[512,16]{0,1:T(8,128)S(1)} %compare_select_fusion) | copy-start | bytes 98308
  32.6 6.7 %copy-start.62 = (f32[16]{0:T(128)S(1)}, f32[16]{0:T(128)}, u32[]{:S(2)}) copy-start(f32[16]{0:T(128)} %param.27) | copy-start | bytes 196
  35.4 26.9 %copy-start.41 = (f32[16]{0:T(128)}, f32[16]{0:T(128)S(1)}, u32[]{:S(2)}) copy-start(f32[16]{0:T(128)S(1)} %get-tuple-element.18) | copy-start | bytes 196
  35.4 26.9 %copy-start.43 = (f32[16]{0:T(128)}, f32[16]{0:T(128)S(1)}, u32[]{:S(2)}) copy-start(f32[16]{0:T(128)S(1)} %get-tuple-element.19) | copy-start | bytes 196
  35.4 26.9 %copy-start.45 = (f32[16]{0:T(128)}, f32[16]{0:T(128)S(1)}, u32[]{:S(2)}) copy-start(f32[16]{0:T(128)S(1)} %get-tuple-element.20) | copy-start | bytes 196
  38.3 7.3 %copy-start.31 = (f32[512,2,8]{0,2,1:T(8,128)}, f32[512,2,8]{0,2,1:T(8,128)S(1)}, u32[]{:S(2)}) copy-start(f32[512,2,8]{0,2,1:T(8,128)S(1)} %reshape_reshape.7) | copy-start | bytes 98308
  39.5 6.1 %copy-start.30 = (f32[512,2,8]{0,2,1:T(8,128)}, f32[512,2,8]{0,2,1:T(8,128)S(1)}, u32[]{:S(2)}) copy-start(f32[512,2,8]{0,2,1:T(8,128)S(1)} %reshape_reshape.6) | copy-start | bytes 98308
  41.5 4.3 %copy-start.27 = (bf16[512,1024]{0,1:T(8,128)(2,1)S(1)}, bf16[512,1024]{0,1:T(8,128)(2,1)}, u32[]{:S(2)}) copy-start(bf16[512,1024]{0,1:T(8,128)(2,1)} %multiply_convert_fusion.3) | copy-start | bytes 3145732
  41.5 4.3 %copy-start.28 = (bf16[512,1024]{0,1:T(8,128)(2,1)S(1)}, bf16[512,1024]{0,1:T(8,128)(2,1)}, u32[]{:S(2)}) copy-start(bf16[512,1024]{0,1:T(8,128)(2,1)} %multiply_convert_fusion.1) | copy-start | bytes 3145732
  41.5 4.3 %copy-start.47 = (f32[1024]{0:T(1024)S(1)}, f32[1024]{0:T(1024)}, u32[]{:S(2)}) copy-start(f32[1024]{0:T(1024)} %param.22) | copy-start | bytes 12292
  45.8 5.6 %copy-start.49 = (f32[512]{0:T(512)S(1)}, f32[512]{0:T(512)}, u32[]{:S(2)}) copy-start(f32[512]{0:T(512)} %param.24) | copy-start | bytes 6148
  65.2 45.2 %collective-permute-start.4 = (bf16[16,8448]{1,0:T(8,128)(2,1)}, bf16[16,8448]{1,0:T(8,128)(2,1)S(1)}, u32[]{:S(2)}, u32[]{:S(2)}) collective-permute-start(bf16[16,8448]{1,0:T(8,128)(2,1)} %pad_maximum_fusion.10), channel_id=1, source_target_pairs={{4,0},{8,4},{12,8},{5,1},{9,5},{13,9},{6,2},{10,6},{14,10},{7,3},{... | collective-permute-start | bytes 811016 | tf_op jit(solution)/shard_map/ppermute | solution.py:25
  75.0 3.9 %copy-start.7 = (bf16[512,1024]{0,1:T(8,128)(2,1)S(1)}, bf16[512,1024]{0,1:T(8,128)(2,1)}, u32[]{:S(2)}) copy-start(bf16[512,1024]{0,1:T(8,128)(2,1)} %get-tuple-element.48) | copy-start | bytes 3145732
  77.0 3.2 %copy-start.10 = (bf16[512,512]{1,0:T(8,128)(2,1)S(1)}, bf16[512,512]{1,0:T(8,128)(2,1)}, u32[]{:S(2)}) copy-start(bf16[512,512]{1,0:T(8,128)(2,1)} %get-tuple-element.53.c_ref.b_ref) | copy-start | bytes 1572868
  93.4 19.5 %collective-permute-start.2 = (bf16[16,8448]{1,0:T(8,128)(2,1)}, bf16[16,8448]{1,0:T(8,128)(2,1)S(1)}, u32[]{:S(2)}, u32[]{:S(2)}) collective-permute-start(bf16[16,8448]{1,0:T(8,128)(2,1)} %pad_maximum_fusion.8), channel_id=1, source_target_pairs={{0,4},{4,8},{8,12},{1,5},{5,9},{9,13},{2,6},{6,10},{10,14},{3,7},{... | collective-permute-start | bytes 811016 | tf_op jit(solution)/shard_map/ppermute | solution.py:25
  107.3 3.3 %copy-start.37 = (f32[16]{0:T(128)S(1)}, f32[16]{0:T(128)}, u32[]{:S(2)}) copy-start(f32[16]{0:T(128)} %copy-done.36) | copy-start | bytes 196
  107.3 3.3 %copy-start.19 = (f32[16,8192]{1,0:T(8,128)S(1)}, f32[16,8192]{1,0:T(8,128)}, u32[]{:S(2)}) copy-start(f32[16,8192]{1,0:T(8,128)} %get-tuple-element.24) | copy-start | bytes 1572868
  107.3 3.3 %copy-start.52 = (f32[16]{0:T(128)S(1)}, f32[16]{0:T(128)}, u32[]{:S(2)}) copy-start(f32[16]{0:T(128)} %get-tuple-element.78) | copy-start | bytes 196
  107.4 6.3 %copy-start.18 = (f32[16,8192]{1,0:T(8,128)S(1)}, f32[16,8192]{1,0:T(8,128)}, u32[]{:S(2)}) copy-start(f32[16,8192]{1,0:T(8,128)} %get-tuple-element.22) | copy-start | bytes 1572868
  107.4 6.3 %copy-start.51 = (f32[16]{0:T(128)S(1)}, f32[16]{0:T(128)}, u32[]{:S(2)}) copy-start(f32[16]{0:T(128)} %get-tuple-element.73) | copy-start | bytes 196
  111.6 10.8 %collective-permute-start.5 = (bf16[16,8448]{1,0:T(8,128)(2,1)}, bf16[16,8448]{1,0:T(8,128)(2,1)}, u32[]{:S(2)}, u32[]{:S(2)}) collective-permute-start(bf16[16,8448]{1,0:T(8,128)(2,1)} %pad_maximum_fusion.11), channel_id=1, source_target_pairs={{8,0},{12,4},{9,1},{13,5},{10,2},{14,6},{11,3},{15,7},{24,16},{28,... | collective-permute-start | bytes 811016 | tf_op jit(solution)/shard_map/ppermute | solution.py:25
  113.8 13.6 %copy-start.9 = (f32[4,16,64,128]{3,2,1,0:T(8,128)S(1)}, f32[4,16,64,128]{3,2,1,0:T(8,128)}, u32[]{:S(2)}) copy-start(f32[4,16,64,128]{3,2,1,0:T(8,128)} %shard_map.148) | copy-start | bytes 6291460
  113.8 13.6 %copy-start.42 = (f32[16]{0:T(128)S(1)}, f32[16]{0:T(128)}, u32[]{:S(2)}) copy-start(f32[16]{0:T(128)} %copy-done.41) | copy-start | bytes 196
  113.8 13.6 %copy-start.44 = (f32[16]{0:T(128)S(1)}, f32[16]{0:T(128)}, u32[]{:S(2)}) copy-start(f32[16]{0:T(128)} %copy-done.43) | copy-start | bytes 196
  113.8 13.6 %copy-start.46 = (f32[16]{0:T(128)S(1)}, f32[16]{0:T(128)}, u32[]{:S(2)}) copy-start(f32[16]{0:T(128)} %copy-done.45) | copy-start | bytes 196
  113.8 13.6 %copy-start.59 = (f32[16]{0:T(128)S(1)}, f32[16]{0:T(128)}, u32[]{:S(2)}) copy-start(f32[16]{0:T(128)} %get-tuple-element.90) | copy-start | bytes 196
  113.9 13.6 %copy-start.60 = (f32[16]{0:T(128)S(1)}, f32[16]{0:T(128)}, u32[]{:S(2)}) copy-start(f32[16]{0:T(128)} %get-tuple-element.91) | copy-start | bytes 196
  113.9 13.6 %copy-start.61 = (f32[16]{0:T(128)S(1)}, f32[16]{0:T(128)}, u32[]{:S(2)}) copy-start(f32[16]{0:T(128)} %get-tuple-element.93) | copy-start | bytes 196
  114.8 17.9 %collective-permute-start.3 = (bf16[16,8448]{1,0:T(8,128)(2,1)}, bf16[16,8448]{1,0:T(8,128)(2,1)}, u32[]{:S(2)}, u32[]{:S(2)}) collective-permute-start(bf16[16,8448]{1,0:T(8,128)(2,1)} %pad_maximum_fusion.9), channel_id=1, source_target_pairs={{0,8},{4,12},{1,9},{5,13},{2,10},{6,14},{3,11},{7,15},{16,24},{20,... | collective-permute-start | bytes 811016 | tf_op jit(solution)/shard_map/ppermute | solution.py:25
  129.4 3.3 %copy-start.24 = (bf16[16,8448]{1,0:T(8,128)(2,1)S(1)}, bf16[16,8448]{1,0:T(8,128)(2,1)}, u32[]{:S(2)}) copy-start(bf16[16,8448]{1,0:T(8,128)(2,1)} %copy-done.23) | copy-start | bytes 811012
  132.7 5.2 %copy-start.8 = (f32[4,16,64,128]{3,2,1,0:T(8,128)S(1)}, f32[4,16,64,128]{3,2,1,0:T(8,128)}, u32[]{:S(2)}) copy-start(f32[4,16,64,128]{3,2,1,0:T(8,128)} %shard_map.146) | copy-start | bytes 6291460
  132.7 5.2 %copy-start.56 = (f32[16]{0:T(128)S(1)}, f32[16]{0:T(128)}, u32[]{:S(2)}) copy-start(f32[16]{0:T(128)} %get-tuple-element.86) | copy-start | bytes 196
  132.7 5.2 %copy-start.57 = (f32[16]{0:T(128)S(1)}, f32[16]{0:T(128)}, u32[]{:S(2)}) copy-start(f32[16]{0:T(128)} %get-tuple-element.87) | copy-start | bytes 196
  132.7 5.2 %copy-start.58 = (f32[16]{0:T(128)S(1)}, f32[16]{0:T(128)}, u32[]{:S(2)}) copy-start(f32[16]{0:T(128)} %get-tuple-element.89) | copy-start | bytes 196
  139.8 3.3 %copy-start.14 = (f32[4,128,512]{2,1,0:T(8,128)S(1)}, f32[4,128,512]{2,1,0:T(8,128)}, u32[]{:S(2)}) copy-start(f32[4,128,512]{2,1,0:T(8,128)} %fusion.31) | copy-start | bytes 3145732
  139.8 3.3 %copy-start.15 = (f32[4,128,512]{2,1,0:T(8,128)S(1)}, f32[4,128,512]{2,1,0:T(8,128)}, u32[]{:S(2)}) copy-start(f32[4,128,512]{2,1,0:T(8,128)} %fusion.30) | copy-start | bytes 3145732
  147.6 8.3 %copy-start.16 = (f32[4,128,512]{2,1,0:T(8,128)S(1)}, f32[4,128,512]{2,1,0:T(8,128)}, u32[]{:S(2)}) copy-start(f32[4,128,512]{2,1,0:T(8,128)} %fusion.33) | copy-start | bytes 3145732
  147.6 8.3 %copy-start.17 = (f32[4,128,512]{2,1,0:T(8,128)S(1)}, f32[4,128,512]{2,1,0:T(8,128)}, u32[]{:S(2)}) copy-start(f32[4,128,512]{2,1,0:T(8,128)} %fusion.32) | copy-start | bytes 3145732
  157.4 3.1 %copy-start.33 = (f32[512,16]{0,1:T(8,128)S(1)}, f32[512,16]{0,1:T(8,128)}, u32[]{:S(2)}) copy-start(f32[512,16]{0,1:T(8,128)} %copy_bitcast_fusion.3) | copy-start | bytes 98308
  160.4 6.6 %copy-start.12 = (f32[512,1024]{0,1:T(8,128)S(1)}, f32[512,1024]{0,1:T(8,128)}, u32[]{:S(2)}) copy-start(f32[512,1024]{0,1:T(8,128)} %get-tuple-element.85) | copy-start | bytes 6291460
  160.4 6.6 %copy-start.48 = (f32[1024]{0:T(1024)S(1)}, f32[1024]{0:T(1024)}, u32[]{:S(2)}) copy-start(f32[1024]{0:T(1024)} %param.28) | copy-start | bytes 12292
  171.8 46.1 %copy-start.1 = (bf16[2048,512]{1,0:T(8,128)(2,1)S(1)}, bf16[2048,512]{1,0:T(8,128)(2,1)}, u32[]{:S(2)}) copy-start(bf16[2048,512]{1,0:T(8,128)(2,1)} %param.19) | copy-start | bytes 6291460
  (24 other events, 44.0 us)
Sparse Core Ops, SparseCore 0:
  173.5 44.3 reduce-scatter.1

commit v3 on v2

--- a/solution.py
+++ b/solution.py
@@ -105,13 +105,13 @@
     )(state_c, values_t, acc_t, delta_t)
 
 
-def block_intra(state_c, values_c, acc_g, acc_t, delta_t, forward, interpret=False):
-    rows = values_c.shape[0]
+def block_intra(state_c, values_t, acc_g, acc_t, delta_t, forward, interpret=False):
+    rows = values_t.shape[1]
     groups, _, per_group = acc_g.shape
     blocks = rows // Q
     width_g = per_group * P_SIZE
 
-    def kernel(c_ref, b_ref, x_ref, a_ref, at_ref, dt_ref, y_ref):
+    def kernel(c_ref, b_ref, xt_ref, a_ref, at_ref, dt_ref, y_ref):
         inner = lax.dot_general(
             c_ref[...], b_ref[...], (((1,), (1,)), ((), ())), preferred_element_type=F32
         )
@@ -124,9 +124,9 @@
             d_row = dt_ref[0, j : j + 1, :]
             differ = jnp.where(mask, a_col - a_row, 0.0)
             m = jnp.where(mask, jnp.exp(differ), 0.0) * d_row * inner
-            x_j = x_ref[:, j * P_SIZE : (j + 1) * P_SIZE]
-            y_ref[:, j * P_SIZE : (j + 1) * P_SIZE] = jnp.dot(
-                m.astype(BF16), x_j, preferred_element_type=F32
+            xt_j = xt_ref[j * P_SIZE : (j + 1) * P_SIZE, :]
+            y_ref[j * P_SIZE : (j + 1) * P_SIZE, :] = lax.dot_general(
+                xt_j, m.astype(BF16), (((1,), (1,)), ((), ())), preferred_element_type=F32
             )
 
     return pl.pallas_call(
@@ -135,15 +135,15 @@
         in_specs=[
             pl.BlockSpec((Q, N), lambda b, g: (b, 2 * g + 1)),
             pl.BlockSpec((Q, N), lambda b, g: (b, 2 * g)),
-            pl.BlockSpec((Q, width_g), lambda b, g: (b, g)),
+            pl.BlockSpec((width_g, Q), lambda b, g: (g, b)),
             pl.BlockSpec((1, Q, per_group), lambda b, g: (g, b, 0)),
             pl.BlockSpec((1, per_group, Q), lambda b, g: (g, 0, b)),
             pl.BlockSpec((1, per_group, Q), lambda b, g: (g, 0, b)),
         ],
-        out_specs=pl.BlockSpec((Q, width_g), lambda b, g: (b, g)),
-        out_shape=jax.ShapeDtypeStruct((rows, groups * width_g), F32),
+        out_specs=pl.BlockSpec((width_g, Q), lambda b, g: (g, b)),
+        out_shape=jax.ShapeDtypeStruct((groups * width_g, rows), F32),
         interpret=interpret,
-    )(state_c, state_c, values_c, acc_g, acc_t, delta_t)
+    )(state_c, state_c, values_t, acc_g, acc_t, delta_t)
 
 
 def conv_silu(padded, kernel, offset, count, forward):
@@ -237,7 +237,8 @@
         acc = jnp.einsum("ts,bsh->bth", mask.astype(F32), ld, precision=HIGHEST)
         blk = jnp.sum(ld, axis=1)
         acc_g, delta_g, acc_t, delta_t = group_layout(acc.reshape(rows, heads), delta, groups, per_group)
-        states = block_states(state_c, values_c.T, acc_t, delta_t, forward)
+        values_t = values_c.T
+        states = block_states(state_c, values_t, acc_t, delta_t, forward)
 
         order = list(range(blocks)) if forward else list(range(blocks - 1, -1, -1))
         block_decay = jnp.exp(blk)
@@ -252,7 +253,7 @@
             log_before = log_before + blk[index]
         total = log_before
         carried = exclusive_carry(total, running, sign)
-        intra = block_intra(state_c, values_c, acc_g, acc_t, delta_t, forward)
+        intra = block_intra(state_c, values_t, acc_g, acc_t, delta_t, forward).T
         start = jnp.stack(
             [local_start[index] + entering[index][:, None, None] * carried for index in range(blocks)]
         )

time: 226 us -> 206 us (0.912)
  local copies, waits for them, and re-layouts: 43.9 us -> 26.8 us
  other arithmetic: 27.5 us -> 24.5 us
    pallas_call x2 -> x0, local copies, waits for them, and re-layouts: 5.93 us -> none  [block_intra(): pl.pallas_call(kernel, grid=(blocks, groups), in_specs=[pl.BlockSpec((Q,...]
    unnamed x140 -> x128, local copies, waits for them, and re-layouts: 10 us -> 6.17 us
    another operation x2, local copies, waits for them, and re-layouts: 3.85 us -> 0.17 us  [local_scan(): jnp.stack([local_start[index] + entering[index][:, None, None] * carried...]
    convert_element_type x2 -> x0, local copies, waits for them, and re-layouts: 2.66 us -> none  [conv_silu(): return jax.nn.silu(total).astype(BF16)]
  transfers between devices with their start and end apart: 7 -> 7, of which waited for: 2 -> 2; matrix products, arithmetic and copies ran while one was open for 25% -> 20% of each run, Pallas kernels for 10% -> 11%
where the time goes in v3:
time: 206 us; the launch traced here: 205 us
  waiting for transfers between devices  46.8 us (23%)
  matrix products  46.3 us (22%)
  Pallas kernels  28.6 us (14%)
  local copies, waits for them, and re-layouts  26.8 us (13%)
  other arithmetic  24.5 us (12%)
  starting transfers between devices  17.9 us (9%)
  between operations  14.3 us (7%)
    reduce_scatter x1, waiting for transfers between devices, on_device(): summed = lax.psum_scatter(partial, 'chan', scatter_dimension=0, tiled=True)  44.5 us
    ppermute x6, starting transfers between devices, shifted(): return lax.ppermute(value, axis, pairs)  17.9 us
    pallas_call x2, Pallas kernels, block_intra(): pl.pallas_call(kernel, grid=(blocks, groups), in_specs=[pl.BlockSpec((Q,...  15.2 us
    dot_general x2, matrix products, project(): gate_in = jnp.dot(source, w_gate, preferred_element_type=F32).astype(BF16)  14.6 us
    pallas_call x2, Pallas kernels, block_states(): pl.pallas_call(kernel, grid=(blocks, groups), in_specs=[pl.BlockSpec((Q,...  13.4 us
    dot_general x2, matrix products, project(): jnp.dot(source, w_values, preferred_element_type=F32) * known[:, None]  9.67 us
    convert_element_type x2, other arithmetic, conv_silu(): return jax.nn.silu(total).astype(BF16)  7.96 us
    dot_general x4, matrix products, local_scan(): jnp.einsum('btn,bkn->btk', c_f32[:, :, group], start[:, group], precision...  6.68 us
  transfers between devices with their start and end apart: 7, of which 2 were waited for; matrix products, arithmetic and copies ran while one was open for 20% of the time, Pallas kernels for 11%

profile of v3, /device:TPU:0, one launch (start us, length us, event | category | flops | bytes accessed | tf_op | source)
XLA Modules:
  0.0 205.3 jit_solution(10313796740273553185)
XLA Ops:
  6.5 0.8 compare_select_fusion.2
  7.5 0.8 fusion.82
  8.3 1.3 collective-permute-start.1
  9.7 3.0 %collective-permute-start = (bf16[3,2176]{1,0:T(4,128)(2,1)S(1)}, bf16[3,2176]{1,0:T(4,128)(2,1)S(1)}, u32[]{:S(2)}, u32[]{:S(2)}) collective-permute-start(bf16[3,2176]{1,0:T(4,128)(2,1)S(1)} %pad_maximum_fusion.15), channel_id=1, source_target_pairs={{0,4},{4,8},{8,12},{1,5},{5,9},{9,13},{2,6},{6,10},{10,14},{3,7},{... | collective-permute-start | bytes 39176 | tf_op jit(solution)/shard_map/ppermute | solution.py:25
  12.8 3.6 %convert_bitcast_fusion = bf16[512,16,128]{0,2,1:T(8,128)(2,1)} fusion(bf16[512,2048]{1,0:T(8,128)(2,1)} %param.15), kind=kOutput, calls=%fused_computation.38 | convolution fusion | flops 269516800 | bytes 4194304 | tf_op jit(solution)/shard_map/rki,ij->rkj/dot_general | solution.py:187
  16.4 3.1 %rev.9 = bf16[512,16,128]{0,2,1:T(8,128)(2,1)} reverse(bf16[512,16,128]{0,2,1:T(8,128)(2,1)} %convert_bitcast_fusion), dimensions={1} | reverse | bytes 4194304 | tf_op jit(solution)/shard_map/jit(_flip)/rev | solution.py:190
  19.5 6.3 %multiply_convert_fusion.3 = bf16[512,1024]{0,1:T(8,128)(2,1)} fusion(bf16[512,2048]{1,0:T(8,128)(2,1)} %param.15, bf16[2048,1024]{1,0:T(8,128)(2,1)} %param.18, f32[512]{0:T(512)S(1)} %get-tuple-element.63), kind=kOutput, calls=%fused_computation.40 | convolution fusion | flops 2148532224 | bytes 7342080 | tf_op jit(solution)/shard_map/dot_general | solution.py:209
  25.8 3.3 %multiply_convert_fusion.1 = bf16[512,1024]{0,1:T(8,128)(2,1)} fusion(bf16[512,2048]{0,1:T(8,128)(2,1)S(1)} %bitcast.315, bf16[2048,1024]{1,0:T(8,128)(2,1)S(1)} %copy-done.13, f32[512]{0:T(512)S(1)} %get-tuple-element.63), kind=kOutput, calls=%fused_computation.37 | convolution fusion | flops 2148532224 | bytes 7342080 | tf_op jit(solution)/shard_map/dot_general | solution.py:209
  29.2 1.3 convolution_convert_fusion.3
  30.8 1.3 convolution_convert_fusion.4
  32.5 1.3 broadcast_multiply_fusion.1
  34.4 0.9 slice_reduce_fusion
  36.0 0.9 slice_reduce_fusion.5
  38.2 1.0 copy.170.a_ref
  39.3 1.1 copy.156.a_ref
  41.3 4.1 %fusion.21 = bf16[6,1024]{0,1:T(8,128)(2,1)S(1)} fusion(bf16[2048,1024]{1,0:T(8,128)(2,1)} %param.18, f32[6]{0:T(128)S(1)} %maximum_convert_fusion, bf16[3,2048]{1,0:T(4,128)(2,1)S(1)} %bitcast.360, bf16[3,2048]{1,0:T(4,128)(2,1)S(1)} %slice.307), kind=kOutput, calls=%fused_computation.54 | convolution fusion | flops 25227264 | bytes 4231192 | tf_op jit(solution)/shard_map/dot_general | solution.py:203
  45.6 5.6 %multiply_convert_fusion.2 = (bf16[512,1024]{0,1:T(8,128)(2,1)}, bf16[512,1024]{0,1:T(8,128)(2,1)}) fusion(bf16[512,1024]{0,1:T(8,128)(2,1)S(1)} %copy-done.20, bf16[3,1024]{0,1:T(8,128)(2,1)S(1)} %get-tuple-element.45, f32[1024]{0:T(1024)S(1)} %bitcast.364, f32[1024]{0:T(1024)S(1)} %bitcast.365, f32[1024]{0:T(1024)S(1)} %bitcast.363, ...), kind=kLoop, calls=%fused_computation.39 | loop fusion | flops 27262976 | bytes 4227072 | tf_op jit(solution)/shard_map/convert_element_type | solution.py:155
  51.2 2.4 %multiply_convert_fusion.5 = (bf16[512,512]{1,0:T(8,128)(2,1)}, bf16[512,512]{1,0:T(8,128)(2,1)}) fusion(bf16[512,512]{1,0:T(8,128)(2,1)S(1)} %convolution_convert_fusion.4, bf16[3,512]{1,0:T(4,128)(2,1)S(1)} %get-tuple-element.55, f32[512]{0:T(512)S(1)} %bitcast.368, f32[512]{0:T(512)S(1)} %bitcast.369, f32[512]{0:T(512)S(1)} %bitcast.367, ...), kind=kLoop, calls=%fused_computation.80 | loop fusion | flops 13631488 | bytes 2113536 | tf_op jit(solution)/shard_map/convert_element_type | solution.py:155
  53.6 6.7 %shard_map.148 = f32[4,16,64,128]{3,2,1,0:T(8,128)} custom-call(bf16[512,512]{1,0:T(8,128)(2,1)} %get-tuple-element.54.c_ref.b_ref, bf16[1024,512]{1,0:T(8,128)(2,1)} %bitcast.321, f32[2,8,512]{2,1,0:T(8,128)} %bitcast.355, f32[2,8,512]{2,1,0:T(8,128)} %bitcast.349), custom_call_target="tpu_custom_call" | custom-call | tf_op jit(solution)/shard_map/pallas_call | solution.py:93
  60.3 1.7 fusion.81
  62.0 1.3 fusion.79
  64.2 1.3 collective-permute-start.4
  65.5 6.7 %shard_map.146 = f32[4,16,64,128]{3,2,1,0:T(8,128)} custom-call(bf16[512,512]{1,0:T(8,128)(2,1)} %get-tuple-element.53.c_ref.b_ref, bf16[1024,512]{1,0:T(8,128)(2,1)} %bitcast.319, f32[2,8,512]{2,1,0:T(8,128)} %bitcast.352, f32[2,8,512]{2,1,0:T(8,128)} %bitcast.357), custom_call_target="tpu_custom_call" | custom-call | tf_op jit(solution)/shard_map/pallas_call | solution.py:93
  72.2 1.7 fusion.80
  74.0 1.3 fusion.78
  77.7 7.6 %shard_map.147 = f32[1024,512]{1,0:T(8,128)} custom-call(bf16[512,512]{1,0:T(8,128)(2,1)} %get-tuple-element.54.c_ref.b_ref, bf16[512,512]{1,0:T(8,128)(2,1)} %get-tuple-element.54.c_ref.b_ref, bf16[1024,512]{1,0:T(8,128)(2,1)} %bitcast.322, f32[2,512,8]{2,1,0:T(8,128)} %copy.170.a_ref, f32[2,8,512]{2,1,0:T(8,128)} %bitcast.356, f32[2,8,512]{2,1,0:T(8,128)} %bitcast.350), custom_call_target="tpu_custom_call" | custom-call | tf_op jit(solution)/shard_map/pallas_call | solution.py:132
  85.4 5.1 %collective-permute-start.2 = (bf16[16,8448]{1,0:T(8,128)(2,1)S(1)}, bf16[16,8448]{1,0:T(8,128)(2,1)S(1)}, u32[]{:S(2)}, u32[]{:S(2)}) collective-permute-start(bf16[16,8448]{1,0:T(8,128)(2,1)S(1)} %copy-done.25), channel_id=1, source_target_pairs={{0,4},{4,8},{8,12},{1,5},{5,9},{9,13},{2,6},{6,10},{10,14},{3,7},{... | collective-permute-start | bytes 811016 | tf_op jit(solution)/shard_map/ppermute | solution.py:25
  91.8 7.6 %shard_map.145 = f32[1024,512]{1,0:T(8,128)} custom-call(bf16[512,512]{1,0:T(8,128)(2,1)} %get-tuple-element.53.c_ref.b_ref, bf16[512,512]{1,0:T(8,128)(2,1)} %get-tuple-element.53.c_ref.b_ref, bf16[1024,512]{1,0:T(8,128)(2,1)} %bitcast.320, f32[2,512,8]{2,1,0:T(8,128)} %copy.156.a_ref, f32[2,8,512]{2,1,0:T(8,128)} %bitcast.353, f32[2,8,512]{2,1,0:T(8,128)} %bitcast.358), custom_call_target="tpu_custom_call" | custom-call | tf_op jit(solution)/shard_map/pallas_call | solution.py:132
  100.7 1.3 collective-permute-start.5
  103.2 6.0 %collective-permute-start.3 = (bf16[16,8448]{1,0:T(8,128)(2,1)}, bf16[16,8448]{1,0:T(8,128)(2,1)}, u32[]{:S(2)}, u32[]{:S(2)}) collective-permute-start(bf16[16,8448]{1,0:T(8,128)(2,1)} %pad_maximum_fusion.9), channel_id=1, source_target_pairs={{0,8},{4,12},{1,9},{5,13},{2,10},{6,14},{3,11},{7,15},{16,24},{20,... | collective-permute-start | bytes 811016 | tf_op jit(solution)/shard_map/ppermute | solution.py:25
  109.2 2.3 %collective-permute-done.5 = bf16[16,8448]{1,0:T(8,128)(2,1)} collective-permute-done((bf16[16,8448]{1,0:T(8,128)(2,1)}, bf16[16,8448]{1,0:T(8,128)(2,1)}, u32[]{:S(2)}, u32[]{:S(2)}) %collective-permute-start.5) | collective-permute-done | bytes 270368 | tf_op jit(solution)/shard_map/ppermute | solution.py:25
  111.5 1.1 convert_add_fusion
  114.1 1.6 fusion.31
  115.8 1.7 fusion.30
  117.5 1.2 convert_add_fusion.1
  119.6 0.8 copy-done.18
  120.4 1.6 fusion.33
  122.1 1.7 fusion.32
  123.7 1.5 pad_maximum_fusion.3
  125.3 3.1 %copy.189 = f32[512,1024]{0,1:T(8,128)} copy(f32[512,1024]{1,0:T(8,128)} %bitcast.324) | data formatting | bytes 4194304 | tf_op jit(solution)/shard_map/reshape | solution.py:268
  128.4 8.0 %bitcast_reduce_fusion = (f32[512,2]{0,1:T(2,128)S(1)}, f32[512,1024]{0,1:T(8,128)}) fusion(bf16[512,2048]{0,1:T(8,128)(2,1)S(1)} %bitcast.318, bf16[2048,1024]{1,0:T(8,128)(2,1)} %param.17, bf16[512,1024]{0,1:T(8,128)(2,1)S(1)} %copy-done.7, f32[1024]{0:T(1024)S(1)} %mul.591, f32[512,1024]{0,1:T(8,128)} %copy.189, f32[512,16]{0,1:T(8,128)S(1)} %copy_bitcast_fusion.2, ...), kind=kOutput, calls=%fused_computation.24 | convolution fusion | flops 2154822656 | bytes 13672448 | tf_op jit(solution)/shard_map/dot_general | solution.py:208
  136.5 1.5 pad_maximum_fusion.1
  138.0 3.0 %copy.188 = f32[512,1024]{0,1:T(8,128)} copy(f32[512,1024]{1,0:T(8,128)} %bitcast.325) | data formatting | bytes 4194304 | tf_op jit(solution)/shard_map/reshape | solution.py:268
  141.0 6.6 %bitcast_reduce_fusion.1 = (f32[512,2]{0,1:T(2,128)S(1)}, f32[512,1024]{0,1:T(8,128)S(1)}) fusion(bf16[512,2048]{1,0:T(8,128)(2,1)S(1)} %copy-done.5, bf16[2048,1024]{1,0:T(8,128)(2,1)} %param.17, bf16[512,1024]{0,1:T(8,128)(2,1)S(1)} %copy-done.6, f32[1024]{0:T(1024)S(1)} %mul.591, f32[512,1024]{0,1:T(8,128)} %copy.188, f32[512,16]{0,1:T(8,128)S(1)} %copy-done.27, ...), kind=kOutput, calls=%fused_computation.31 | convolution fusion | flops 2154822656 | bytes 13672448 | tf_op jit(solution)/shard_map/dot_general | solution.py:208
  148.1 1.8 copy-done.57
  149.9 2.5 %convolution_convert_fusion = bf16[512,2048]{1,0:T(8,128)(2,1)S(1)} fusion(bf16[1024,2048]{1,0:T(8,128)(2,1)S(1)} %copy-done.57, bf16[512,1024]{0,1:T(8,128)(2,1)S(1)} %get-tuple-element.62, bf16[512,1024]{0,1:T(8,128)(2,1)S(1)} %get-tuple-element.61), kind=kOutput, calls=%fused_computation | convolution fusion | flops 2150629376 | bytes 8388608 | tf_op jit(solution)/shard_map/dot_general | solution.py:280
  152.4 1.5 copy.254
  153.9 44.5 %reduce-scatter.2.cloned.1.call-done = bf16[1,512,512]{2,1,0:T(8,128)(2,1)} async-done(((bf16[4,512,512]{2,1,0:T(8,128)(2,1)}), bf16[1,512,512]{2,1,0:T(8,128)(2,1)}) %reduce-scatter.2.cloned.1.call-update) | async-done | bytes 524304 | tf_op jit(solution)/shard_map/reduce_scatter | solution.py:282
  (200 shorter events, 14.7 us)
Async XLA Ops:
  6.5 22.6 %copy-start = (bf16[2048,512]{1,0:T(8,128)(2,1)S(1)}, bf16[2048,512]{1,0:T(8,128)(2,1)}, u32[]{:S(2)}) copy-start(bf16[2048,512]{1,0:T(8,128)(2,1)} %param.19) | copy-start | bytes 6291460
  6.5 191.9 %reduce-scatter.2.cloned.1.call-start = ((), (), s32[]{:S(2)}) async-start(), calls=%async_computation.1 | async-start | bytes 2621440 | tf_op jit(solution)/shard_map/reduce_scatter | solution.py:282
  8.3 32.1 %collective-permute-start.1 = (bf16[3,2176]{1,0:T(4,128)(2,1)S(1)}, bf16[3,2176]{1,0:T(4,128)(2,1)S(1)}, u32[]{:S(2)}, u32[]{:S(2)}) collective-permute-start(bf16[3,2176]{1,0:T(4,128)(2,1)S(1)} %pad_maximum_fusion.16), channel_id=1, source_target_pairs={{4,0},{8,4},{12,8},{5,1},{9,5},{13,9},{6,2},{10,6},{14,10},{7,3},{... | collective-permute-start | bytes 39176 | tf_op jit(solution)/shard_map/ppermute | solution.py:25
  9.7 31.0 %collective-permute-start = (bf16[3,2176]{1,0:T(4,128)(2,1)S(1)}, bf16[3,2176]{1,0:T(4,128)(2,1)S(1)}, u32[]{:S(2)}, u32[]{:S(2)}) collective-permute-start(bf16[3,2176]{1,0:T(4,128)(2,1)S(1)} %pad_maximum_fusion.15), channel_id=1, source_target_pairs={{0,4},{4,8},{8,12},{1,5},{5,9},{9,13},{2,6},{6,10},{10,14},{3,7},{... | collective-permute-start | bytes 39176 | tf_op jit(solution)/shard_map/ppermute | solution.py:25
  19.5 6.3 %copy-start.2 = (bf16[512,16,128]{0,2,1:T(8,128)(2,1)S(1)}, bf16[512,16,128]{0,2,1:T(8,128)(2,1)}, u32[]{:S(2)}) copy-start(bf16[512,16,128]{0,2,1:T(8,128)(2,1)} %rev.9) | copy-start | bytes 6291460
  19.5 6.3 %copy-start.13 = (bf16[2048,1024]{1,0:T(8,128)(2,1)S(1)}, bf16[2048,1024]{1,0:T(8,128)(2,1)}, u32[]{:S(2)}) copy-start(bf16[2048,1024]{1,0:T(8,128)(2,1)} %param.18) | copy-start | bytes 12582916
  32.1 2.2 %copy-start.29 = (f32[4,512]{1,0:T(4,128)S(1)}, f32[4,512]{1,0:T(4,128)}, u32[]{:S(2)}) copy-start(f32[4,512]{1,0:T(4,128)} %param.23) | copy-start | bytes 24580
  32.5 7.9 %copy-start.22 = (f32[512,16]{0,1:T(8,128)}, f32[512,16]{0,1:T(8,128)S(1)}, u32[]{:S(2)}) copy-start(f32[512,16]{0,1:T(8,128)S(1)} %compare_select_fusion) | copy-start | bytes 98308
  32.5 6.7 %copy-start.56 = (f32[16]{0:T(128)S(1)}, f32[16]{0:T(128)}, u32[]{:S(2)}) copy-start(f32[16]{0:T(128)} %param.27) | copy-start | bytes 196
  35.3 2.2 %copy-start.30 = (f32[16]{0:T(128)}, f32[16]{0:T(128)S(1)}, u32[]{:S(2)}) copy-start(f32[16]{0:T(128)S(1)} %get-tuple-element.92) | copy-start | bytes 196
  35.3 26.7 %copy-start.35 = (f32[16]{0:T(128)}, f32[16]{0:T(128)S(1)}, u32[]{:S(2)}) copy-start(f32[16]{0:T(128)S(1)} %get-tuple-element.18) | copy-start | bytes 196
  35.3 26.7 %copy-start.37 = (f32[16]{0:T(128)}, f32[16]{0:T(128)S(1)}, u32[]{:S(2)}) copy-start(f32[16]{0:T(128)S(1)} %get-tuple-element.19) | copy-start | bytes 196
  35.3 26.7 %copy-start.39 = (f32[16]{0:T(128)}, f32[16]{0:T(128)S(1)}, u32[]{:S(2)}) copy-start(f32[16]{0:T(128)S(1)} %get-tuple-element.20) | copy-start | bytes 196
  38.2 7.3 %copy-start.24 = (f32[512,2,8]{0,2,1:T(8,128)}, f32[512,2,8]{0,2,1:T(8,128)S(1)}, u32[]{:S(2)}) copy-start(f32[512,2,8]{0,2,1:T(8,128)S(1)} %reshape_reshape.7) | copy-start | bytes 98308
  39.3 6.1 %copy-start.23 = (f32[512,2,8]{0,2,1:T(8,128)}, f32[512,2,8]{0,2,1:T(8,128)S(1)}, u32[]{:S(2)}) copy-start(f32[512,2,8]{0,2,1:T(8,128)S(1)} %reshape_reshape.6) | copy-start | bytes 98308
  41.3 4.3 %copy-start.20 = (bf16[512,1024]{0,1:T(8,128)(2,1)S(1)}, bf16[512,1024]{0,1:T(8,128)(2,1)}, u32[]{:S(2)}) copy-start(bf16[512,1024]{0,1:T(8,128)(2,1)} %multiply_convert_fusion.3) | copy-start | bytes 3145732
  41.3 4.3 %copy-start.21 = (bf16[512,1024]{0,1:T(8,128)(2,1)S(1)}, bf16[512,1024]{0,1:T(8,128)(2,1)}, u32[]{:S(2)}) copy-start(bf16[512,1024]{0,1:T(8,128)(2,1)} %multiply_convert_fusion.1) | copy-start | bytes 3145732
  41.3 4.3 %copy-start.41 = (f32[1024]{0:T(1024)S(1)}, f32[1024]{0:T(1024)}, u32[]{:S(2)}) copy-start(f32[1024]{0:T(1024)} %param.22) | copy-start | bytes 12292
  45.6 5.6 %copy-start.43 = (f32[512]{0:T(512)S(1)}, f32[512]{0:T(512)}, u32[]{:S(2)}) copy-start(f32[512]{0:T(512)} %param.24) | copy-start | bytes 6148
  64.2 35.2 %collective-permute-start.4 = (bf16[16,8448]{1,0:T(8,128)(2,1)}, bf16[16,8448]{1,0:T(8,128)(2,1)S(1)}, u32[]{:S(2)}, u32[]{:S(2)}) collective-permute-start(bf16[16,8448]{1,0:T(8,128)(2,1)} %pad_maximum_fusion.10), channel_id=1, source_target_pairs={{4,0},{8,4},{12,8},{5,1},{9,5},{13,9},{6,2},{10,6},{14,10},{7,3},{... | collective-permute-start | bytes 811016 | tf_op jit(solution)/shard_map/ppermute | solution.py:25
  73.9 2.2 %copy-start.11 = (bf16[512,512]{1,0:T(8,128)(2,1)S(1)}, bf16[512,512]{1,0:T(8,128)(2,1)}, u32[]{:S(2)}) copy-start(bf16[512,512]{1,0:T(8,128)(2,1)} %get-tuple-element.54.c_ref.b_ref) | copy-start | bytes 1572868
  74.0 2.3 %copy-start.10 = (bf16[512,512]{1,0:T(8,128)(2,1)S(1)}, bf16[512,512]{1,0:T(8,128)(2,1)}, u32[]{:S(2)}) copy-start(bf16[512,512]{1,0:T(8,128)(2,1)} %get-tuple-element.53.c_ref.b_ref) | copy-start | bytes 1572868
  77.7 7.6 %copy-start.25 = (bf16[16,8448]{1,0:T(8,128)(2,1)S(1)}, bf16[16,8448]{1,0:T(8,128)(2,1)}, u32[]{:S(2)}) copy-start(bf16[16,8448]{1,0:T(8,128)(2,1)} %pad_maximum_fusion.8) | copy-start | bytes 811012
  85.4 16.6 %collective-permute-start.2 = (bf16[16,8448]{1,0:T(8,128)(2,1)S(1)}, bf16[16,8448]{1,0:T(8,128)(2,1)S(1)}, u32[]{:S(2)}, u32[]{:S(2)}) collective-permute-start(bf16[16,8448]{1,0:T(8,128)(2,1)S(1)} %copy-done.25), channel_id=1, source_target_pairs={{0,4},{4,8},{8,12},{1,5},{5,9},{9,13},{2,6},{6,10},{10,14},{3,7},{... | collective-permute-start | bytes 811016 | tf_op jit(solution)/shard_map/ppermute | solution.py:25
  91.8 7.8 %copy-start.31 = (f32[16]{0:T(128)S(1)}, f32[16]{0:T(128)}, u32[]{:S(2)}) copy-start(f32[16]{0:T(128)} %copy-done.30) | copy-start | bytes 196
  91.8 7.8 %copy-start.46 = (f32[16]{0:T(128)S(1)}, f32[16]{0:T(128)}, u32[]{:S(2)}) copy-start(f32[16]{0:T(128)} %get-tuple-element.78) | copy-start | bytes 196
  91.8 10.4 %copy-start.45 = (f32[16]{0:T(128)S(1)}, f32[16]{0:T(128)}, u32[]{:S(2)}) copy-start(f32[16]{0:T(128)} %get-tuple-element.73) | copy-start | bytes 196
  100.7 10.8 %collective-permute-start.5 = (bf16[16,8448]{1,0:T(8,128)(2,1)}, bf16[16,8448]{1,0:T(8,128)(2,1)}, u32[]{:S(2)}, u32[]{:S(2)}) collective-permute-start(bf16[16,8448]{1,0:T(8,128)(2,1)} %pad_maximum_fusion.11), channel_id=1, source_target_pairs={{8,0},{12,4},{9,1},{13,5},{10,2},{14,6},{11,3},{15,7},{24,16},{28,... | collective-permute-start | bytes 811016 | tf_op jit(solution)/shard_map/ppermute | solution.py:25
  102.3 10.5 %copy-start.9 = (f32[4,16,64,128]{3,2,1,0:T(8,128)S(1)}, f32[4,16,64,128]{3,2,1,0:T(8,128)}, u32[]{:S(2)}) copy-start(f32[4,16,64,128]{3,2,1,0:T(8,128)} %shard_map.148) | copy-start | bytes 6291460
  102.3 10.5 %copy-start.36 = (f32[16]{0:T(128)S(1)}, f32[16]{0:T(128)}, u32[]{:S(2)}) copy-start(f32[16]{0:T(128)} %copy-done.35) | copy-start | bytes 196
  102.3 10.5 %copy-start.38 = (f32[16]{0:T(128)S(1)}, f32[16]{0:T(128)}, u32[]{:S(2)}) copy-start(f32[16]{0:T(128)} %copy-done.37) | copy-start | bytes 196
  102.3 10.5 %copy-start.40 = (f32[16]{0:T(128)S(1)}, f32[16]{0:T(128)}, u32[]{:S(2)}) copy-start(f32[16]{0:T(128)} %copy-done.39) | copy-start | bytes 196
  102.3 10.5 %copy-start.53 = (f32[16]{0:T(128)S(1)}, f32[16]{0:T(128)}, u32[]{:S(2)}) copy-start(f32[16]{0:T(128)} %get-tuple-element.90) | copy-start | bytes 196
  102.4 10.5 %copy-start.54 = (f32[16]{0:T(128)S(1)}, f32[16]{0:T(128)}, u32[]{:S(2)}) copy-start(f32[16]{0:T(128)} %get-tuple-element.91) | copy-start | bytes 196
  102.4 10.5 %copy-start.55 = (f32[16]{0:T(128)S(1)}, f32[16]{0:T(128)}, u32[]{:S(2)}) copy-start(f32[16]{0:T(128)} %get-tuple-element.93) | copy-start | bytes 196
  103.2 14.2 %collective-permute-start.3 = (bf16[16,8448]{1,0:T(8,128)(2,1)}, bf16[16,8448]{1,0:T(8,128)(2,1)}, u32[]{:S(2)}, u32[]{:S(2)}) collective-permute-start(bf16[16,8448]{1,0:T(8,128)(2,1)} %pad_maximum_fusion.9), channel_id=1, source_target_pairs={{0,8},{4,12},{1,9},{5,13},{2,10},{6,14},{3,11},{7,15},{16,24},{20,... | collective-permute-start | bytes 811016 | tf_op jit(solution)/shard_map/ppermute | solution.py:25
  120.4 3.3 %copy-start.14 = (f32[4,128,512]{2,1,0:T(8,128)S(1)}, f32[4,128,512]{2,1,0:T(8,128)}, u32[]{:S(2)}) copy-start(f32[4,128,512]{2,1,0:T(8,128)} %fusion.31) | copy-start | bytes 3145732
  120.4 3.3 %copy-start.15 = (f32[4,128,512]{2,1,0:T(8,128)S(1)}, f32[4,128,512]{2,1,0:T(8,128)}, u32[]{:S(2)}) copy-start(f32[4,128,512]{2,1,0:T(8,128)} %fusion.30) | copy-start | bytes 3145732
  125.3 3.1 %copy-start.3 = (bf16[512,16,128]{0,2,1:T(8,128)(2,1)S(1)}, bf16[512,16,128]{0,2,1:T(8,128)(2,1)}, u32[]{:S(2)}) copy-start(bf16[512,16,128]{0,2,1:T(8,128)(2,1)} %rev.9) | copy-start | bytes 6291460
  125.3 3.1 %copy-start.7 = (bf16[512,1024]{0,1:T(8,128)(2,1)S(1)}, bf16[512,1024]{0,1:T(8,128)(2,1)}, u32[]{:S(2)}) copy-start(bf16[512,1024]{0,1:T(8,128)(2,1)} %get-tuple-element.48) | copy-start | bytes 3145732
  128.4 8.0 %copy-start.16 = (f32[4,128,512]{2,1,0:T(8,128)S(1)}, f32[4,128,512]{2,1,0:T(8,128)}, u32[]{:S(2)}) copy-start(f32[4,128,512]{2,1,0:T(8,128)} %fusion.33) | copy-start | bytes 3145732
  128.4 8.0 %copy-start.17 = (f32[4,128,512]{2,1,0:T(8,128)S(1)}, f32[4,128,512]{2,1,0:T(8,128)}, u32[]{:S(2)}) copy-start(f32[4,128,512]{2,1,0:T(8,128)} %fusion.32) | copy-start | bytes 3145732
  138.0 3.1 %copy-start.5 = (bf16[512,2048]{1,0:T(8,128)(2,1)S(1)}, bf16[512,2048]{1,0:T(8,128)(2,1)}, u32[]{:S(2)}) copy-start(bf16[512,2048]{1,0:T(8,128)(2,1)} %param.15) | copy-start | bytes 6291460
  138.0 3.1 %copy-start.6 = (bf16[512,1024]{0,1:T(8,128)(2,1)S(1)}, bf16[512,1024]{0,1:T(8,128)(2,1)}, u32[]{:S(2)}) copy-start(bf16[512,1024]{0,1:T(8,128)(2,1)} %get-tuple-element.47) | copy-start | bytes 3145732
  138.0 3.1 %copy-start.27 = (f32[512,16]{0,1:T(8,128)S(1)}, f32[512,16]{0,1:T(8,128)}, u32[]{:S(2)}) copy-start(f32[512,16]{0,1:T(8,128)} %copy_bitcast_fusion.3) | copy-start | bytes 98308
  141.0 6.6 %copy-start.12 = (f32[512,1024]{0,1:T(8,128)S(1)}, f32[512,1024]{0,1:T(8,128)}, u32[]{:S(2)}) copy-start(f32[512,1024]{0,1:T(8,128)} %get-tuple-element.85) | copy-start | bytes 6291460
  141.0 6.6 %copy-start.42 = (f32[1024]{0:T(1024)S(1)}, f32[1024]{0:T(1024)}, u32[]{:S(2)}) copy-start(f32[1024]{0:T(1024)} %param.28) | copy-start | bytes 12292
  152.4 46.1 %copy-start.1 = (bf16[2048,512]{1,0:T(8,128)(2,1)S(1)}, bf16[2048,512]{1,0:T(8,128)(2,1)}, u32[]{:S(2)}) copy-start(bf16[2048,512]{1,0:T(8,128)(2,1)} %param.19) | copy-start | bytes 6291460
  (18 other events, 28.1 us)
Sparse Core Ops, SparseCore 0:
  154.0 44.3 reduce-scatter.1

commit v4 on v3

--- a/solution.py
+++ b/solution.py
@@ -144,6 +144,47 @@
         out_shape=jax.ShapeDtypeStruct((groups * width_g, rows), F32),
         interpret=interpret,
     )(state_c, state_c, values_t, acc_g, acc_t, delta_t)
+
+
+def block_finish(intra_t, state_c, values_t, acc_t, start, skip_col, interpret=False):
+    rows = values_t.shape[1]
+    groups, per_group, _ = acc_t.shape
+    blocks = rows // Q
+    width_g = per_group * P_SIZE
+
+    def kernel(y_ref, c_ref, xt_ref, at_ref, s_ref, k_ref, o_ref):
+        c_blk = c_ref[...]
+        dims = (((1,), (1,)), ((), ()))
+        for j in range(per_group):
+            lo_row, hi_row = j * P_SIZE, (j + 1) * P_SIZE
+            s_j = s_ref[0, j]
+            s_hi = s_j.astype(BF16)
+            s_lo = (s_j - s_hi.astype(F32)).astype(BF16)
+            inter = lax.dot_general(s_hi, c_blk, dims, preferred_element_type=F32) + lax.dot_general(
+                s_lo, c_blk, dims, preferred_element_type=F32
+            )
+            inter = inter * jnp.exp(at_ref[0, j : j + 1, :])
+            o_ref[lo_row:hi_row, :] = (
+                y_ref[lo_row:hi_row, :]
+                + inter
+                + k_ref[lo_row:hi_row, :] * xt_ref[lo_row:hi_row, :].astype(F32)
+            )
+
+    return pl.pallas_call(
+        kernel,
+        grid=(blocks, groups),
+        in_specs=[
+            pl.BlockSpec((width_g, Q), lambda b, g: (g, b)),
+            pl.BlockSpec((Q, N), lambda b, g: (b, 2 * g + 1)),
+            pl.BlockSpec((width_g, Q), lambda b, g: (g, b)),
+            pl.BlockSpec((1, per_group, Q), lambda b, g: (g, 0, b)),
+            pl.BlockSpec((1, per_group, P_SIZE, N), lambda b, g: (b, g, 0, 0)),
+            pl.BlockSpec((width_g, 1), lambda b, g: (g, 0)),
+        ],
+        out_specs=pl.BlockSpec((width_g, Q), lambda b, g: (g, b)),
+        out_shape=jax.ShapeDtypeStruct((groups * width_g, rows), F32),
+        interpret=interpret,
+    )(intra_t, state_c, values_t, acc_t, start, skip_col)
 
 
 def conv_silu(padded, kernel, offset, count, forward):
@@ -253,21 +294,12 @@
             log_before = log_before + blk[index]
         total = log_before
         carried = exclusive_carry(total, running, sign)
-        intra = block_intra(state_c, values_t, acc_g, acc_t, delta_t, forward).T
+        intra_t = block_intra(state_c, values_t, acc_g, acc_t, delta_t, forward)
         start = jnp.stack(
             [local_start[index] + entering[index][:, None, None] * carried for index in range(blocks)]
         )
-        start = start.reshape(blocks, groups, per_group * P_SIZE, N)
-        c_f32 = c_vec.astype(F32)
-        inter = jnp.concatenate(
-            [
-                jnp.einsum("btn,bkn->btk", c_f32[:, :, group], start[:, group], precision=HIGHEST)
-                for group in range(groups)
-            ],
-            axis=2,
-        ).reshape(rows, heads, P_SIZE) * jnp.exp(acc).reshape(rows, heads)[:, :, None]
-        x = values_c.astype(F32).reshape(rows, heads, P_SIZE)
-        outputs = intra.reshape(rows, heads, P_SIZE) + inter + skip_gain[None, :, None] * x
+        skip_col = jnp.repeat(skip_gain, P_SIZE)[:, None]
+        outputs = block_finish(intra_t, state_c, values_t, acc_t, start, skip_col).T
         gated = outputs.reshape(rows, heads * P_SIZE) * jax.nn.silu(gate_in.astype(F32))
         grouped = gated.reshape(rows, groups, per_group * P_SIZE)
         scale = lax.rsqrt(jnp.mean(grouped * grouped, axis=-1, keepdims=True) + EPSILON)

time: 206 us -> 202 us (0.981)
  Pallas kernels: 28.6 us -> 45.8 us
  local copies, waits for them, and re-layouts: 26.8 us -> 17.7 us
  matrix products: 46.3 us -> 37.9 us
  other arithmetic: 24.5 us -> 19.2 us
    pallas_call x0 -> x2, Pallas kernels: none -> 17.3 us  [block_finish(): pl.pallas_call(kernel, grid=(blocks, groups), in_specs=[pl.BlockSpec((wid...]
    dot_general x4 -> x0, matrix products: 6.68 us -> none  [local_scan(): jnp.einsum('btn,bkn->btk', c_f32[:, :, group], start[:, group], precision...]
    reshape x4 -> x0, local copies, waits for them, and re-layouts: 6.43 us -> none  [the longest x2 6.18 us: local_scan(): inter = jnp.concatenate([jnp.einsum('btn,bkn->btk', c_f32[:, :, group], s...]
    transpose x0 -> x1, other arithmetic: none -> 5.59 us  [local_scan(): values_t = values_c.T]
    convert_element_type x2 -> x1, other arithmetic: 7.96 us -> 2.4 us  [conv_silu(): return jax.nn.silu(total).astype(BF16)]
    concatenate x2 -> x0, other arithmetic: 3.04 us -> none  [local_scan(): jnp.concatenate([jnp.einsum('btn,bkn->btk', c_f32[:, :, group], start[:,...]
    another operation x2, other arithmetic: 0.34 us -> 2.92 us  [local_scan(): jnp.stack([local_start[index] + entering[index][:, None, None] * carried...]
    add x2 -> x0, other arithmetic: 2.32 us -> none  [exclusive_carry(): x_state = jnp.exp(x_log)[:, None] * r_state + x_state]
  transfers between devices with their start and end apart: 7 -> 7, of which waited for: 2 -> 2; matrix products, arithmetic and copies ran while one was open for 20% -> 20% of each run, Pallas kernels for 11% -> 15%
where the time goes in v4:
time: 202 us; the launch traced here: 200 us
  waiting for transfers between devices  48.3 us (24%)
  Pallas kernels  45.8 us (23%)
  matrix products  37.9 us (19%)
  other arithmetic  19.2 us (10%)
  local copies, waits for them, and re-layouts  17.7 us (9%)
  starting transfers between devices  17.3 us (9%)
  between operations  14 us (7%)
    reduce_scatter x1, waiting for transfers between devices, on_device(): summed = lax.psum_scatter(partial, 'chan', scatter_dimension=0, tiled=True)  44.5 us
    pallas_call x2, Pallas kernels, block_finish(): pl.pallas_call(kernel, grid=(blocks, groups), in_specs=[pl.BlockSpec((wid...  17.3 us
    ppermute x6, starting transfers between devices, shifted(): return lax.ppermute(value, axis, pairs)  17.3 us
    pallas_call x2, Pallas kernels, block_intra(): pl.pallas_call(kernel, grid=(blocks, groups), in_specs=[pl.BlockSpec((Q,...  15.2 us
    pallas_call x2, Pallas kernels, block_states(): pl.pallas_call(kernel, grid=(blocks, groups), in_specs=[pl.BlockSpec((Q,...  13.3 us
    dot_general x2, matrix products, project(): gate_in = jnp.dot(source, w_gate, preferred_element_type=F32).astype(BF16)  12.9 us
    dot_general x2, matrix products, project(): jnp.dot(source, w_values, preferred_element_type=F32) * known[:, None]  9.7 us
    transpose x1, other arithmetic, local_scan(): values_t = values_c.T  5.59 us
  transfers between devices with their start and end apart: 7, of which 2 were waited for; matrix products, arithmetic and copies ran while one was open for 20% of the time, Pallas kernels for 15%

profile of v4, /device:TPU:0, one launch (start us, length us, event | category | flops | bytes accessed | tf_op | source)
XLA Modules:
  0.0 200.2 jit_solution(2172317307528375143)
XLA Ops:
  6.5 0.8 compare_select_fusion.2
  7.5 0.8 fusion.72
  8.3 1.3 collective-permute-start.1
  9.7 3.0 %collective-permute-start = (bf16[3,2176]{1,0:T(4,128)(2,1)S(1)}, bf16[3,2176]{1,0:T(4,128)(2,1)S(1)}, u32[]{:S(2)}, u32[]{:S(2)}) collective-permute-start(bf16[3,2176]{1,0:T(4,128)(2,1)S(1)} %pad_maximum_fusion.13), channel_id=1, source_target_pairs={{0,4},{4,8},{8,12},{1,5},{5,9},{9,13},{2,6},{6,10},{10,14},{3,7},{... | collective-permute-start | bytes 39176 | tf_op jit(solution)/shard_map/ppermute | solution.py:25
  12.8 3.6 %convert_bitcast_fusion = bf16[512,16,128]{0,2,1:T(8,128)(2,1)} fusion(bf16[512,2048]{1,0:T(8,128)(2,1)} %param.15), kind=kOutput, calls=%fused_computation.30 | convolution fusion | flops 269516800 | bytes 4194304 | tf_op jit(solution)/shard_map/rki,ij->rkj/dot_general | solution.py:228
  16.4 3.1 %rev.9 = bf16[512,16,128]{0,2,1:T(8,128)(2,1)} reverse(bf16[512,16,128]{0,2,1:T(8,128)(2,1)} %convert_bitcast_fusion), dimensions={1} | reverse | bytes 4194304 | tf_op jit(solution)/shard_map/jit(_flip)/rev | solution.py:231
  19.5 6.3 %multiply_convert_fusion.3 = bf16[512,1024]{0,1:T(8,128)(2,1)} fusion(bf16[512,2048]{1,0:T(8,128)(2,1)} %param.15, bf16[2048,1024]{1,0:T(8,128)(2,1)} %param.18, f32[512]{0:T(512)S(1)} %get-tuple-element.63), kind=kOutput, calls=%fused_computation.32 | convolution fusion | flops 2148532224 | bytes 7342080 | tf_op jit(solution)/shard_map/dot_general | solution.py:250
  25.8 3.4 %multiply_convert_fusion.1 = bf16[512,1024]{0,1:T(8,128)(2,1)} fusion(bf16[512,2048]{0,1:T(8,128)(2,1)S(1)} %bitcast.231, bf16[2048,1024]{1,0:T(8,128)(2,1)S(1)} %copy-done.8, f32[512]{0:T(512)S(1)} %get-tuple-element.63), kind=kOutput, calls=%fused_computation.29 | convolution fusion | flops 2148532224 | bytes 7342080 | tf_op jit(solution)/shard_map/dot_general | solution.py:250
  29.2 1.3 convolution_convert_fusion.3
  30.8 1.3 convolution_convert_fusion.4
  32.1 0.4 compare_select_fusion
  32.6 1.3 broadcast_multiply_fusion.1
  35.3 1.0 copy.121.a_ref
  36.4 1.3 broadcast_in_dim_reshape.5.k_ref
  37.7 1.0 copy.112.a_ref
  39.3 0.4 convolution_convert_fusion.8
  39.7 4.1 %fusion.17 = bf16[6,1024]{0,1:T(8,128)(2,1)S(1)} fusion(bf16[2048,1024]{1,0:T(8,128)(2,1)} %param.18, f32[6]{0:T(128)S(1)} %maximum_convert_fusion, bf16[3,2048]{1,0:T(4,128)(2,1)S(1)} %bitcast.262, bf16[3,2048]{1,0:T(4,128)(2,1)S(1)} %slice.267), kind=kOutput, calls=%fused_computation.46 | convolution fusion | flops 25227264 | bytes 4231192 | tf_op jit(solution)/shard_map/dot_general | solution.py:244
  44.0 5.6 %fusion.26 = (bf16[1024,512]{1,0:T(8,128)(2,1)}, bf16[1024,512]{1,0:T(8,128)(2,1)}) fusion(bf16[512,1024]{0,1:T(8,128)(2,1)S(1)} %copy-done.10, f32[1024]{0:T(1024)S(1)} %bitcast.266, bf16[3,1024]{0,1:T(8,128)(2,1)S(1)} %get-tuple-element.45, f32[1024]{0:T(1024)S(1)} %bitcast.267, f32[1024]{0:T(1024)S(1)} %bitcast.265, f32[1024]{0:T(1024)S(1)} %bitcast.264, ...), kind=kLoop, calls=%fused_computation.65 | loop fusion | flops 27262976 | bytes 4227072 | tf_op jit(solution)/shard_map/transpose | solution.py:281
  49.6 2.4 %multiply_convert_fusion.5 = (bf16[512,512]{1,0:T(8,128)(2,1)}, bf16[512,512]{1,0:T(8,128)(2,1)}) fusion(bf16[512,512]{1,0:T(8,128)(2,1)S(1)} %convolution_convert_fusion.4, bf16[3,512]{1,0:T(4,128)(2,1)S(1)} %get-tuple-element.55, f32[512]{0:T(512)S(1)} %bitcast.270, f32[512]{0:T(512)S(1)} %bitcast.271, f32[512]{0:T(512)S(1)} %bitcast.269, ...), kind=kLoop, calls=%fused_computation.64 | loop fusion | flops 13631488 | bytes 2113536 | tf_op jit(solution)/shard_map/convert_element_type | solution.py:196
  52.0 6.7 %shard_map.149 = f32[4,16,64,128]{3,2,1,0:T(8,128)} custom-call(bf16[512,512]{1,0:T(8,128)(2,1)} %get-tuple-element.54.c_ref.b_ref, bf16[1024,512]{1,0:T(8,128)(2,1)} %get-tuple-element.48.xt_ref, f32[2,8,512]{2,1,0:T(8,128)} %bitcast.254, f32[2,8,512]{2,1,0:T(8,128)} %bitcast.257), custom_call_target="tpu_custom_call" | custom-call | tf_op jit(solution)/shard_map/pallas_call | solution.py:93
  58.6 1.7 fusion.71
  60.4 1.3 fusion.69
  61.8 0.7 pad_maximum_fusion.8
  62.5 1.3 collective-permute-start.4
  63.8 6.7 %shard_map.146 = f32[4,16,64,128]{3,2,1,0:T(8,128)} custom-call(bf16[512,512]{1,0:T(8,128)(2,1)} %get-tuple-element.53.c_ref.b_ref, bf16[1024,512]{1,0:T(8,128)(2,1)} %get-tuple-element.47.xt_ref, f32[2,8,512]{2,1,0:T(8,128)} %bitcast.250, f32[2,8,512]{2,1,0:T(8,128)} %bitcast.259), custom_call_target="tpu_custom_call" | custom-call | tf_op jit(solution)/shard_map/pallas_call | solution.py:93
  70.5 1.7 fusion.70
  72.2 1.3 fusion.68
  73.6 7.6 %shard_map.148.y_ref = f32[1024,512]{1,0:T(8,128)} custom-call(bf16[512,512]{1,0:T(8,128)(2,1)} %get-tuple-element.54.c_ref.b_ref, bf16[512,512]{1,0:T(8,128)(2,1)} %get-tuple-element.54.c_ref.b_ref, bf16[1024,512]{1,0:T(8,128)(2,1)} %get-tuple-element.48.xt_ref, f32[2,512,8]{2,1,0:T(8,128)} %copy.121.a_ref, f32[2,8,512]{2,1,0:T(8,128)} %bitcast.255, ...), custom_call_target="tpu_custom_call" | custom-call | tf_op jit(solution)/shard_map/pallas_call | solution.py:132
  81.3 5.1 %collective-permute-start.2 = (bf16[16,8448]{1,0:T(8,128)(2,1)S(1)}, bf16[16,8448]{1,0:T(8,128)(2,1)S(1)}, u32[]{:S(2)}, u32[]{:S(2)}) collective-permute-start(bf16[16,8448]{1,0:T(8,128)(2,1)S(1)} %pad_maximum_fusion.6), channel_id=1, source_target_pairs={{0,4},{4,8},{8,12},{1,5},{5,9},{9,13},{2,6},{6,10},{10,14},{3,7},{... | collective-permute-start | bytes 811016 | tf_op jit(solution)/shard_map/ppermute | solution.py:25
  86.4 7.6 %shard_map.145.y_ref = f32[1024,512]{1,0:T(8,128)} custom-call(bf16[512,512]{1,0:T(8,128)(2,1)} %get-tuple-element.53.c_ref.b_ref, bf16[512,512]{1,0:T(8,128)(2,1)} %get-tuple-element.53.c_ref.b_ref, bf16[1024,512]{1,0:T(8,128)(2,1)} %get-tuple-element.47.xt_ref, f32[2,512,8]{2,1,0:T(8,128)} %copy.112.a_ref, f32[2,8,512]{2,1,0:T(8,128)} %bitcast.251, ...), custom_call_target="tpu_custom_call" | custom-call | tf_op jit(solution)/shard_map/pallas_call | solution.py:132
  94.5 0.8 pad_maximum_fusion.9
  95.2 1.3 collective-permute-start.5
  97.0 5.3 %collective-permute-start.3 = (bf16[16,8448]{1,0:T(8,128)(2,1)S(1)}, bf16[16,8448]{1,0:T(8,128)(2,1)S(1)}, u32[]{:S(2)}, u32[]{:S(2)}) collective-permute-start(bf16[16,8448]{1,0:T(8,128)(2,1)S(1)} %pad_maximum_fusion.7), channel_id=1, source_target_pairs={{0,8},{4,12},{1,9},{5,13},{2,10},{6,14},{3,11},{7,15},{16,24},{20,... | collective-permute-start | bytes 811016 | tf_op jit(solution)/shard_map/ppermute | solution.py:25
  102.3 3.7 %collective-permute-done.5 = bf16[16,8448]{1,0:T(8,128)(2,1)} collective-permute-done((bf16[16,8448]{1,0:T(8,128)(2,1)}, bf16[16,8448]{1,0:T(8,128)(2,1)}, u32[]{:S(2)}, u32[]{:S(2)}) %collective-permute-start.5) | collective-permute-done | bytes 270368 | tf_op jit(solution)/shard_map/ppermute | solution.py:25
  106.1 1.1 fusion.33
  107.3 0.3 multiply_add_fusion.2
  107.6 1.4 pad_maximum_fusion.1.s_ref
  109.0 8.6 %shard_map.150 = f32[1024,512]{1,0:T(8,128)} custom-call(f32[1024,512]{1,0:T(8,128)} %shard_map.148.y_ref, bf16[512,512]{1,0:T(8,128)(2,1)} %get-tuple-element.54.c_ref.b_ref, bf16[1024,512]{1,0:T(8,128)(2,1)} %get-tuple-element.48.xt_ref, f32[2,8,512]{2,1,0:T(8,128)} %bitcast.256, f32[4,16,64,128]{3,2,1,0:T(8,128)} %pad_maximum_fusion.1.s_ref, ...), custom_call_target="tpu_custom_call" | custom-call | tf_op jit(solution)/shard_map/pallas_call | solution.py:173
  117.7 7.1 %bitcast_reduce_fusion = (f32[512,2]{0,1:T(2,128)S(1)}, f32[512,1024]{0,1:T(8,128)}) fusion(bf16[512,2048]{0,1:T(8,128)(2,1)S(1)} %bitcast.234, bf16[2048,1024]{1,0:T(8,128)(2,1)} %param.17, f32[1024,512]{1,0:T(8,128)} %shard_map.150), kind=kOutput, calls=%fused_computation.22 | convolution fusion | flops 2152201216 | bytes 10489856 | tf_op jit(solution)/shard_map/dot_general | solution.py:249
  125.0 1.3 copy-done.4
  126.6 1.5 pad_maximum_fusion.s_ref
  128.1 8.6 %shard_map.147 = f32[1024,512]{1,0:T(8,128)} custom-call(f32[1024,512]{1,0:T(8,128)} %shard_map.145.y_ref, bf16[512,512]{1,0:T(8,128)(2,1)} %get-tuple-element.53.c_ref.b_ref, bf16[1024,512]{1,0:T(8,128)(2,1)} %get-tuple-element.47.xt_ref, f32[2,8,512]{2,1,0:T(8,128)} %bitcast.252, f32[4,16,64,128]{3,2,1,0:T(8,128)} %pad_maximum_fusion.s_ref, ...), custom_call_target="tpu_custom_call" | custom-call | tf_op jit(solution)/shard_map/pallas_call | solution.py:173
  136.8 5.8 %bitcast_reduce_fusion.1 = (f32[512,2]{0,1:T(2,128)S(1)}, f32[512,1024]{0,1:T(8,128)S(1)}) fusion(bf16[512,2048]{1,0:T(8,128)(2,1)S(1)} %copy-done.7, bf16[2048,1024]{1,0:T(8,128)(2,1)} %param.17, f32[1024,512]{1,0:T(8,128)} %shard_map.147), kind=kOutput, calls=%fused_computation.26 | convolution fusion | flops 2152201216 | bytes 10489856 | tf_op jit(solution)/shard_map/dot_general | solution.py:249
  142.6 0.4 fusion.14
  143.0 1.8 copy-done.23
  144.8 2.5 %convolution_convert_fusion = bf16[512,2048]{1,0:T(8,128)(2,1)S(1)} fusion(bf16[1024,2048]{1,0:T(8,128)(2,1)S(1)} %copy-done.23, bf16[512,1024]{0,1:T(8,128)(2,1)S(1)} %get-tuple-element.62, bf16[512,1024]{0,1:T(8,128)(2,1)S(1)} %get-tuple-element.61), kind=kOutput, calls=%fused_computation | convolution fusion | flops 2150629376 | bytes 8388608 | tf_op jit(solution)/shard_map/dot_general | solution.py:312
  147.3 1.5 copy.190
  148.9 44.5 %reduce-scatter.2.cloned.1.call-done = bf16[1,512,512]{2,1,0:T(8,128)(2,1)} async-done(((bf16[4,512,512]{2,1,0:T(8,128)(2,1)}), bf16[1,512,512]{2,1,0:T(8,128)(2,1)}) %reduce-scatter.2.cloned.1.call-update) | async-done | bytes 524304 | tf_op jit(solution)/shard_map/reduce_scatter | solution.py:314
  (116 shorter events, 4.7 us)
Async XLA Ops:
  6.5 22.7 %copy-start = (bf16[2048,512]{1,0:T(8,128)(2,1)S(1)}, bf16[2048,512]{1,0:T(8,128)(2,1)}, u32[]{:S(2)}) copy-start(bf16[2048,512]{1,0:T(8,128)(2,1)} %param.19) | copy-start | bytes 6291460
  6.5 186.8 %reduce-scatter.2.cloned.1.call-start = ((), (), s32[]{:S(2)}) async-start(), calls=%async_computation.1 | async-start | bytes 2621440 | tf_op jit(solution)/shard_map/reduce_scatter | solution.py:314
  8.3 30.4 %collective-permute-start.1 = (bf16[3,2176]{1,0:T(4,128)(2,1)S(1)}, bf16[3,2176]{1,0:T(4,128)(2,1)S(1)}, u32[]{:S(2)}, u32[]{:S(2)}) collective-permute-start(bf16[3,2176]{1,0:T(4,128)(2,1)S(1)} %pad_maximum_fusion.14), channel_id=1, source_target_pairs={{4,0},{8,4},{12,8},{5,1},{9,5},{13,9},{6,2},{10,6},{14,10},{7,3},{... | collective-permute-start | bytes 39176 | tf_op jit(solution)/shard_map/ppermute | solution.py:25
  9.7 29.4 %collective-permute-start = (bf16[3,2176]{1,0:T(4,128)(2,1)S(1)}, bf16[3,2176]{1,0:T(4,128)(2,1)S(1)}, u32[]{:S(2)}, u32[]{:S(2)}) collective-permute-start(bf16[3,2176]{1,0:T(4,128)(2,1)S(1)} %pad_maximum_fusion.13), channel_id=1, source_target_pairs={{0,4},{4,8},{8,12},{1,5},{5,9},{9,13},{2,6},{6,10},{10,14},{3,7},{... | collective-permute-start | bytes 39176 | tf_op jit(solution)/shard_map/ppermute | solution.py:25
  19.5 6.3 %copy-start.2 = (bf16[512,16,128]{0,2,1:T(8,128)(2,1)S(1)}, bf16[512,16,128]{0,2,1:T(8,128)(2,1)}, u32[]{:S(2)}) copy-start(bf16[512,16,128]{0,2,1:T(8,128)(2,1)} %rev.9) | copy-start | bytes 6291460
  19.5 6.3 %copy-start.8 = (bf16[2048,1024]{1,0:T(8,128)(2,1)S(1)}, bf16[2048,1024]{1,0:T(8,128)(2,1)}, u32[]{:S(2)}) copy-start(bf16[2048,1024]{1,0:T(8,128)(2,1)} %param.18) | copy-start | bytes 12582916
  29.2 1.6 copy-start.6
  30.8 1.3 copy-start.24
  30.8 1.3 copy-start.15
  30.8 1.3 copy-start.21
  32.1 2.2 %copy-start.16 = (f32[4,1024]{1,0:T(4,128)S(1)}, f32[4,1024]{1,0:T(4,128)}, u32[]{:S(2)}) copy-start(f32[4,1024]{1,0:T(4,128)} %param.21) | copy-start | bytes 49156
  32.1 2.2 %copy-start.17 = (f32[4,512]{1,0:T(4,128)S(1)}, f32[4,512]{1,0:T(4,128)}, u32[]{:S(2)}) copy-start(f32[4,512]{1,0:T(4,128)} %param.23) | copy-start | bytes 24580
  32.5 5.2 %copy-start.14 = (f32[512,16]{0,1:T(8,128)}, f32[512,16]{0,1:T(8,128)S(1)}, u32[]{:S(2)}) copy-start(f32[512,16]{0,1:T(8,128)S(1)} %compare_select_fusion) | copy-start | bytes 98308
  32.6 3.7 %copy-start.22 = (f32[16]{0:T(128)S(1)}, f32[16]{0:T(128)}, u32[]{:S(2)}) copy-start(f32[16]{0:T(128)} %param.27) | copy-start | bytes 196
  35.3 8.5 %copy-start.13 = (f32[512,2,8]{0,2,1:T(8,128)}, f32[512,2,8]{0,2,1:T(8,128)S(1)}, u32[]{:S(2)}) copy-start(f32[512,2,8]{0,2,1:T(8,128)S(1)} %reshape_reshape.7) | copy-start | bytes 98308
  37.7 6.1 %copy-start.12 = (f32[512,2,8]{0,2,1:T(8,128)}, f32[512,2,8]{0,2,1:T(8,128)S(1)}, u32[]{:S(2)}) copy-start(f32[512,2,8]{0,2,1:T(8,128)S(1)} %reshape_reshape.6) | copy-start | bytes 98308
  39.7 4.3 %copy-start.10 = (bf16[512,1024]{0,1:T(8,128)(2,1)S(1)}, bf16[512,1024]{0,1:T(8,128)(2,1)}, u32[]{:S(2)}) copy-start(bf16[512,1024]{0,1:T(8,128)(2,1)} %multiply_convert_fusion.3) | copy-start | bytes 3145732
  39.7 4.3 %copy-start.11 = (bf16[512,1024]{0,1:T(8,128)(2,1)S(1)}, bf16[512,1024]{0,1:T(8,128)(2,1)}, u32[]{:S(2)}) copy-start(bf16[512,1024]{0,1:T(8,128)(2,1)} %multiply_convert_fusion.1) | copy-start | bytes 3145732
  39.7 4.3 %copy-start.18 = (f32[1024]{0:T(1024)S(1)}, f32[1024]{0:T(1024)}, u32[]{:S(2)}) copy-start(f32[1024]{0:T(1024)} %param.22) | copy-start | bytes 12292
  44.0 5.6 %copy-start.20 = (f32[512]{0:T(512)S(1)}, f32[512]{0:T(512)}, u32[]{:S(2)}) copy-start(f32[512]{0:T(512)} %param.24) | copy-start | bytes 6148
  62.5 31.4 %collective-permute-start.4 = (bf16[16,8448]{1,0:T(8,128)(2,1)}, bf16[16,8448]{1,0:T(8,128)(2,1)S(1)}, u32[]{:S(2)}, u32[]{:S(2)}) collective-permute-start(bf16[16,8448]{1,0:T(8,128)(2,1)} %pad_maximum_fusion.8), channel_id=1, source_target_pairs={{4,0},{8,4},{12,8},{5,1},{9,5},{13,9},{6,2},{10,6},{14,10},{7,3},{... | collective-permute-start | bytes 811016 | tf_op jit(solution)/shard_map/ppermute | solution.py:25
  81.3 15.2 %collective-permute-start.2 = (bf16[16,8448]{1,0:T(8,128)(2,1)S(1)}, bf16[16,8448]{1,0:T(8,128)(2,1)S(1)}, u32[]{:S(2)}, u32[]{:S(2)}) collective-permute-start(bf16[16,8448]{1,0:T(8,128)(2,1)S(1)} %pad_maximum_fusion.6), channel_id=1, source_target_pairs={{0,4},{4,8},{8,12},{1,5},{5,9},{9,13},{2,6},{6,10},{10,14},{3,7},{... | collective-permute-start | bytes 811016 | tf_op jit(solution)/shard_map/ppermute | solution.py:25
  94.5 12.8 %copy-start.5 = (f32[4,16,64,128]{3,2,1,0:T(8,128)S(1)}, f32[4,16,64,128]{3,2,1,0:T(8,128)}, u32[]{:S(2)}) copy-start(f32[4,16,64,128]{3,2,1,0:T(8,128)} %shard_map.149) | copy-start | bytes 6291460
  95.2 10.8 %collective-permute-start.5 = (bf16[16,8448]{1,0:T(8,128)(2,1)}, bf16[16,8448]{1,0:T(8,128)(2,1)}, u32[]{:S(2)}, u32[]{:S(2)}) collective-permute-start(bf16[16,8448]{1,0:T(8,128)(2,1)} %pad_maximum_fusion.9), channel_id=1, source_target_pairs={{8,0},{12,4},{9,1},{13,5},{10,2},{14,6},{11,3},{15,7},{24,16},{28,... | collective-permute-start | bytes 811016 | tf_op jit(solution)/shard_map/ppermute | solution.py:25
  97.0 27.7 %collective-permute-start.3 = (bf16[16,8448]{1,0:T(8,128)(2,1)S(1)}, bf16[16,8448]{1,0:T(8,128)(2,1)S(1)}, u32[]{:S(2)}, u32[]{:S(2)}) collective-permute-start(bf16[16,8448]{1,0:T(8,128)(2,1)S(1)} %pad_maximum_fusion.7), channel_id=1, source_target_pairs={{0,8},{4,12},{1,9},{5,13},{2,10},{6,14},{3,11},{7,15},{16,24},{20,... | collective-permute-start | bytes 811016 | tf_op jit(solution)/shard_map/ppermute | solution.py:25
  109.0 8.7 %copy-start.3 = (bf16[512,16,128]{0,2,1:T(8,128)(2,1)S(1)}, bf16[512,16,128]{0,2,1:T(8,128)(2,1)}, u32[]{:S(2)}) copy-start(bf16[512,16,128]{0,2,1:T(8,128)(2,1)} %rev.9) | copy-start | bytes 6291460
  124.7 1.6 copy-start.4
  128.1 8.6 %copy-start.7 = (bf16[512,2048]{1,0:T(8,128)(2,1)S(1)}, bf16[512,2048]{1,0:T(8,128)(2,1)}, u32[]{:S(2)}) copy-start(bf16[512,2048]{1,0:T(8,128)(2,1)} %param.15) | copy-start | bytes 6291460
  136.8 5.9 %copy-start.9 = (f32[512,1024]{0,1:T(8,128)S(1)}, f32[512,1024]{0,1:T(8,128)}, u32[]{:S(2)}) copy-start(f32[512,1024]{0,1:T(8,128)} %get-tuple-element.85) | copy-start | bytes 6291460
  136.8 5.9 %copy-start.19 = (f32[1024]{0:T(1024)S(1)}, f32[1024]{0:T(1024)}, u32[]{:S(2)}) copy-start(f32[1024]{0:T(1024)} %param.28) | copy-start | bytes 12292
  142.6 2.2 %copy-start.23 = (bf16[1024,2048]{1,0:T(8,128)(2,1)S(1)}, bf16[1024,2048]{1,0:T(8,128)(2,1)}, u32[]{:S(2)}) copy-start(bf16[1024,2048]{1,0:T(8,128)(2,1)} %param.29) | copy-start | bytes 12582916
  147.3 46.1 %copy-start.1 = (bf16[2048,512]{1,0:T(8,128)(2,1)S(1)}, bf16[2048,512]{1,0:T(8,128)(2,1)}, u32[]{:S(2)}) copy-start(bf16[2048,512]{1,0:T(8,128)(2,1)} %param.19) | copy-start | bytes 6291460
Sparse Core Ops, SparseCore 0:
  149.0 44.3 reduce-scatter.1

commit v5 on v4

--- a/solution.py
+++ b/solution.py
@@ -146,15 +146,16 @@
     )(state_c, state_c, values_t, acc_g, acc_t, delta_t)
 
 
-def block_finish(intra_t, state_c, values_t, acc_t, start, skip_col, interpret=False):
+def block_finish(intra_t, state_c, values_t, acc_t, start, skip_col, gate_t, gain_col, interpret=False):
     rows = values_t.shape[1]
     groups, per_group, _ = acc_t.shape
     blocks = rows // Q
     width_g = per_group * P_SIZE
 
-    def kernel(y_ref, c_ref, xt_ref, at_ref, s_ref, k_ref, o_ref):
+    def kernel(y_ref, c_ref, xt_ref, at_ref, s_ref, k_ref, g_ref, n_ref, o_ref):
         c_blk = c_ref[...]
         dims = (((1,), (1,)), ((), ()))
+        total = jnp.zeros((1, Q), F32)
         for j in range(per_group):
             lo_row, hi_row = j * P_SIZE, (j + 1) * P_SIZE
             s_j = s_ref[0, j]
@@ -164,11 +165,19 @@
                 s_lo, c_blk, dims, preferred_element_type=F32
             )
             inter = inter * jnp.exp(at_ref[0, j : j + 1, :])
-            o_ref[lo_row:hi_row, :] = (
+            out = (
                 y_ref[lo_row:hi_row, :]
                 + inter
                 + k_ref[lo_row:hi_row, :] * xt_ref[lo_row:hi_row, :].astype(F32)
             )
+            gate = g_ref[lo_row:hi_row, :].astype(F32)
+            gated = out * (gate / (1.0 + jnp.exp(-gate)))
+            total = total + jnp.sum(gated * gated, axis=0, keepdims=True)
+            o_ref[lo_row:hi_row, :] = gated
+        scale = lax.rsqrt(total / width_g + EPSILON)
+        for j in range(per_group):
+            lo_row, hi_row = j * P_SIZE, (j + 1) * P_SIZE
+            o_ref[lo_row:hi_row, :] = o_ref[lo_row:hi_row, :] * scale * n_ref[lo_row:hi_row, :]
 
     return pl.pallas_call(
         kernel,
@@ -179,12 +188,14 @@
             pl.BlockSpec((width_g, Q), lambda b, g: (g, b)),
             pl.BlockSpec((1, per_group, Q), lambda b, g: (g, 0, b)),
             pl.BlockSpec((1, per_group, P_SIZE, N), lambda b, g: (b, g, 0, 0)),
+            pl.BlockSpec((width_g, 1), lambda b, g: (g, 0)),
+            pl.BlockSpec((width_g, Q), lambda b, g: (g, b)),
             pl.BlockSpec((width_g, 1), lambda b, g: (g, 0)),
         ],
         out_specs=pl.BlockSpec((width_g, Q), lambda b, g: (g, b)),
         out_shape=jax.ShapeDtypeStruct((groups * width_g, rows), F32),
         interpret=interpret,
-    )(intra_t, state_c, values_t, acc_t, start, skip_col)
+    )(intra_t, state_c, values_t, acc_t, start, skip_col, gate_t, gain_col)
 
 
 def conv_silu(padded, kernel, offset, count, forward):
@@ -299,11 +310,10 @@
             [local_start[index] + entering[index][:, None, None] * carried for index in range(blocks)]
         )
         skip_col = jnp.repeat(skip_gain, P_SIZE)[:, None]
-        outputs = block_finish(intra_t, state_c, values_t, acc_t, start, skip_col).T
-        gated = outputs.reshape(rows, heads * P_SIZE) * jax.nn.silu(gate_in.astype(F32))
-        grouped = gated.reshape(rows, groups, per_group * P_SIZE)
-        scale = lax.rsqrt(jnp.mean(grouped * grouped, axis=-1, keepdims=True) + EPSILON)
-        return ((grouped * scale).reshape(rows, heads * P_SIZE) * norm_gain[None, :]).astype(BF16)
+        normed = block_finish(
+            intra_t, state_c, values_t, acc_t, start, skip_col, gate_in.T, norm_gain[:, None]
+        )
+        return normed.T.astype(BF16)
 
     forward_out = local_scan(project(hidden), True)
     backward_out = local_scan(project(hidden_rev), False)

time: 202 us -> 207 us (1.025)
  waiting for transfers between devices: 48.3 us -> 44.4 us
  matrix products: 37.9 us -> 40.8 us
  starting transfers between devices: 17.3 us -> 19.6 us
  other arithmetic: 19.2 us -> 21.4 us
    ppermute x6, waiting for transfers between devices: 3.74 us -> 0.02 us  [shifted(): return lax.ppermute(value, axis, pairs)]
    dot_general x1, matrix products: 2.5 us -> 5.36 us  [on_device(): partial = jnp.dot(combined, w_out, preferred_element_type=F32).astype(BF16)]
    unnamed x58 -> x56, local copies, waits for them, and re-layouts: 4.1 us -> 1.53 us
    ppermute x6, starting transfers between devices: 17.3 us -> 19.6 us  [shifted(): return lax.ppermute(value, axis, pairs)]
  transfers between devices with their start and end apart: 7 -> 7, of which waited for: 2 -> 1; matrix products, arithmetic and copies ran while one was open for 20% -> 24% of each run, Pallas kernels for 15% -> 11%
where the time goes in v5:
time: 207 us; the launch traced here: 206 us
  Pallas kernels  47.2 us (23%)
  waiting for transfers between devices  44.4 us (21%)
  matrix products  40.8 us (20%)
  other arithmetic  21.4 us (10%)
  starting transfers between devices  19.6 us (9%)
  local copies, waits for them, and re-layouts  18.2 us (9%)
  between operations  14 us (7%)
    reduce_scatter x1, waiting for transfers between devices, on_device(): summed = lax.psum_scatter(partial, 'chan', scatter_dimension=0, tiled=True)  44.3 us
    ppermute x6, starting transfers between devices, shifted(): return lax.ppermute(value, axis, pairs)  19.6 us
    pallas_call x2, Pallas kernels, block_finish(): pl.pallas_call(kernel, grid=(blocks, groups), in_specs=[pl.BlockSpec((wid...  18.8 us
    pallas_call x2, Pallas kernels, block_intra(): pl.pallas_call(kernel, grid=(blocks, groups), in_specs=[pl.BlockSpec((Q,...  15.2 us
    pallas_call x2, Pallas kernels, block_states(): pl.pallas_call(kernel, grid=(blocks, groups), in_specs=[pl.BlockSpec((Q,...  13.3 us
    dot_general x2, matrix products, project(): gate_in = jnp.dot(source, w_gate, preferred_element_type=F32).astype(BF16)  11.7 us
    dot_general x2, matrix products, project(): jnp.dot(source, w_values, preferred_element_type=F32) * known[:, None]  9.09 us
    transpose x1, other arithmetic, local_scan(): values_t = values_c.T  5.4 us
  transfers between devices with their start and end apart: 7, of which 1 were waited for; matrix products, arithmetic and copies ran while one was open for 24% of the time, Pallas kernels for 11%

profile of v5, /device:TPU:0, one launch (start us, length us, event | category | flops | bytes accessed | tf_op | source)
XLA Modules:
  0.0 205.6 jit_solution(11471232255353449463)
XLA Ops:
  6.5 0.8 compare_select_fusion.2
  7.5 0.8 fusion.63
  8.3 1.3 collective-permute-start.1
  9.7 3.2 %collective-permute-start = (bf16[3,2176]{1,0:T(4,128)(2,1)S(1)}, bf16[3,2176]{1,0:T(4,128)(2,1)S(1)}, u32[]{:S(2)}, u32[]{:S(2)}) collective-permute-start(bf16[3,2176]{1,0:T(4,128)(2,1)S(1)} %pad_maximum_fusion.13), channel_id=1, source_target_pairs={{0,4},{4,8},{8,12},{1,5},{5,9},{9,13},{2,6},{6,10},{10,14},{3,7},{... | collective-permute-start | bytes 39176 | tf_op jit(solution)/shard_map/ppermute | solution.py:25
  12.9 3.6 %convert_bitcast_fusion = bf16[512,16,128]{0,2,1:T(8,128)(2,1)} fusion(bf16[512,2048]{1,0:T(8,128)(2,1)} %param.15), kind=kOutput, calls=%fused_computation.10 | convolution fusion | flops 269516800 | bytes 4194304 | tf_op jit(solution)/shard_map/rki,ij->rkj/dot_general | solution.py:239
  16.5 1.2 convolution_convert_fusion.4
  17.8 3.1 %rev.9 = bf16[512,16,128]{0,2,1:T(8,128)(2,1)} reverse(bf16[512,16,128]{0,2,1:T(8,128)(2,1)} %convert_bitcast_fusion), dimensions={1} | reverse | bytes 4194304 | tf_op jit(solution)/shard_map/jit(_flip)/rev | solution.py:242
  20.9 3.0 %convolution_convert_fusion.3 = bf16[512,512]{1,0:T(8,128)(2,1)S(1)} fusion(bf16[512,2048]{0,1:T(8,128)(2,1)} %bitcast.214, bf16[2048,512]{1,0:T(8,128)(2,1)S(1)} %copy-done), kind=kOutput, calls=%fused_computation.20 | convolution fusion | flops 1074003968 | bytes 4718592 | tf_op jit(solution)/shard_map/dot_general | solution.py:262
  23.9 5.7 %multiply_convert_fusion.3 = bf16[512,1024]{0,1:T(8,128)(2,1)} fusion(bf16[512,2048]{1,0:T(8,128)(2,1)S(1)} %copy-done.6, bf16[2048,1024]{1,0:T(8,128)(2,1)} %param.18, f32[512]{0:T(512)S(1)} %get-tuple-element.61), kind=kOutput, calls=%fused_computation.12 | convolution fusion | flops 2148532224 | bytes 7342080 | tf_op jit(solution)/shard_map/dot_general | solution.py:261
  29.7 3.4 %multiply_convert_fusion.1 = bf16[512,1024]{0,1:T(8,128)(2,1)} fusion(bf16[512,2048]{0,1:T(8,128)(2,1)S(1)} %bitcast.216, bf16[2048,1024]{1,0:T(8,128)(2,1)S(1)} %copy-done.8, f32[512]{0:T(512)S(1)} %get-tuple-element.61), kind=kOutput, calls=%fused_computation.9 | convolution fusion | flops 2148532224 | bytes 7342080 | tf_op jit(solution)/shard_map/dot_general | solution.py:261
  33.5 1.3 broadcast_multiply_fusion.1
  35.7 6.2 %fusion.5.g_ref = bf16[1024,512]{1,0:T(8,128)(2,1)} fusion(bf16[512,2048]{0,1:T(8,128)(2,1)} %bitcast.215, bf16[2048,1024]{1,0:T(8,128)(2,1)} %param.17), kind=kOutput, calls=%fused_computation.19 | convolution fusion | flops 2148007936 | bytes 7340032 | tf_op jit(solution)/shard_map/dot_general | solution.py:260
  42.4 0.6 reshape_reshape.7
  44.6 4.2 %fusion.6 = bf16[6,1024]{0,1:T(8,128)(2,1)S(1)} fusion(bf16[2048,1024]{1,0:T(8,128)(2,1)} %param.18, f32[6]{0:T(128)S(1)} %maximum_convert_fusion, bf16[3,2048]{1,0:T(4,128)(2,1)S(1)} %bitcast.245, bf16[3,2048]{1,0:T(4,128)(2,1)S(1)} %slice.267), kind=kOutput, calls=%fused_computation.27 | convolution fusion | flops 25227264 | bytes 4231192 | tf_op jit(solution)/shard_map/dot_general | solution.py:255
  48.9 2.4 %multiply_convert_fusion.5 = (bf16[512,512]{1,0:T(8,128)(2,1)}, bf16[512,512]{1,0:T(8,128)(2,1)}) fusion(bf16[512,512]{1,0:T(8,128)(2,1)S(1)} %convolution_convert_fusion.4, bf16[3,512]{1,0:T(4,128)(2,1)S(1)} %get-tuple-element.55, f32[512]{0:T(512)S(1)} %bitcast.253, f32[512]{0:T(512)S(1)} %bitcast.254, f32[512]{0:T(512)S(1)} %bitcast.252, ...), kind=kLoop, calls=%fused_computation.47 | loop fusion | flops 13631488 | bytes 2113536 | tf_op jit(solution)/shard_map/convert_element_type | solution.py:207
  51.3 5.4 %fusion.17 = (bf16[1024,512]{1,0:T(8,128)(2,1)}, bf16[1024,512]{1,0:T(8,128)(2,1)}) fusion(bf16[512,1024]{0,1:T(8,128)(2,1)S(1)} %copy-done.10, f32[1024]{0:T(1024)S(1)} %bitcast.249, bf16[3,1024]{0,1:T(8,128)(2,1)S(1)} %get-tuple-element.45, f32[1024]{0:T(1024)S(1)} %bitcast.250, f32[1024]{0:T(1024)S(1)} %bitcast.248, f32[1024]{0:T(1024)S(1)} %bitcast.247, ...), kind=kLoop, calls=%fused_computation.48 | loop fusion | flops 27262976 | bytes 4227072 | tf_op jit(solution)/shard_map/transpose | solution.py:292
  56.7 6.6 %shard_map.149 = f32[4,16,64,128]{3,2,1,0:T(8,128)} custom-call(bf16[512,512]{1,0:T(8,128)(2,1)} %get-tuple-element.54.c_ref.b_ref, bf16[1024,512]{1,0:T(8,128)(2,1)} %get-tuple-element.48.xt_ref, f32[2,8,512]{2,1,0:T(8,128)} %bitcast.236, f32[2,8,512]{2,1,0:T(8,128)} %bitcast.240), custom_call_target="tpu_custom_call" | custom-call | tf_op jit(solution)/shard_map/pallas_call | solution.py:93
  63.4 1.8 fusion.62
  65.1 1.3 fusion.60
  66.5 0.7 pad_maximum_fusion.8
  67.3 1.3 collective-permute-start.4
  68.6 6.7 %shard_map.146 = f32[4,16,64,128]{3,2,1,0:T(8,128)} custom-call(bf16[512,512]{1,0:T(8,128)(2,1)} %get-tuple-element.53.c_ref.b_ref, bf16[1024,512]{1,0:T(8,128)(2,1)} %get-tuple-element.47.xt_ref, f32[2,8,512]{2,1,0:T(8,128)} %bitcast.232, f32[2,8,512]{2,1,0:T(8,128)} %bitcast.242), custom_call_target="tpu_custom_call" | custom-call | tf_op jit(solution)/shard_map/pallas_call | solution.py:93
  75.2 1.8 fusion.61
  77.0 1.3 fusion.59
  78.4 0.7 pad_maximum_fusion.6
  79.1 5.8 %collective-permute-start.2 = (bf16[16,8448]{1,0:T(8,128)(2,1)}, bf16[16,8448]{1,0:T(8,128)(2,1)}, u32[]{:S(2)}, u32[]{:S(2)}) collective-permute-start(bf16[16,8448]{1,0:T(8,128)(2,1)} %pad_maximum_fusion.6), channel_id=1, source_target_pairs={{0,4},{4,8},{8,12},{1,5},{5,9},{9,13},{2,6},{6,10},{10,14},{3,7},{... | collective-permute-start | bytes 811016 | tf_op jit(solution)/shard_map/ppermute | solution.py:25
  85.4 0.7 pad_maximum_fusion.9
  86.2 1.3 collective-permute-start.5
  87.5 0.7 fusion.64
  88.4 1.1 fusion.20
  89.7 6.8 %collective-permute-start.3 = (bf16[16,8448]{1,0:T(8,128)(2,1)S(1)}, bf16[16,8448]{1,0:T(8,128)(2,1)S(1)}, u32[]{:S(2)}, u32[]{:S(2)}) collective-permute-start(bf16[16,8448]{1,0:T(8,128)(2,1)S(1)} %pad_maximum_fusion.7), channel_id=1, source_target_pairs={{0,8},{4,12},{1,9},{5,13},{2,10},{6,14},{3,11},{7,15},{16,24},{20,... | collective-permute-start | bytes 811016 | tf_op jit(solution)/shard_map/ppermute | solution.py:25
  96.5 5.5 %convolution_convert_fusion.2.g_ref = bf16[1024,512]{1,0:T(8,128)(2,1)} fusion(bf16[2048,1024]{1,0:T(8,128)(2,1)} %param.17, bf16[512,2048]{1,0:T(8,128)(2,1)S(1)} %copy-done.7), kind=kOutput, calls=%fused_computation.18 | convolution fusion | flops 2148007936 | bytes 7340032 | tf_op jit(solution)/shard_map/dot_general | solution.py:260
  102.1 1.0 copy.121.a_ref
  103.1 1.3 broadcast_in_dim_reshape.5.k_ref
  104.4 1.0 copy.116.n_ref
  105.5 1.1 copy.112.a_ref
  106.5 7.6 %shard_map.148.y_ref = f32[1024,512]{1,0:T(8,128)} custom-call(bf16[512,512]{1,0:T(8,128)(2,1)} %get-tuple-element.54.c_ref.b_ref, bf16[512,512]{1,0:T(8,128)(2,1)} %get-tuple-element.54.c_ref.b_ref, bf16[1024,512]{1,0:T(8,128)(2,1)} %get-tuple-element.48.xt_ref, f32[2,512,8]{2,1,0:T(8,128)} %copy.121.a_ref, f32[2,8,512]{2,1,0:T(8,128)} %bitcast.237, ...), custom_call_target="tpu_custom_call" | custom-call | tf_op jit(solution)/shard_map/pallas_call | solution.py:132
  114.1 7.6 %shard_map.145.y_ref = f32[1024,512]{1,0:T(8,128)} custom-call(bf16[512,512]{1,0:T(8,128)(2,1)} %get-tuple-element.53.c_ref.b_ref, bf16[512,512]{1,0:T(8,128)(2,1)} %get-tuple-element.53.c_ref.b_ref, bf16[1024,512]{1,0:T(8,128)(2,1)} %get-tuple-element.47.xt_ref, f32[2,512,8]{2,1,0:T(8,128)} %copy.112.a_ref, f32[2,8,512]{2,1,0:T(8,128)} %bitcast.233, ...), custom_call_target="tpu_custom_call" | custom-call | tf_op jit(solution)/shard_map/pallas_call | solution.py:132
  121.7 1.2 fusion.24
  123.0 1.1 fusion.21
  124.6 1.5 pad_maximum_fusion.1.s_ref
  126.1 0.8 copy-done.4
  127.2 1.5 pad_maximum_fusion.s_ref
  128.7 9.3 %shard_map.150 = f32[1024,512]{1,0:T(8,128)} custom-call(f32[1024,512]{1,0:T(8,128)} %shard_map.148.y_ref, bf16[512,512]{1,0:T(8,128)(2,1)} %get-tuple-element.54.c_ref.b_ref, bf16[1024,512]{1,0:T(8,128)(2,1)} %get-tuple-element.48.xt_ref, f32[2,8,512]{2,1,0:T(8,128)} %bitcast.238, f32[4,16,64,128]{3,2,1,0:T(8,128)} %pad_maximum_fusion.1.s_ref, ...), custom_call_target="tpu_custom_call" | custom-call | tf_op jit(solution)/shard_map/pallas_call | solution.py:182
  138.0 9.5 %shard_map.147 = f32[1024,512]{1,0:T(8,128)} custom-call(f32[1024,512]{1,0:T(8,128)} %shard_map.145.y_ref, bf16[512,512]{1,0:T(8,128)(2,1)} %get-tuple-element.53.c_ref.b_ref, bf16[1024,512]{1,0:T(8,128)(2,1)} %get-tuple-element.47.xt_ref, f32[2,8,512]{2,1,0:T(8,128)} %bitcast.234, f32[4,16,64,128]{3,2,1,0:T(8,128)} %pad_maximum_fusion.s_ref, ...), custom_call_target="tpu_custom_call" | custom-call | tf_op jit(solution)/shard_map/pallas_call | solution.py:182
  147.5 5.4 %convolution_convert_fusion = bf16[512,2048]{1,0:T(8,128)(2,1)S(1)} fusion(bf16[1024,2048]{1,0:T(8,128)(2,1)} %param.29, f32[1024,512]{1,0:T(8,128)S(1)} %copy-done.9, f32[1024,512]{1,0:T(8,128)} %shard_map.147), kind=kOutput, calls=%fused_computation | convolution fusion | flops 2151677952 | bytes 10485760 | tf_op jit(solution)/shard_map/dot_general | solution.py:322
  152.9 1.6 copy.190
  154.4 44.3 %reduce-scatter.2.cloned.1.call-done = bf16[1,512,512]{2,1,0:T(8,128)(2,1)} async-done(((bf16[4,512,512]{2,1,0:T(8,128)(2,1)}), bf16[1,512,512]{2,1,0:T(8,128)(2,1)}) %reduce-scatter.2.cloned.1.call-update) | async-done | bytes 524304 | tf_op jit(solution)/shard_map/reduce_scatter | solution.py:324
  (112 shorter events, 5.7 us)
Async XLA Ops:
  6.5 10.0 %copy-start = (bf16[2048,512]{1,0:T(8,128)(2,1)S(1)}, bf16[2048,512]{1,0:T(8,128)(2,1)}, u32[]{:S(2)}) copy-start(bf16[2048,512]{1,0:T(8,128)(2,1)} %param.19) | copy-start | bytes 6291460
  6.5 192.2 %reduce-scatter.2.cloned.1.call-start = ((), (), s32[]{:S(2)}) async-start(), calls=%async_computation.1 | async-start | bytes 2621440 | tf_op jit(solution)/shard_map/reduce_scatter | solution.py:324
  8.3 35.3 %collective-permute-start.1 = (bf16[3,2176]{1,0:T(4,128)(2,1)S(1)}, bf16[3,2176]{1,0:T(4,128)(2,1)S(1)}, u32[]{:S(2)}, u32[]{:S(2)}) collective-permute-start(bf16[3,2176]{1,0:T(4,128)(2,1)S(1)} %pad_maximum_fusion.14), channel_id=1, source_target_pairs={{4,0},{8,4},{12,8},{5,1},{9,5},{13,9},{6,2},{10,6},{14,10},{7,3},{... | collective-permute-start | bytes 39176 | tf_op jit(solution)/shard_map/ppermute | solution.py:25
  9.7 6.8 %copy-start.5 = (bf16[512,2048]{1,0:T(8,128)(2,1)S(1)}, bf16[512,2048]{1,0:T(8,128)(2,1)}, u32[]{:S(2)}) copy-start(bf16[512,2048]{1,0:T(8,128)(2,1)} %param.15) | copy-start | bytes 6291460
  9.7 34.1 %collective-permute-start = (bf16[3,2176]{1,0:T(4,128)(2,1)S(1)}, bf16[3,2176]{1,0:T(4,128)(2,1)S(1)}, u32[]{:S(2)}, u32[]{:S(2)}) collective-permute-start(bf16[3,2176]{1,0:T(4,128)(2,1)S(1)} %pad_maximum_fusion.13), channel_id=1, source_target_pairs={{0,4},{4,8},{8,12},{1,5},{5,9},{9,13},{2,6},{6,10},{10,14},{3,7},{... | collective-permute-start | bytes 39176 | tf_op jit(solution)/shard_map/ppermute | solution.py:25
  20.9 3.0 %copy-start.6 = (bf16[512,2048]{1,0:T(8,128)(2,1)S(1)}, bf16[512,2048]{1,0:T(8,128)(2,1)}, u32[]{:S(2)}) copy-start(bf16[512,2048]{1,0:T(8,128)(2,1)} %param.15) | copy-start | bytes 6291460
  23.9 5.7 %copy-start.2 = (bf16[512,16,128]{0,2,1:T(8,128)(2,1)S(1)}, bf16[512,16,128]{0,2,1:T(8,128)(2,1)}, u32[]{:S(2)}) copy-start(bf16[512,16,128]{0,2,1:T(8,128)(2,1)} %rev.9) | copy-start | bytes 6291460
  23.9 5.7 %copy-start.8 = (bf16[2048,1024]{1,0:T(8,128)(2,1)S(1)}, bf16[2048,1024]{1,0:T(8,128)(2,1)}, u32[]{:S(2)}) copy-start(bf16[2048,1024]{1,0:T(8,128)(2,1)} %param.18) | copy-start | bytes 12582916
  29.7 3.4 %copy-start.23 = (f32[16]{0:T(128)S(1)}, f32[16]{0:T(128)}, u32[]{:S(2)}) copy-start(f32[16]{0:T(128)} %param.26) | copy-start | bytes 196
  29.7 3.4 %copy-start.15 = (bf16[2048,16]{0,1:T(8,128)(2,1)S(1)}, bf16[2048,16]{0,1:T(8,128)(2,1)}, u32[]{:S(2)}) copy-start(bf16[2048,16]{0,1:T(8,128)(2,1)} %param.20) | copy-start | bytes 196612
  29.7 3.4 %copy-start.21 = (f32[16]{0:T(128)S(1)}, f32[16]{0:T(128)}, u32[]{:S(2)}) copy-start(f32[16]{0:T(128)} %param.25) | copy-start | bytes 196
  33.1 2.2 %copy-start.17 = (f32[4,512]{1,0:T(4,128)S(1)}, f32[4,512]{1,0:T(4,128)}, u32[]{:S(2)}) copy-start(f32[4,512]{1,0:T(4,128)} %param.23) | copy-start | bytes 24580
  33.1 2.2 %copy-start.16 = (f32[4,1024]{1,0:T(4,128)S(1)}, f32[4,1024]{1,0:T(4,128)}, u32[]{:S(2)}) copy-start(f32[4,1024]{1,0:T(4,128)} %param.21) | copy-start | bytes 49156
  33.5 8.4 %copy-start.14 = (f32[512,16]{0,1:T(8,128)}, f32[512,16]{0,1:T(8,128)S(1)}, u32[]{:S(2)}) copy-start(f32[512,16]{0,1:T(8,128)S(1)} %compare_select_fusion) | copy-start | bytes 98308
  44.6 4.3 %copy-start.20 = (f32[512]{0:T(512)S(1)}, f32[512]{0:T(512)}, u32[]{:S(2)}) copy-start(f32[512]{0:T(512)} %param.24) | copy-start | bytes 6148
  48.7 2.6 %copy-start.10 = (bf16[512,1024]{0,1:T(8,128)(2,1)S(1)}, bf16[512,1024]{0,1:T(8,128)(2,1)}, u32[]{:S(2)}) copy-start(bf16[512,1024]{0,1:T(8,128)(2,1)} %multiply_convert_fusion.3) | copy-start | bytes 3145732
  48.7 2.6 %copy-start.11 = (bf16[512,1024]{0,1:T(8,128)(2,1)S(1)}, bf16[512,1024]{0,1:T(8,128)(2,1)}, u32[]{:S(2)}) copy-start(bf16[512,1024]{0,1:T(8,128)(2,1)} %multiply_convert_fusion.1) | copy-start | bytes 3145732
  48.7 2.6 %copy-start.19 = (f32[1024]{0:T(1024)S(1)}, f32[1024]{0:T(1024)}, u32[]{:S(2)}) copy-start(f32[1024]{0:T(1024)} %param.22) | copy-start | bytes 12292
  67.3 17.7 %collective-permute-start.4 = (bf16[16,8448]{1,0:T(8,128)(2,1)}, bf16[16,8448]{1,0:T(8,128)(2,1)S(1)}, u32[]{:S(2)}, u32[]{:S(2)}) collective-permute-start(bf16[16,8448]{1,0:T(8,128)(2,1)} %pad_maximum_fusion.8), channel_id=1, source_target_pairs={{4,0},{8,4},{12,8},{5,1},{9,5},{13,9},{6,2},{10,6},{14,10},{7,3},{... | collective-permute-start | bytes 811016 | tf_op jit(solution)/shard_map/ppermute | solution.py:25
  78.2 18.3 %copy-start.7 = (bf16[512,2048]{1,0:T(8,128)(2,1)S(1)}, bf16[512,2048]{1,0:T(8,128)(2,1)}, u32[]{:S(2)}) copy-start(bf16[512,2048]{1,0:T(8,128)(2,1)} %param.15) | copy-start | bytes 6291460
  79.1 8.4 %collective-permute-start.2 = (bf16[16,8448]{1,0:T(8,128)(2,1)}, bf16[16,8448]{1,0:T(8,128)(2,1)}, u32[]{:S(2)}, u32[]{:S(2)}) collective-permute-start(bf16[16,8448]{1,0:T(8,128)(2,1)} %pad_maximum_fusion.6), channel_id=1, source_target_pairs={{0,4},{4,8},{8,12},{1,5},{5,9},{9,13},{2,6},{6,10},{10,14},{3,7},{... | collective-permute-start | bytes 811016 | tf_op jit(solution)/shard_map/ppermute | solution.py:25
  86.2 35.5 %collective-permute-start.5 = (bf16[16,8448]{1,0:T(8,128)(2,1)}, bf16[16,8448]{1,0:T(8,128)(2,1)}, u32[]{:S(2)}, u32[]{:S(2)}) collective-permute-start(bf16[16,8448]{1,0:T(8,128)(2,1)} %pad_maximum_fusion.9), channel_id=1, source_target_pairs={{8,0},{12,4},{9,1},{13,5},{10,2},{14,6},{11,3},{15,7},{24,16},{28,... | collective-permute-start | bytes 811016 | tf_op jit(solution)/shard_map/ppermute | solution.py:25
  89.6 12.4 %copy-start.13 = (f32[512,2,8]{0,2,1:T(8,128)S(1)}, f32[512,2,8]{0,2,1:T(8,128)}, u32[]{:S(2)}) copy-start(f32[512,2,8]{0,2,1:T(8,128)} %reshape_reshape.7) | copy-start | bytes 98308
  89.7 13.4 %copy-start.22 = (f32[16]{0:T(128)S(1)}, f32[16]{0:T(128)}, u32[]{:S(2)}) copy-start(f32[16]{0:T(128)} %param.27) | copy-start | bytes 196
  89.7 14.8 %copy-start.18 = (f32[1024]{0:T(1024)S(1)}, f32[1024]{0:T(1024)}, u32[]{:S(2)}) copy-start(f32[1024]{0:T(1024)} %param.28) | copy-start | bytes 12292
  89.7 15.8 %copy-start.12 = (f32[512,2,8]{0,2,1:T(8,128)S(1)}, f32[512,2,8]{0,2,1:T(8,128)}, u32[]{:S(2)}) copy-start(f32[512,2,8]{0,2,1:T(8,128)} %reshape_reshape.6) | copy-start | bytes 98308
  89.7 33.4 %collective-permute-start.3 = (bf16[16,8448]{1,0:T(8,128)(2,1)S(1)}, bf16[16,8448]{1,0:T(8,128)(2,1)S(1)}, u32[]{:S(2)}, u32[]{:S(2)}) collective-permute-start(bf16[16,8448]{1,0:T(8,128)(2,1)S(1)} %pad_maximum_fusion.7), channel_id=1, source_target_pairs={{0,8},{4,12},{1,9},{5,13},{2,10},{6,14},{3,11},{7,15},{16,24},{20,... | collective-permute-start | bytes 811016 | tf_op jit(solution)/shard_map/ppermute | solution.py:25
  121.7 2.6 %copy-start.3 = (f32[4,16,64,128]{3,2,1,0:T(8,128)S(1)}, f32[4,16,64,128]{3,2,1,0:T(8,128)}, u32[]{:S(2)}) copy-start(f32[4,16,64,128]{3,2,1,0:T(8,128)} %shard_map.149) | copy-start | bytes 6291460
  124.6 2.3 %copy-start.4 = (f32[4,16,64,128]{3,2,1,0:T(8,128)S(1)}, f32[4,16,64,128]{3,2,1,0:T(8,128)}, u32[]{:S(2)}) copy-start(f32[4,16,64,128]{3,2,1,0:T(8,128)} %shard_map.146) | copy-start | bytes 6291460
  138.0 9.5 %copy-start.9 = (f32[1024,512]{1,0:T(8,128)S(1)}, f32[1024,512]{1,0:T(8,128)}, u32[]{:S(2)}) copy-start(f32[1024,512]{1,0:T(8,128)} %shard_map.150) | copy-start | bytes 6291460
  152.8 45.9 %copy-start.1 = (bf16[2048,512]{1,0:T(8,128)(2,1)S(1)}, bf16[2048,512]{1,0:T(8,128)(2,1)}, u32[]{:S(2)}) copy-start(bf16[2048,512]{1,0:T(8,128)(2,1)} %param.19) | copy-start | bytes 6291460
Sparse Core Ops, SparseCore 0:
  154.6 44.1 reduce-scatter.1

commit v6 on v4

--- a/solution.py
+++ b/solution.py
@@ -153,35 +153,37 @@
     width_g = per_group * P_SIZE
 
     def kernel(y_ref, c_ref, xt_ref, at_ref, s_ref, k_ref, o_ref):
-        c_blk = c_ref[...]
         dims = (((1,), (1,)), ((), ()))
-        for j in range(per_group):
-            lo_row, hi_row = j * P_SIZE, (j + 1) * P_SIZE
-            s_j = s_ref[0, j]
-            s_hi = s_j.astype(BF16)
-            s_lo = (s_j - s_hi.astype(F32)).astype(BF16)
-            inter = lax.dot_general(s_hi, c_blk, dims, preferred_element_type=F32) + lax.dot_general(
-                s_lo, c_blk, dims, preferred_element_type=F32
-            )
-            inter = inter * jnp.exp(at_ref[0, j : j + 1, :])
-            o_ref[lo_row:hi_row, :] = (
-                y_ref[lo_row:hi_row, :]
-                + inter
-                + k_ref[lo_row:hi_row, :] * xt_ref[lo_row:hi_row, :].astype(F32)
-            )
+        for b in range(blocks):
+            cols = slice(b * Q, (b + 1) * Q)
+            c_blk = c_ref[cols, :]
+            for j in range(per_group):
+                lo_row, hi_row = j * P_SIZE, (j + 1) * P_SIZE
+                s_j = s_ref[b, j]
+                s_hi = s_j.astype(BF16)
+                s_lo = (s_j - s_hi.astype(F32)).astype(BF16)
+                inter = lax.dot_general(
+                    s_hi, c_blk, dims, preferred_element_type=F32
+                ) + lax.dot_general(s_lo, c_blk, dims, preferred_element_type=F32)
+                inter = inter * jnp.exp(at_ref[0, j : j + 1, cols])
+                o_ref[lo_row:hi_row, cols] = (
+                    y_ref[lo_row:hi_row, cols]
+                    + inter
+                    + k_ref[lo_row:hi_row, :] * xt_ref[lo_row:hi_row, cols].astype(F32)
+                )
 
     return pl.pallas_call(
         kernel,
-        grid=(blocks, groups),
+        grid=(groups,),
         in_specs=[
-            pl.BlockSpec((width_g, Q), lambda b, g: (g, b)),
-            pl.BlockSpec((Q, N), lambda b, g: (b, 2 * g + 1)),
-            pl.BlockSpec((width_g, Q), lambda b, g: (g, b)),
-            pl.BlockSpec((1, per_group, Q), lambda b, g: (g, 0, b)),
-            pl.BlockSpec((1, per_group, P_SIZE, N), lambda b, g: (b, g, 0, 0)),
-            pl.BlockSpec((width_g, 1), lambda b, g: (g, 0)),
+            pl.BlockSpec((width_g, rows), lambda g: (g, 0)),
+            pl.BlockSpec((rows, N), lambda g: (0, 2 * g + 1)),
+            pl.BlockSpec((width_g, rows), lambda g: (g, 0)),
+            pl.BlockSpec((1, per_group, rows), lambda g: (g, 0, 0)),
+            pl.BlockSpec((blocks, per_group, P_SIZE, N), lambda g: (0, g, 0, 0)),
+            pl.BlockSpec((width_g, 1), lambda g: (g, 0)),
         ],
-        out_specs=pl.BlockSpec((width_g, Q), lambda b, g: (g, b)),
+        out_specs=pl.BlockSpec((width_g, rows), lambda g: (g, 0)),
         out_shape=jax.ShapeDtypeStruct((groups * width_g, rows), F32),
         interpret=interpret,
     )(intra_t, state_c, values_t, acc_t, start, skip_col)

time: 202 us -> 196 us (0.970)
  Pallas kernels: 45.8 us -> 40.8 us
    pallas_call x2, Pallas kernels: 17.3 us -> 12.3 us  [block_finish(): pl.pallas_call(kernel, grid=(groups,), in_specs=[pl.BlockSpec((width_g, r...]
  transfers between devices with their start and end apart: 7 -> 7, of which waited for: 2 -> 2; matrix products, arithmetic and copies ran while one was open for 20% -> 21% of each run, Pallas kernels for 15% -> 14%
where the time goes in v6:
time: 196 us; the launch traced here: 195 us
  waiting for transfers between devices  48.3 us (25%)
  Pallas kernels  40.8 us (21%)
  matrix products  37.9 us (19%)
  other arithmetic  19.2 us (10%)
  local copies, waits for them, and re-layouts  17.7 us (9%)
  starting transfers between devices  17.3 us (9%)
  between operations  14 us (7%)
    reduce_scatter x1, waiting for transfers between devices, on_device(): summed = lax.psum_scatter(partial, 'chan', scatter_dimension=0, tiled=True)  44.5 us
    ppermute x6, starting transfers between devices, shifted(): return lax.ppermute(value, axis, pairs)  17.3 us
    pallas_call x2, Pallas kernels, block_intra(): pl.pallas_call(kernel, grid=(blocks, groups), in_specs=[pl.BlockSpec((Q,...  15.2 us
    pallas_call x2, Pallas kernels, block_states(): pl.pallas_call(kernel, grid=(blocks, groups), in_specs=[pl.BlockSpec((Q,...  13.3 us
    dot_general x2, matrix products, project(): gate_in = jnp.dot(source, w_gate, preferred_element_type=F32).astype(BF16)  12.9 us
    pallas_call x2, Pallas kernels, block_finish(): pl.pallas_call(kernel, grid=(groups,), in_specs=[pl.BlockSpec((width_g, r...  12.3 us
    dot_general x2, matrix products, project(): jnp.dot(source, w_values, preferred_element_type=F32) * known[:, None]  9.7 us
    transpose x1, other arithmetic, local_scan(): values_t = values_c.T  5.59 us
  transfers between devices with their start and end apart: 7, of which 2 were waited for; matrix products, arithmetic and copies ran while one was open for 21% of the time, Pallas kernels for 14%

profile of v6, /device:TPU:0, one launch (start us, length us, event | category | flops | bytes accessed | tf_op | source)
XLA Modules:
  0.0 195.2 jit_solution(10032000410734991065)
XLA Ops:
  6.5 0.8 compare_select_fusion.2
  7.5 0.8 fusion.72
  8.3 1.3 collective-permute-start.1
  9.7 3.0 %collective-permute-start = (bf16[3,2176]{1,0:T(4,128)(2,1)S(1)}, bf16[3,2176]{1,0:T(4,128)(2,1)S(1)}, u32[]{:S(2)}, u32[]{:S(2)}) collective-permute-start(bf16[3,2176]{1,0:T(4,128)(2,1)S(1)} %pad_maximum_fusion.13), channel_id=1, source_target_pairs={{0,4},{4,8},{8,12},{1,5},{5,9},{9,13},{2,6},{6,10},{10,14},{3,7},{... | collective-permute-start | bytes 39176 | tf_op jit(solution)/shard_map/ppermute | solution.py:25
  12.8 3.6 %convert_bitcast_fusion = bf16[512,16,128]{0,2,1:T(8,128)(2,1)} fusion(bf16[512,2048]{1,0:T(8,128)(2,1)} %param.15), kind=kOutput, calls=%fused_computation.30 | convolution fusion | flops 269516800 | bytes 4194304 | tf_op jit(solution)/shard_map/rki,ij->rkj/dot_general | solution.py:230
  16.4 3.1 %rev.9 = bf16[512,16,128]{0,2,1:T(8,128)(2,1)} reverse(bf16[512,16,128]{0,2,1:T(8,128)(2,1)} %convert_bitcast_fusion), dimensions={1} | reverse | bytes 4194304 | tf_op jit(solution)/shard_map/jit(_flip)/rev | solution.py:233
  19.5 6.3 %multiply_convert_fusion.3 = bf16[512,1024]{0,1:T(8,128)(2,1)} fusion(bf16[512,2048]{1,0:T(8,128)(2,1)} %param.15, bf16[2048,1024]{1,0:T(8,128)(2,1)} %param.18, f32[512]{0:T(512)S(1)} %get-tuple-element.63), kind=kOutput, calls=%fused_computation.32 | convolution fusion | flops 2148532224 | bytes 7342080 | tf_op jit(solution)/shard_map/dot_general | solution.py:252
  25.8 3.4 %multiply_convert_fusion.1 = bf16[512,1024]{0,1:T(8,128)(2,1)} fusion(bf16[512,2048]{0,1:T(8,128)(2,1)S(1)} %bitcast.231, bf16[2048,1024]{1,0:T(8,128)(2,1)S(1)} %copy-done.8, f32[512]{0:T(512)S(1)} %get-tuple-element.63), kind=kOutput, calls=%fused_computation.29 | convolution fusion | flops 2148532224 | bytes 7342080 | tf_op jit(solution)/shard_map/dot_general | solution.py:252
  29.2 1.3 convolution_convert_fusion.3
  30.8 1.3 convolution_convert_fusion.4
  32.1 0.4 compare_select_fusion
  32.6 1.3 broadcast_multiply_fusion.1
  35.3 1.0 copy.121.a_ref
  36.4 1.3 broadcast_in_dim_reshape.5.k_ref
  37.7 1.0 copy.112.a_ref
  39.3 0.4 convolution_convert_fusion.8
  39.7 4.1 %fusion.17 = bf16[6,1024]{0,1:T(8,128)(2,1)S(1)} fusion(bf16[2048,1024]{1,0:T(8,128)(2,1)} %param.18, f32[6]{0:T(128)S(1)} %maximum_convert_fusion, bf16[3,2048]{1,0:T(4,128)(2,1)S(1)} %bitcast.262, bf16[3,2048]{1,0:T(4,128)(2,1)S(1)} %slice.267), kind=kOutput, calls=%fused_computation.46 | convolution fusion | flops 25227264 | bytes 4231192 | tf_op jit(solution)/shard_map/dot_general | solution.py:246
  44.0 5.6 %fusion.26 = (bf16[1024,512]{1,0:T(8,128)(2,1)}, bf16[1024,512]{1,0:T(8,128)(2,1)}) fusion(bf16[512,1024]{0,1:T(8,128)(2,1)S(1)} %copy-done.10, f32[1024]{0:T(1024)S(1)} %bitcast.266, bf16[3,1024]{0,1:T(8,128)(2,1)S(1)} %get-tuple-element.45, f32[1024]{0:T(1024)S(1)} %bitcast.267, f32[1024]{0:T(1024)S(1)} %bitcast.265, f32[1024]{0:T(1024)S(1)} %bitcast.264, ...), kind=kLoop, calls=%fused_computation.65 | loop fusion | flops 27262976 | bytes 4227072 | tf_op jit(solution)/shard_map/transpose | solution.py:283
  49.6 2.4 %multiply_convert_fusion.5 = (bf16[512,512]{1,0:T(8,128)(2,1)}, bf16[512,512]{1,0:T(8,128)(2,1)}) fusion(bf16[512,512]{1,0:T(8,128)(2,1)S(1)} %convolution_convert_fusion.4, bf16[3,512]{1,0:T(4,128)(2,1)S(1)} %get-tuple-element.55, f32[512]{0:T(512)S(1)} %bitcast.270, f32[512]{0:T(512)S(1)} %bitcast.271, f32[512]{0:T(512)S(1)} %bitcast.269, ...), kind=kLoop, calls=%fused_computation.64 | loop fusion | flops 13631488 | bytes 2113536 | tf_op jit(solution)/shard_map/convert_element_type | solution.py:198
  52.0 6.7 %shard_map.149 = f32[4,16,64,128]{3,2,1,0:T(8,128)} custom-call(bf16[512,512]{1,0:T(8,128)(2,1)} %get-tuple-element.54.c_ref.b_ref, bf16[1024,512]{1,0:T(8,128)(2,1)} %get-tuple-element.48.xt_ref, f32[2,8,512]{2,1,0:T(8,128)} %bitcast.254, f32[2,8,512]{2,1,0:T(8,128)} %bitcast.257), custom_call_target="tpu_custom_call" | custom-call | tf_op jit(solution)/shard_map/pallas_call | solution.py:93
  58.6 1.7 fusion.71
  60.4 1.3 fusion.69
  61.8 0.7 pad_maximum_fusion.8
  62.5 1.3 collective-permute-start.4
  63.8 6.7 %shard_map.146 = f32[4,16,64,128]{3,2,1,0:T(8,128)} custom-call(bf16[512,512]{1,0:T(8,128)(2,1)} %get-tuple-element.53.c_ref.b_ref, bf16[1024,512]{1,0:T(8,128)(2,1)} %get-tuple-element.47.xt_ref, f32[2,8,512]{2,1,0:T(8,128)} %bitcast.250, f32[2,8,512]{2,1,0:T(8,128)} %bitcast.259), custom_call_target="tpu_custom_call" | custom-call | tf_op jit(solution)/shard_map/pallas_call | solution.py:93
  70.5 1.7 fusion.70
  72.2 1.3 fusion.68
  73.6 7.6 %shard_map.148.y_ref = f32[1024,512]{1,0:T(8,128)} custom-call(bf16[512,512]{1,0:T(8,128)(2,1)} %get-tuple-element.54.c_ref.b_ref, bf16[512,512]{1,0:T(8,128)(2,1)} %get-tuple-element.54.c_ref.b_ref, bf16[1024,512]{1,0:T(8,128)(2,1)} %get-tuple-element.48.xt_ref, f32[2,512,8]{2,1,0:T(8,128)} %copy.121.a_ref, f32[2,8,512]{2,1,0:T(8,128)} %bitcast.255, ...), custom_call_target="tpu_custom_call" | custom-call | tf_op jit(solution)/shard_map/pallas_call | solution.py:132
  81.3 5.1 %collective-permute-start.2 = (bf16[16,8448]{1,0:T(8,128)(2,1)S(1)}, bf16[16,8448]{1,0:T(8,128)(2,1)S(1)}, u32[]{:S(2)}, u32[]{:S(2)}) collective-permute-start(bf16[16,8448]{1,0:T(8,128)(2,1)S(1)} %pad_maximum_fusion.6), channel_id=1, source_target_pairs={{0,4},{4,8},{8,12},{1,5},{5,9},{9,13},{2,6},{6,10},{10,14},{3,7},{... | collective-permute-start | bytes 811016 | tf_op jit(solution)/shard_map/ppermute | solution.py:25
  86.4 7.6 %shard_map.145.y_ref = f32[1024,512]{1,0:T(8,128)} custom-call(bf16[512,512]{1,0:T(8,128)(2,1)} %get-tuple-element.53.c_ref.b_ref, bf16[512,512]{1,0:T(8,128)(2,1)} %get-tuple-element.53.c_ref.b_ref, bf16[1024,512]{1,0:T(8,128)(2,1)} %get-tuple-element.47.xt_ref, f32[2,512,8]{2,1,0:T(8,128)} %copy.112.a_ref, f32[2,8,512]{2,1,0:T(8,128)} %bitcast.251, ...), custom_call_target="tpu_custom_call" | custom-call | tf_op jit(solution)/shard_map/pallas_call | solution.py:132
  94.5 0.8 pad_maximum_fusion.9
  95.2 1.3 collective-permute-start.5
  97.0 5.3 %collective-permute-start.3 = (bf16[16,8448]{1,0:T(8,128)(2,1)S(1)}, bf16[16,8448]{1,0:T(8,128)(2,1)S(1)}, u32[]{:S(2)}, u32[]{:S(2)}) collective-permute-start(bf16[16,8448]{1,0:T(8,128)(2,1)S(1)} %pad_maximum_fusion.7), channel_id=1, source_target_pairs={{0,8},{4,12},{1,9},{5,13},{2,10},{6,14},{3,11},{7,15},{16,24},{20,... | collective-permute-start | bytes 811016 | tf_op jit(solution)/shard_map/ppermute | solution.py:25
  102.3 3.7 %collective-permute-done.5 = bf16[16,8448]{1,0:T(8,128)(2,1)} collective-permute-done((bf16[16,8448]{1,0:T(8,128)(2,1)}, bf16[16,8448]{1,0:T(8,128)(2,1)}, u32[]{:S(2)}, u32[]{:S(2)}) %collective-permute-start.5) | collective-permute-done | bytes 270368 | tf_op jit(solution)/shard_map/ppermute | solution.py:25
  106.1 1.1 fusion.33
  107.3 0.3 multiply_add_fusion.2
  107.6 1.4 pad_maximum_fusion.1.s_ref
  109.0 6.1 %shard_map.150 = f32[1024,512]{1,0:T(8,128)} custom-call(f32[1024,512]{1,0:T(8,128)} %shard_map.148.y_ref, bf16[512,512]{1,0:T(8,128)(2,1)} %get-tuple-element.54.c_ref.b_ref, bf16[1024,512]{1,0:T(8,128)(2,1)} %get-tuple-element.48.xt_ref, f32[2,8,512]{2,1,0:T(8,128)} %bitcast.256, f32[4,16,64,128]{3,2,1,0:T(8,128)} %pad_maximum_fusion.1.s_ref, ...), custom_call_target="tpu_custom_call" | custom-call | tf_op jit(solution)/shard_map/pallas_call | solution.py:175
  115.1 7.1 %bitcast_reduce_fusion = (f32[512,2]{0,1:T(2,128)S(1)}, f32[512,1024]{0,1:T(8,128)}) fusion(bf16[512,2048]{0,1:T(8,128)(2,1)S(1)} %bitcast.234, bf16[2048,1024]{1,0:T(8,128)(2,1)} %param.17, f32[1024,512]{1,0:T(8,128)} %shard_map.150), kind=kOutput, calls=%fused_computation.22 | convolution fusion | flops 2152201216 | bytes 10489856 | tf_op jit(solution)/shard_map/dot_general | solution.py:251
  122.5 1.3 copy-done.4
  124.1 1.5 pad_maximum_fusion.s_ref
  125.6 6.1 %shard_map.147 = f32[1024,512]{1,0:T(8,128)} custom-call(f32[1024,512]{1,0:T(8,128)} %shard_map.145.y_ref, bf16[512,512]{1,0:T(8,128)(2,1)} %get-tuple-element.53.c_ref.b_ref, bf16[1024,512]{1,0:T(8,128)(2,1)} %get-tuple-element.47.xt_ref, f32[2,8,512]{2,1,0:T(8,128)} %bitcast.252, f32[4,16,64,128]{3,2,1,0:T(8,128)} %pad_maximum_fusion.s_ref, ...), custom_call_target="tpu_custom_call" | custom-call | tf_op jit(solution)/shard_map/pallas_call | solution.py:175
  131.8 5.8 %bitcast_reduce_fusion.1 = (f32[512,2]{0,1:T(2,128)S(1)}, f32[512,1024]{0,1:T(8,128)S(1)}) fusion(bf16[512,2048]{1,0:T(8,128)(2,1)S(1)} %copy-done.7, bf16[2048,1024]{1,0:T(8,128)(2,1)} %param.17, f32[1024,512]{1,0:T(8,128)} %shard_map.147), kind=kOutput, calls=%fused_computation.26 | convolution fusion | flops 2152201216 | bytes 10489856 | tf_op jit(solution)/shard_map/dot_general | solution.py:251
  137.6 0.4 fusion.14
  138.0 1.8 copy-done.23
  139.8 2.5 %convolution_convert_fusion = bf16[512,2048]{1,0:T(8,128)(2,1)S(1)} fusion(bf16[1024,2048]{1,0:T(8,128)(2,1)S(1)} %copy-done.23, bf16[512,1024]{0,1:T(8,128)(2,1)S(1)} %get-tuple-element.62, bf16[512,1024]{0,1:T(8,128)(2,1)S(1)} %get-tuple-element.61), kind=kOutput, calls=%fused_computation | convolution fusion | flops 2150629376 | bytes 8388608 | tf_op jit(solution)/shard_map/dot_general | solution.py:314
  142.3 1.5 copy.190
  143.9 44.5 %reduce-scatter.2.cloned.1.call-done = bf16[1,512,512]{2,1,0:T(8,128)(2,1)} async-done(((bf16[4,512,512]{2,1,0:T(8,128)(2,1)}), bf16[1,512,512]{2,1,0:T(8,128)(2,1)}) %reduce-scatter.2.cloned.1.call-update) | async-done | bytes 524304 | tf_op jit(solution)/shard_map/reduce_scatter | solution.py:316
  (116 shorter events, 4.7 us)
Async XLA Ops:
  6.5 22.7 %copy-start = (bf16[2048,512]{1,0:T(8,128)(2,1)S(1)}, bf16[2048,512]{1,0:T(8,128)(2,1)}, u32[]{:S(2)}) copy-start(bf16[2048,512]{1,0:T(8,128)(2,1)} %param.19) | copy-start | bytes 6291460
  6.5 181.8 %reduce-scatter.2.cloned.1.call-start = ((), (), s32[]{:S(2)}) async-start(), calls=%async_computation.1 | async-start | bytes 2621440 | tf_op jit(solution)/shard_map/reduce_scatter | solution.py:316
  8.3 30.4 %collective-permute-start.1 = (bf16[3,2176]{1,0:T(4,128)(2,1)S(1)}, bf16[3,2176]{1,0:T(4,128)(2,1)S(1)}, u32[]{:S(2)}, u32[]{:S(2)}) collective-permute-start(bf16[3,2176]{1,0:T(4,128)(2,1)S(1)} %pad_maximum_fusion.14), channel_id=1, source_target_pairs={{4,0},{8,4},{12,8},{5,1},{9,5},{13,9},{6,2},{10,6},{14,10},{7,3},{... | collective-permute-start | bytes 39176 | tf_op jit(solution)/shard_map/ppermute | solution.py:25
  9.7 29.4 %collective-permute-start = (bf16[3,2176]{1,0:T(4,128)(2,1)S(1)}, bf16[3,2176]{1,0:T(4,128)(2,1)S(1)}, u32[]{:S(2)}, u32[]{:S(2)}) collective-permute-start(bf16[3,2176]{1,0:T(4,128)(2,1)S(1)} %pad_maximum_fusion.13), channel_id=1, source_target_pairs={{0,4},{4,8},{8,12},{1,5},{5,9},{9,13},{2,6},{6,10},{10,14},{3,7},{... | collective-permute-start | bytes 39176 | tf_op jit(solution)/shard_map/ppermute | solution.py:25
  19.5 6.3 %copy-start.2 = (bf16[512,16,128]{0,2,1:T(8,128)(2,1)S(1)}, bf16[512,16,128]{0,2,1:T(8,128)(2,1)}, u32[]{:S(2)}) copy-start(bf16[512,16,128]{0,2,1:T(8,128)(2,1)} %rev.9) | copy-start | bytes 6291460
  19.5 6.3 %copy-start.8 = (bf16[2048,1024]{1,0:T(8,128)(2,1)S(1)}, bf16[2048,1024]{1,0:T(8,128)(2,1)}, u32[]{:S(2)}) copy-start(bf16[2048,1024]{1,0:T(8,128)(2,1)} %param.18) | copy-start | bytes 12582916
  29.2 1.6 copy-start.6
  30.8 1.3 copy-start.24
  30.8 1.3 copy-start.15
  30.8 1.3 copy-start.21
  32.1 2.2 %copy-start.16 = (f32[4,1024]{1,0:T(4,128)S(1)}, f32[4,1024]{1,0:T(4,128)}, u32[]{:S(2)}) copy-start(f32[4,1024]{1,0:T(4,128)} %param.21) | copy-start | bytes 49156
  32.1 2.2 %copy-start.17 = (f32[4,512]{1,0:T(4,128)S(1)}, f32[4,512]{1,0:T(4,128)}, u32[]{:S(2)}) copy-start(f32[4,512]{1,0:T(4,128)} %param.23) | copy-start | bytes 24580
  32.5 5.2 %copy-start.14 = (f32[512,16]{0,1:T(8,128)}, f32[512,16]{0,1:T(8,128)S(1)}, u32[]{:S(2)}) copy-start(f32[512,16]{0,1:T(8,128)S(1)} %compare_select_fusion) | copy-start | bytes 98308
  32.6 3.7 %copy-start.22 = (f32[16]{0:T(128)S(1)}, f32[16]{0:T(128)}, u32[]{:S(2)}) copy-start(f32[16]{0:T(128)} %param.27) | copy-start | bytes 196
  35.3 8.5 %copy-start.13 = (f32[512,2,8]{0,2,1:T(8,128)}, f32[512,2,8]{0,2,1:T(8,128)S(1)}, u32[]{:S(2)}) copy-start(f32[512,2,8]{0,2,1:T(8,128)S(1)} %reshape_reshape.7) | copy-start | bytes 98308
  37.7 6.1 %copy-start.12 = (f32[512,2,8]{0,2,1:T(8,128)}, f32[512,2,8]{0,2,1:T(8,128)S(1)}, u32[]{:S(2)}) copy-start(f32[512,2,8]{0,2,1:T(8,128)S(1)} %reshape_reshape.6) | copy-start | bytes 98308
  39.7 4.3 %copy-start.10 = (bf16[512,1024]{0,1:T(8,128)(2,1)S(1)}, bf16[512,1024]{0,1:T(8,128)(2,1)}, u32[]{:S(2)}) copy-start(bf16[512,1024]{0,1:T(8,128)(2,1)} %multiply_convert_fusion.3) | copy-start | bytes 3145732
  39.7 4.3 %copy-start.11 = (bf16[512,1024]{0,1:T(8,128)(2,1)S(1)}, bf16[512,1024]{0,1:T(8,128)(2,1)}, u32[]{:S(2)}) copy-start(bf16[512,1024]{0,1:T(8,128)(2,1)} %multiply_convert_fusion.1) | copy-start | bytes 3145732
  39.7 4.3 %copy-start.18 = (f32[1024]{0:T(1024)S(1)}, f32[1024]{0:T(1024)}, u32[]{:S(2)}) copy-start(f32[1024]{0:T(1024)} %param.22) | copy-start | bytes 12292
  44.0 5.6 %copy-start.20 = (f32[512]{0:T(512)S(1)}, f32[512]{0:T(512)}, u32[]{:S(2)}) copy-start(f32[512]{0:T(512)} %param.24) | copy-start | bytes 6148
  62.5 31.4 %collective-permute-start.4 = (bf16[16,8448]{1,0:T(8,128)(2,1)}, bf16[16,8448]{1,0:T(8,128)(2,1)S(1)}, u32[]{:S(2)}, u32[]{:S(2)}) collective-permute-start(bf16[16,8448]{1,0:T(8,128)(2,1)} %pad_maximum_fusion.8), channel_id=1, source_target_pairs={{4,0},{8,4},{12,8},{5,1},{9,5},{13,9},{6,2},{10,6},{14,10},{7,3},{... | collective-permute-start | bytes 811016 | tf_op jit(solution)/shard_map/ppermute | solution.py:25
  81.3 15.2 %collective-permute-start.2 = (bf16[16,8448]{1,0:T(8,128)(2,1)S(1)}, bf16[16,8448]{1,0:T(8,128)(2,1)S(1)}, u32[]{:S(2)}, u32[]{:S(2)}) collective-permute-start(bf16[16,8448]{1,0:T(8,128)(2,1)S(1)} %pad_maximum_fusion.6), channel_id=1, source_target_pairs={{0,4},{4,8},{8,12},{1,5},{5,9},{9,13},{2,6},{6,10},{10,14},{3,7},{... | collective-permute-start | bytes 811016 | tf_op jit(solution)/shard_map/ppermute | solution.py:25
  94.5 12.8 %copy-start.5 = (f32[4,16,64,128]{3,2,1,0:T(8,128)S(1)}, f32[4,16,64,128]{3,2,1,0:T(8,128)}, u32[]{:S(2)}) copy-start(f32[4,16,64,128]{3,2,1,0:T(8,128)} %shard_map.149) | copy-start | bytes 6291460
  95.2 10.8 %collective-permute-start.5 = (bf16[16,8448]{1,0:T(8,128)(2,1)}, bf16[16,8448]{1,0:T(8,128)(2,1)}, u32[]{:S(2)}, u32[]{:S(2)}) collective-permute-start(bf16[16,8448]{1,0:T(8,128)(2,1)} %pad_maximum_fusion.9), channel_id=1, source_target_pairs={{8,0},{12,4},{9,1},{13,5},{10,2},{14,6},{11,3},{15,7},{24,16},{28,... | collective-permute-start | bytes 811016 | tf_op jit(solution)/shard_map/ppermute | solution.py:25
  97.0 25.2 %collective-permute-start.3 = (bf16[16,8448]{1,0:T(8,128)(2,1)S(1)}, bf16[16,8448]{1,0:T(8,128)(2,1)S(1)}, u32[]{:S(2)}, u32[]{:S(2)}) collective-permute-start(bf16[16,8448]{1,0:T(8,128)(2,1)S(1)} %pad_maximum_fusion.7), channel_id=1, source_target_pairs={{0,8},{4,12},{1,9},{5,13},{2,10},{6,14},{3,11},{7,15},{16,24},{20,... | collective-permute-start | bytes 811016 | tf_op jit(solution)/shard_map/ppermute | solution.py:25
  109.0 6.1 %copy-start.3 = (bf16[512,16,128]{0,2,1:T(8,128)(2,1)S(1)}, bf16[512,16,128]{0,2,1:T(8,128)(2,1)}, u32[]{:S(2)}) copy-start(bf16[512,16,128]{0,2,1:T(8,128)(2,1)} %rev.9) | copy-start | bytes 6291460
  122.2 1.6 copy-start.4
  125.6 6.2 %copy-start.7 = (bf16[512,2048]{1,0:T(8,128)(2,1)S(1)}, bf16[512,2048]{1,0:T(8,128)(2,1)}, u32[]{:S(2)}) copy-start(bf16[512,2048]{1,0:T(8,128)(2,1)} %param.15) | copy-start | bytes 6291460
  131.7 5.9 %copy-start.9 = (f32[512,1024]{0,1:T(8,128)S(1)}, f32[512,1024]{0,1:T(8,128)}, u32[]{:S(2)}) copy-start(f32[512,1024]{0,1:T(8,128)} %get-tuple-element.85) | copy-start | bytes 6291460
  131.7 5.9 %copy-start.19 = (f32[1024]{0:T(1024)S(1)}, f32[1024]{0:T(1024)}, u32[]{:S(2)}) copy-start(f32[1024]{0:T(1024)} %param.28) | copy-start | bytes 12292
  137.6 2.2 %copy-start.23 = (bf16[1024,2048]{1,0:T(8,128)(2,1)S(1)}, bf16[1024,2048]{1,0:T(8,128)(2,1)}, u32[]{:S(2)}) copy-start(bf16[1024,2048]{1,0:T(8,128)(2,1)} %param.29) | copy-start | bytes 12582916
  142.3 46.1 %copy-start.1 = (bf16[2048,512]{1,0:T(8,128)(2,1)S(1)}, bf16[2048,512]{1,0:T(8,128)(2,1)}, u32[]{:S(2)}) copy-start(bf16[2048,512]{1,0:T(8,128)(2,1)} %param.19) | copy-start | bytes 6291460
Sparse Core Ops, SparseCore 0:
  144.0 44.3 reduce-scatter.1

commit v7 on v6

--- a/solution.py
+++ b/solution.py
@@ -77,29 +77,31 @@
     width_g = per_group * P_SIZE
 
     def kernel(b_ref, xt_ref, at_ref, dt_ref, s_ref):
-        b_blk = b_ref[...]
+      for blk in range(blocks):
+        cols = slice(blk * Q, (blk + 1) * Q)
+        b_blk = b_ref[cols, :]
         for j in range(per_group):
-            a_row = at_ref[0, j : j + 1, :]
-            d_row = dt_ref[0, j : j + 1, :]
+            a_row = at_ref[0, j : j + 1, cols]
+            d_row = dt_ref[0, j : j + 1, cols]
             a_end = a_row[:, Q - 1 : Q] if forward else a_row[:, 0:1]
-            xt_j = xt_ref[j * P_SIZE : (j + 1) * P_SIZE, :]
+            xt_j = xt_ref[j * P_SIZE : (j + 1) * P_SIZE, cols]
             tx = (jnp.exp(a_end - a_row) * d_row) * xt_j.astype(F32)
             t_hi = tx.astype(BF16)
             t_lo = (tx - t_hi.astype(F32)).astype(BF16)
-            s_ref[0, j] = jnp.dot(t_hi, b_blk, preferred_element_type=F32) + jnp.dot(
+            s_ref[blk, j] = jnp.dot(t_hi, b_blk, preferred_element_type=F32) + jnp.dot(
                 t_lo, b_blk, preferred_element_type=F32
             )
 
     return pl.pallas_call(
         kernel,
-        grid=(blocks, groups),
+        grid=(groups,),
         in_specs=[
-            pl.BlockSpec((Q, N), lambda b, g: (b, 2 * g)),
-            pl.BlockSpec((width_g, Q), lambda b, g: (g, b)),
-            pl.BlockSpec((1, per_group, Q), lambda b, g: (g, 0, b)),
-            pl.BlockSpec((1, per_group, Q), lambda b, g: (g, 0, b)),
+            pl.BlockSpec((rows, N), lambda g: (0, 2 * g)),
+            pl.BlockSpec((width_g, rows), lambda g: (g, 0)),
+            pl.BlockSpec((1, per_group, rows), lambda g: (g, 0, 0)),
+            pl.BlockSpec((1, per_group, rows), lambda g: (g, 0, 0)),
         ],
-        out_specs=pl.BlockSpec((1, per_group, P_SIZE, N), lambda b, g: (b, g, 0, 0)),
+        out_specs=pl.BlockSpec((blocks, per_group, P_SIZE, N), lambda g: (0, g, 0, 0)),
         out_shape=jax.ShapeDtypeStruct((blocks, groups * per_group, P_SIZE, N), F32),
         interpret=interpret,
     )(state_c, values_t, acc_t, delta_t)

time: 196 us -> 190 us (0.969)
  Pallas kernels: 40.8 us -> 34.6 us
    pallas_call x2, Pallas kernels: 13.3 us -> 7.16 us  [block_states(): pl.pallas_call(kernel, grid=(groups,), in_specs=[pl.BlockSpec((rows, N),...]
  transfers between devices with their start and end apart: 7 -> 7, of which waited for: 2 -> 2; matrix products, arithmetic and copies ran while one was open for 21% -> 22% of each run, Pallas kernels for 14% -> 13%
where the time goes in v7:
time: 190 us; the launch traced here: 189 us
  waiting for transfers between devices  48.3 us (25%)
  matrix products  37.9 us (20%)
  Pallas kernels  34.6 us (18%)
  other arithmetic  19.2 us (10%)
  local copies, waits for them, and re-layouts  17.7 us (9%)
  starting transfers between devices  17.3 us (9%)
  between operations  14 us (7%)
    reduce_scatter x1, waiting for transfers between devices, on_device(): summed = lax.psum_scatter(partial, 'chan', scatter_dimension=0, tiled=True)  44.5 us
    ppermute x6, starting transfers between devices, shifted(): return lax.ppermute(value, axis, pairs)  17.3 us
    pallas_call x2, Pallas kernels, block_intra(): pl.pallas_call(kernel, grid=(blocks, groups), in_specs=[pl.BlockSpec((Q,...  15.2 us
    dot_general x2, matrix products, project(): gate_in = jnp.dot(source, w_gate, preferred_element_type=F32).astype(BF16)  12.9 us
    pallas_call x2, Pallas kernels, block_finish(): pl.pallas_call(kernel, grid=(groups,), in_specs=[pl.BlockSpec((width_g, r...  12.3 us
    dot_general x2, matrix products, project(): jnp.dot(source, w_values, preferred_element_type=F32) * known[:, None]  9.7 us
    pallas_call x2, Pallas kernels, block_states(): pl.pallas_call(kernel, grid=(groups,), in_specs=[pl.BlockSpec((rows, N),...  7.16 us
    transpose x1, other arithmetic, local_scan(): values_t = values_c.T  5.59 us
  transfers between devices with their start and end apart: 7, of which 2 were waited for; matrix products, arithmetic and copies ran while one was open for 22% of the time, Pallas kernels for 13%

profile of v7, /device:TPU:0, one launch (start us, length us, event | category | flops | bytes accessed | tf_op | source)
XLA Modules:
  0.0 189.1 jit_solution(4420971380116476472)
XLA Ops:
  6.5 0.8 compare_select_fusion.2
  7.5 0.8 fusion.72
  8.3 1.3 collective-permute-start.1
  9.7 3.0 %collective-permute-start = (bf16[3,2176]{1,0:T(4,128)(2,1)S(1)}, bf16[3,2176]{1,0:T(4,128)(2,1)S(1)}, u32[]{:S(2)}, u32[]{:S(2)}) collective-permute-start(bf16[3,2176]{1,0:T(4,128)(2,1)S(1)} %pad_maximum_fusion.13), channel_id=1, source_target_pairs={{0,4},{4,8},{8,12},{1,5},{5,9},{9,13},{2,6},{6,10},{10,14},{3,7},{... | collective-permute-start | bytes 39176 | tf_op jit(solution)/shard_map/ppermute | solution.py:25
  12.8 3.6 %convert_bitcast_fusion = bf16[512,16,128]{0,2,1:T(8,128)(2,1)} fusion(bf16[512,2048]{1,0:T(8,128)(2,1)} %param.15), kind=kOutput, calls=%fused_computation.30 | convolution fusion | flops 269516800 | bytes 4194304 | tf_op jit(solution)/shard_map/rki,ij->rkj/dot_general | solution.py:232
  16.4 3.1 %rev.9 = bf16[512,16,128]{0,2,1:T(8,128)(2,1)} reverse(bf16[512,16,128]{0,2,1:T(8,128)(2,1)} %convert_bitcast_fusion), dimensions={1} | reverse | bytes 4194304 | tf_op jit(solution)/shard_map/jit(_flip)/rev | solution.py:235
  19.5 6.3 %multiply_convert_fusion.3 = bf16[512,1024]{0,1:T(8,128)(2,1)} fusion(bf16[512,2048]{1,0:T(8,128)(2,1)} %param.15, bf16[2048,1024]{1,0:T(8,128)(2,1)} %param.18, f32[512]{0:T(512)S(1)} %get-tuple-element.63), kind=kOutput, calls=%fused_computation.32 | convolution fusion | flops 2148532224 | bytes 7342080 | tf_op jit(solution)/shard_map/dot_general | solution.py:254
  25.8 3.4 %multiply_convert_fusion.1 = bf16[512,1024]{0,1:T(8,128)(2,1)} fusion(bf16[512,2048]{0,1:T(8,128)(2,1)S(1)} %bitcast.231, bf16[2048,1024]{1,0:T(8,128)(2,1)S(1)} %copy-done.8, f32[512]{0:T(512)S(1)} %get-tuple-element.63), kind=kOutput, calls=%fused_computation.29 | convolution fusion | flops 2148532224 | bytes 7342080 | tf_op jit(solution)/shard_map/dot_general | solution.py:254
  29.2 1.3 convolution_convert_fusion.3
  30.8 1.3 convolution_convert_fusion.4
  32.1 0.4 compare_select_fusion
  32.6 1.3 broadcast_multiply_fusion.1
  35.3 1.0 copy.121.a_ref
  36.4 1.3 broadcast_in_dim_reshape.5.k_ref
  37.7 1.0 copy.112.a_ref
  39.3 0.4 convolution_convert_fusion.8
  39.7 4.1 %fusion.17 = bf16[6,1024]{0,1:T(8,128)(2,1)S(1)} fusion(bf16[2048,1024]{1,0:T(8,128)(2,1)} %param.18, f32[6]{0:T(128)S(1)} %maximum_convert_fusion, bf16[3,2048]{1,0:T(4,128)(2,1)S(1)} %bitcast.262, bf16[3,2048]{1,0:T(4,128)(2,1)S(1)} %slice.267), kind=kOutput, calls=%fused_computation.46 | convolution fusion | flops 25227264 | bytes 4231192 | tf_op jit(solution)/shard_map/dot_general | solution.py:248
  44.0 5.6 %fusion.26 = (bf16[1024,512]{1,0:T(8,128)(2,1)}, bf16[1024,512]{1,0:T(8,128)(2,1)}) fusion(bf16[512,1024]{0,1:T(8,128)(2,1)S(1)} %copy-done.10, f32[1024]{0:T(1024)S(1)} %bitcast.266, bf16[3,1024]{0,1:T(8,128)(2,1)S(1)} %get-tuple-element.45, f32[1024]{0:T(1024)S(1)} %bitcast.267, f32[1024]{0:T(1024)S(1)} %bitcast.265, f32[1024]{0:T(1024)S(1)} %bitcast.264, ...), kind=kLoop, calls=%fused_computation.65 | loop fusion | flops 27262976 | bytes 4227072 | tf_op jit(solution)/shard_map/transpose | solution.py:285
  49.6 2.4 %multiply_convert_fusion.5 = (bf16[512,512]{1,0:T(8,128)(2,1)}, bf16[512,512]{1,0:T(8,128)(2,1)}) fusion(bf16[512,512]{1,0:T(8,128)(2,1)S(1)} %convolution_convert_fusion.4, bf16[3,512]{1,0:T(4,128)(2,1)S(1)} %get-tuple-element.55, f32[512]{0:T(512)S(1)} %bitcast.270, f32[512]{0:T(512)S(1)} %bitcast.271, f32[512]{0:T(512)S(1)} %bitcast.269, ...), kind=kLoop, calls=%fused_computation.64 | loop fusion | flops 13631488 | bytes 2113536 | tf_op jit(solution)/shard_map/convert_element_type | solution.py:200
  52.0 3.6 %shard_map.149 = f32[4,16,64,128]{3,2,1,0:T(8,128)} custom-call(bf16[512,512]{1,0:T(8,128)(2,1)} %get-tuple-element.54.c_ref.b_ref, bf16[1024,512]{1,0:T(8,128)(2,1)} %get-tuple-element.48.xt_ref, f32[2,8,512]{2,1,0:T(8,128)} %bitcast.254, f32[2,8,512]{2,1,0:T(8,128)} %bitcast.257), custom_call_target="tpu_custom_call" | custom-call | tf_op jit(solution)/shard_map/pallas_call | solution.py:95
  55.5 1.7 fusion.71
  57.3 1.3 fusion.69
  58.7 0.7 pad_maximum_fusion.8
  59.4 1.3 collective-permute-start.4
  60.7 3.6 %shard_map.146 = f32[4,16,64,128]{3,2,1,0:T(8,128)} custom-call(bf16[512,512]{1,0:T(8,128)(2,1)} %get-tuple-element.53.c_ref.b_ref, bf16[1024,512]{1,0:T(8,128)(2,1)} %get-tuple-element.47.xt_ref, f32[2,8,512]{2,1,0:T(8,128)} %bitcast.250, f32[2,8,512]{2,1,0:T(8,128)} %bitcast.259), custom_call_target="tpu_custom_call" | custom-call | tf_op jit(solution)/shard_map/pallas_call | solution.py:95
  64.3 1.7 fusion.70
  66.0 1.3 fusion.68
  67.5 7.6 %shard_map.148.y_ref = f32[1024,512]{1,0:T(8,128)} custom-call(bf16[512,512]{1,0:T(8,128)(2,1)} %get-tuple-element.54.c_ref.b_ref, bf16[512,512]{1,0:T(8,128)(2,1)} %get-tuple-element.54.c_ref.b_ref, bf16[1024,512]{1,0:T(8,128)(2,1)} %get-tuple-element.48.xt_ref, f32[2,512,8]{2,1,0:T(8,128)} %copy.121.a_ref, f32[2,8,512]{2,1,0:T(8,128)} %bitcast.255, ...), custom_call_target="tpu_custom_call" | custom-call | tf_op jit(solution)/shard_map/pallas_call | solution.py:134
  75.1 5.1 %collective-permute-start.2 = (bf16[16,8448]{1,0:T(8,128)(2,1)S(1)}, bf16[16,8448]{1,0:T(8,128)(2,1)S(1)}, u32[]{:S(2)}, u32[]{:S(2)}) collective-permute-start(bf16[16,8448]{1,0:T(8,128)(2,1)S(1)} %pad_maximum_fusion.6), channel_id=1, source_target_pairs={{0,4},{4,8},{8,12},{1,5},{5,9},{9,13},{2,6},{6,10},{10,14},{3,7},{... | collective-permute-start | bytes 811016 | tf_op jit(solution)/shard_map/ppermute | solution.py:25
  80.2 7.6 %shard_map.145.y_ref = f32[1024,512]{1,0:T(8,128)} custom-call(bf16[512,512]{1,0:T(8,128)(2,1)} %get-tuple-element.53.c_ref.b_ref, bf16[512,512]{1,0:T(8,128)(2,1)} %get-tuple-element.53.c_ref.b_ref, bf16[1024,512]{1,0:T(8,128)(2,1)} %get-tuple-element.47.xt_ref, f32[2,512,8]{2,1,0:T(8,128)} %copy.112.a_ref, f32[2,8,512]{2,1,0:T(8,128)} %bitcast.251, ...), custom_call_target="tpu_custom_call" | custom-call | tf_op jit(solution)/shard_map/pallas_call | solution.py:134
  88.3 0.8 pad_maximum_fusion.9
  89.1 1.3 collective-permute-start.5
  90.9 5.3 %collective-permute-start.3 = (bf16[16,8448]{1,0:T(8,128)(2,1)S(1)}, bf16[16,8448]{1,0:T(8,128)(2,1)S(1)}, u32[]{:S(2)}, u32[]{:S(2)}) collective-permute-start(bf16[16,8448]{1,0:T(8,128)(2,1)S(1)} %pad_maximum_fusion.7), channel_id=1, source_target_pairs={{0,8},{4,12},{1,9},{5,13},{2,10},{6,14},{3,11},{7,15},{16,24},{20,... | collective-permute-start | bytes 811016 | tf_op jit(solution)/shard_map/ppermute | solution.py:25
  96.2 3.7 %collective-permute-done.5 = bf16[16,8448]{1,0:T(8,128)(2,1)} collective-permute-done((bf16[16,8448]{1,0:T(8,128)(2,1)}, bf16[16,8448]{1,0:T(8,128)(2,1)}, u32[]{:S(2)}, u32[]{:S(2)}) %collective-permute-start.5) | collective-permute-done | bytes 270368 | tf_op jit(solution)/shard_map/ppermute | solution.py:25
  99.9 1.1 fusion.33
  101.1 0.3 multiply_add_fusion.2
  101.4 1.4 pad_maximum_fusion.1.s_ref
  102.9 6.1 %shard_map.150 = f32[1024,512]{1,0:T(8,128)} custom-call(f32[1024,512]{1,0:T(8,128)} %shard_map.148.y_ref, bf16[512,512]{1,0:T(8,128)(2,1)} %get-tuple-element.54.c_ref.b_ref, bf16[1024,512]{1,0:T(8,128)(2,1)} %get-tuple-element.48.xt_ref, f32[2,8,512]{2,1,0:T(8,128)} %bitcast.256, f32[4,16,64,128]{3,2,1,0:T(8,128)} %pad_maximum_fusion.1.s_ref, ...), custom_call_target="tpu_custom_call" | custom-call | tf_op jit(solution)/shard_map/pallas_call | solution.py:177
  109.0 7.1 %bitcast_reduce_fusion = (f32[512,2]{0,1:T(2,128)S(1)}, f32[512,1024]{0,1:T(8,128)}) fusion(bf16[512,2048]{0,1:T(8,128)(2,1)S(1)} %bitcast.234, bf16[2048,1024]{1,0:T(8,128)(2,1)} %param.17, f32[1024,512]{1,0:T(8,128)} %shard_map.150), kind=kOutput, calls=%fused_computation.22 | convolution fusion | flops 2152201216 | bytes 10489856 | tf_op jit(solution)/shard_map/dot_general | solution.py:253
  116.3 1.3 copy-done.4
  117.9 1.5 pad_maximum_fusion.s_ref
  119.4 6.1 %shard_map.147 = f32[1024,512]{1,0:T(8,128)} custom-call(f32[1024,512]{1,0:T(8,128)} %shard_map.145.y_ref, bf16[512,512]{1,0:T(8,128)(2,1)} %get-tuple-element.53.c_ref.b_ref, bf16[1024,512]{1,0:T(8,128)(2,1)} %get-tuple-element.47.xt_ref, f32[2,8,512]{2,1,0:T(8,128)} %bitcast.252, f32[4,16,64,128]{3,2,1,0:T(8,128)} %pad_maximum_fusion.s_ref, ...), custom_call_target="tpu_custom_call" | custom-call | tf_op jit(solution)/shard_map/pallas_call | solution.py:177
  125.6 5.8 %bitcast_reduce_fusion.1 = (f32[512,2]{0,1:T(2,128)S(1)}, f32[512,1024]{0,1:T(8,128)S(1)}) fusion(bf16[512,2048]{1,0:T(8,128)(2,1)S(1)} %copy-done.7, bf16[2048,1024]{1,0:T(8,128)(2,1)} %param.17, f32[1024,512]{1,0:T(8,128)} %shard_map.147), kind=kOutput, calls=%fused_computation.26 | convolution fusion | flops 2152201216 | bytes 10489856 | tf_op jit(solution)/shard_map/dot_general | solution.py:253
  131.5 0.4 fusion.14
  131.9 1.8 copy-done.23
  133.7 2.5 %convolution_convert_fusion = bf16[512,2048]{1,0:T(8,128)(2,1)S(1)} fusion(bf16[1024,2048]{1,0:T(8,128)(2,1)S(1)} %copy-done.23, bf16[512,1024]{0,1:T(8,128)(2,1)S(1)} %get-tuple-element.62, bf16[512,1024]{0,1:T(8,128)(2,1)S(1)} %get-tuple-element.61), kind=kOutput, calls=%fused_computation | convolution fusion | flops 2150629376 | bytes 8388608 | tf_op jit(solution)/shard_map/dot_general | solution.py:316
  136.2 1.5 copy.190
  137.7 44.5 %reduce-scatter.2.cloned.1.call-done = bf16[1,512,512]{2,1,0:T(8,128)(2,1)} async-done(((bf16[4,512,512]{2,1,0:T(8,128)(2,1)}), bf16[1,512,512]{2,1,0:T(8,128)(2,1)}) %reduce-scatter.2.cloned.1.call-update) | async-done | bytes 524304 | tf_op jit(solution)/shard_map/reduce_scatter | solution.py:318
  (116 shorter events, 4.7 us)
Async XLA Ops:
  6.5 22.7 %copy-start = (bf16[2048,512]{1,0:T(8,128)(2,1)S(1)}, bf16[2048,512]{1,0:T(8,128)(2,1)}, u32[]{:S(2)}) copy-start(bf16[2048,512]{1,0:T(8,128)(2,1)} %param.19) | copy-start | bytes 6291460
  6.5 175.7 %reduce-scatter.2.cloned.1.call-start = ((), (), s32[]{:S(2)}) async-start(), calls=%async_computation.1 | async-start | bytes 2621440 | tf_op jit(solution)/shard_map/reduce_scatter | solution.py:318
  8.3 30.4 %collective-permute-start.1 = (bf16[3,2176]{1,0:T(4,128)(2,1)S(1)}, bf16[3,2176]{1,0:T(4,128)(2,1)S(1)}, u32[]{:S(2)}, u32[]{:S(2)}) collective-permute-start(bf16[3,2176]{1,0:T(4,128)(2,1)S(1)} %pad_maximum_fusion.14), channel_id=1, source_target_pairs={{4,0},{8,4},{12,8},{5,1},{9,5},{13,9},{6,2},{10,6},{14,10},{7,3},{... | collective-permute-start | bytes 39176 | tf_op jit(solution)/shard_map/ppermute | solution.py:25
  9.7 29.4 %collective-permute-start = (bf16[3,2176]{1,0:T(4,128)(2,1)S(1)}, bf16[3,2176]{1,0:T(4,128)(2,1)S(1)}, u32[]{:S(2)}, u32[]{:S(2)}) collective-permute-start(bf16[3,2176]{1,0:T(4,128)(2,1)S(1)} %pad_maximum_fusion.13), channel_id=1, source_target_pairs={{0,4},{4,8},{8,12},{1,5},{5,9},{9,13},{2,6},{6,10},{10,14},{3,7},{... | collective-permute-start | bytes 39176 | tf_op jit(solution)/shard_map/ppermute | solution.py:25
  19.5 6.3 %copy-start.2 = (bf16[512,16,128]{0,2,1:T(8,128)(2,1)S(1)}, bf16[512,16,128]{0,2,1:T(8,128)(2,1)}, u32[]{:S(2)}) copy-start(bf16[512,16,128]{0,2,1:T(8,128)(2,1)} %rev.9) | copy-start | bytes 6291460
  19.5 6.3 %copy-start.8 = (bf16[2048,1024]{1,0:T(8,128)(2,1)S(1)}, bf16[2048,1024]{1,0:T(8,128)(2,1)}, u32[]{:S(2)}) copy-start(bf16[2048,1024]{1,0:T(8,128)(2,1)} %param.18) | copy-start | bytes 12582916
  29.2 1.6 copy-start.6
  30.8 1.3 copy-start.24
  30.8 1.3 copy-start.15
  30.8 1.3 copy-start.21
  32.1 2.2 %copy-start.16 = (f32[4,1024]{1,0:T(4,128)S(1)}, f32[4,1024]{1,0:T(4,128)}, u32[]{:S(2)}) copy-start(f32[4,1024]{1,0:T(4,128)} %param.21) | copy-start | bytes 49156
  32.1 2.2 %copy-start.17 = (f32[4,512]{1,0:T(4,128)S(1)}, f32[4,512]{1,0:T(4,128)}, u32[]{:S(2)}) copy-start(f32[4,512]{1,0:T(4,128)} %param.23) | copy-start | bytes 24580
  32.5 5.2 %copy-start.14 = (f32[512,16]{0,1:T(8,128)}, f32[512,16]{0,1:T(8,128)S(1)}, u32[]{:S(2)}) copy-start(f32[512,16]{0,1:T(8,128)S(1)} %compare_select_fusion) | copy-start | bytes 98308
  32.6 3.7 %copy-start.22 = (f32[16]{0:T(128)S(1)}, f32[16]{0:T(128)}, u32[]{:S(2)}) copy-start(f32[16]{0:T(128)} %param.27) | copy-start | bytes 196
  35.3 8.5 %copy-start.13 = (f32[512,2,8]{0,2,1:T(8,128)}, f32[512,2,8]{0,2,1:T(8,128)S(1)}, u32[]{:S(2)}) copy-start(f32[512,2,8]{0,2,1:T(8,128)S(1)} %reshape_reshape.7) | copy-start | bytes 98308
  37.7 6.1 %copy-start.12 = (f32[512,2,8]{0,2,1:T(8,128)}, f32[512,2,8]{0,2,1:T(8,128)S(1)}, u32[]{:S(2)}) copy-start(f32[512,2,8]{0,2,1:T(8,128)S(1)} %reshape_reshape.6) | copy-start | bytes 98308
  39.7 4.3 %copy-start.10 = (bf16[512,1024]{0,1:T(8,128)(2,1)S(1)}, bf16[512,1024]{0,1:T(8,128)(2,1)}, u32[]{:S(2)}) copy-start(bf16[512,1024]{0,1:T(8,128)(2,1)} %multiply_convert_fusion.3) | copy-start | bytes 3145732
  39.7 4.3 %copy-start.11 = (bf16[512,1024]{0,1:T(8,128)(2,1)S(1)}, bf16[512,1024]{0,1:T(8,128)(2,1)}, u32[]{:S(2)}) copy-start(bf16[512,1024]{0,1:T(8,128)(2,1)} %multiply_convert_fusion.1) | copy-start | bytes 3145732
  39.7 4.3 %copy-start.18 = (f32[1024]{0:T(1024)S(1)}, f32[1024]{0:T(1024)}, u32[]{:S(2)}) copy-start(f32[1024]{0:T(1024)} %param.22) | copy-start | bytes 12292
  44.0 5.6 %copy-start.20 = (f32[512]{0:T(512)S(1)}, f32[512]{0:T(512)}, u32[]{:S(2)}) copy-start(f32[512]{0:T(512)} %param.24) | copy-start | bytes 6148
  59.4 28.4 %collective-permute-start.4 = (bf16[16,8448]{1,0:T(8,128)(2,1)}, bf16[16,8448]{1,0:T(8,128)(2,1)S(1)}, u32[]{:S(2)}, u32[]{:S(2)}) collective-permute-start(bf16[16,8448]{1,0:T(8,128)(2,1)} %pad_maximum_fusion.8), channel_id=1, source_target_pairs={{4,0},{8,4},{12,8},{5,1},{9,5},{13,9},{6,2},{10,6},{14,10},{7,3},{... | collective-permute-start | bytes 811016 | tf_op jit(solution)/shard_map/ppermute | solution.py:25
  75.1 15.2 %collective-permute-start.2 = (bf16[16,8448]{1,0:T(8,128)(2,1)S(1)}, bf16[16,8448]{1,0:T(8,128)(2,1)S(1)}, u32[]{:S(2)}, u32[]{:S(2)}) collective-permute-start(bf16[16,8448]{1,0:T(8,128)(2,1)S(1)} %pad_maximum_fusion.6), channel_id=1, source_target_pairs={{0,4},{4,8},{8,12},{1,5},{5,9},{9,13},{2,6},{6,10},{10,14},{3,7},{... | collective-permute-start | bytes 811016 | tf_op jit(solution)/shard_map/ppermute | solution.py:25
  88.3 12.8 %copy-start.5 = (f32[4,16,64,128]{3,2,1,0:T(8,128)S(1)}, f32[4,16,64,128]{3,2,1,0:T(8,128)}, u32[]{:S(2)}) copy-start(f32[4,16,64,128]{3,2,1,0:T(8,128)} %shard_map.149) | copy-start | bytes 6291460
  89.1 10.8 %collective-permute-start.5 = (bf16[16,8448]{1,0:T(8,128)(2,1)}, bf16[16,8448]{1,0:T(8,128)(2,1)}, u32[]{:S(2)}, u32[]{:S(2)}) collective-permute-start(bf16[16,8448]{1,0:T(8,128)(2,1)} %pad_maximum_fusion.9), channel_id=1, source_target_pairs={{8,0},{12,4},{9,1},{13,5},{10,2},{14,6},{11,3},{15,7},{24,16},{28,... | collective-permute-start | bytes 811016 | tf_op jit(solution)/shard_map/ppermute | solution.py:25
  90.9 25.2 %collective-permute-start.3 = (bf16[16,8448]{1,0:T(8,128)(2,1)S(1)}, bf16[16,8448]{1,0:T(8,128)(2,1)S(1)}, u32[]{:S(2)}, u32[]{:S(2)}) collective-permute-start(bf16[16,8448]{1,0:T(8,128)(2,1)S(1)} %pad_maximum_fusion.7), channel_id=1, source_target_pairs={{0,8},{4,12},{1,9},{5,13},{2,10},{6,14},{3,11},{7,15},{16,24},{20,... | collective-permute-start | bytes 811016 | tf_op jit(solution)/shard_map/ppermute | solution.py:25
  102.9 6.1 %copy-start.3 = (bf16[512,16,128]{0,2,1:T(8,128)(2,1)S(1)}, bf16[512,16,128]{0,2,1:T(8,128)(2,1)}, u32[]{:S(2)}) copy-start(bf16[512,16,128]{0,2,1:T(8,128)(2,1)} %rev.9) | copy-start | bytes 6291460
  116.0 1.6 copy-start.4
  119.4 6.2 %copy-start.7 = (bf16[512,2048]{1,0:T(8,128)(2,1)S(1)}, bf16[512,2048]{1,0:T(8,128)(2,1)}, u32[]{:S(2)}) copy-start(bf16[512,2048]{1,0:T(8,128)(2,1)} %param.15) | copy-start | bytes 6291460
  125.6 5.9 %copy-start.9 = (f32[512,1024]{0,1:T(8,128)S(1)}, f32[512,1024]{0,1:T(8,128)}, u32[]{:S(2)}) copy-start(f32[512,1024]{0,1:T(8,128)} %get-tuple-element.85) | copy-start | bytes 6291460
  125.6 5.9 %copy-start.19 = (f32[1024]{0:T(1024)S(1)}, f32[1024]{0:T(1024)}, u32[]{:S(2)}) copy-start(f32[1024]{0:T(1024)} %param.28) | copy-start | bytes 12292
  131.5 2.2 %copy-start.23 = (bf16[1024,2048]{1,0:T(8,128)(2,1)S(1)}, bf16[1024,2048]{1,0:T(8,128)(2,1)}, u32[]{:S(2)}) copy-start(bf16[1024,2048]{1,0:T(8,128)(2,1)} %param.29) | copy-start | bytes 12582916
  136.2 46.1 %copy-start.1 = (bf16[2048,512]{1,0:T(8,128)(2,1)S(1)}, bf16[2048,512]{1,0:T(8,128)(2,1)}, u32[]{:S(2)}) copy-start(bf16[2048,512]{1,0:T(8,128)(2,1)} %param.19) | copy-start | bytes 6291460
Sparse Core Ops, SparseCore 0:
  137.8 44.3 reduce-scatter.1

commit v8 on v7

--- a/solution.py
+++ b/solution.py
@@ -114,35 +114,37 @@
     width_g = per_group * P_SIZE
 
     def kernel(c_ref, b_ref, xt_ref, a_ref, at_ref, dt_ref, y_ref):
-        inner = lax.dot_general(
-            c_ref[...], b_ref[...], (((1,), (1,)), ((), ())), preferred_element_type=F32
-        )
         row = lax.broadcasted_iota(jnp.int32, (Q, Q), 0)
         col = lax.broadcasted_iota(jnp.int32, (Q, Q), 1)
         mask = row >= col if forward else row <= col
-        for j in range(per_group):
-            a_col = a_ref[0, :, j : j + 1]
-            a_row = at_ref[0, j : j + 1, :]
-            d_row = dt_ref[0, j : j + 1, :]
-            differ = jnp.where(mask, a_col - a_row, 0.0)
-            m = jnp.where(mask, jnp.exp(differ), 0.0) * d_row * inner
-            xt_j = xt_ref[j * P_SIZE : (j + 1) * P_SIZE, :]
-            y_ref[j * P_SIZE : (j + 1) * P_SIZE, :] = lax.dot_general(
-                xt_j, m.astype(BF16), (((1,), (1,)), ((), ())), preferred_element_type=F32
+        for blk in range(blocks):
+            cols = slice(blk * Q, (blk + 1) * Q)
+            inner = lax.dot_general(
+                c_ref[cols, :], b_ref[cols, :], (((1,), (1,)), ((), ())), preferred_element_type=F32
             )
+            for j in range(per_group):
+                a_col = a_ref[0, cols, j : j + 1]
+                a_row = at_ref[0, j : j + 1, cols]
+                d_row = dt_ref[0, j : j + 1, cols]
+                differ = jnp.where(mask, a_col - a_row, 0.0)
+                m = jnp.where(mask, jnp.exp(differ), 0.0) * d_row * inner
+                xt_j = xt_ref[j * P_SIZE : (j + 1) * P_SIZE, cols]
+                y_ref[j * P_SIZE : (j + 1) * P_SIZE, cols] = lax.dot_general(
+                    xt_j, m.astype(BF16), (((1,), (1,)), ((), ())), preferred_element_type=F32
+                )
 
     return pl.pallas_call(
         kernel,
-        grid=(blocks, groups),
+        grid=(groups,),
         in_specs=[
-            pl.BlockSpec((Q, N), lambda b, g: (b, 2 * g + 1)),
-            pl.BlockSpec((Q, N), lambda b, g: (b, 2 * g)),
-            pl.BlockSpec((width_g, Q), lambda b, g: (g, b)),
-            pl.BlockSpec((1, Q, per_group), lambda b, g: (g, b, 0)),
-            pl.BlockSpec((1, per_group, Q), lambda b, g: (g, 0, b)),
-            pl.BlockSpec((1, per_group, Q), lambda b, g: (g, 0, b)),
+            pl.BlockSpec((rows, N), lambda g: (0, 2 * g + 1)),
+            pl.BlockSpec((rows, N), lambda g: (0, 2 * g)),
+            pl.BlockSpec((width_g, rows), lambda g: (g, 0)),
+            pl.BlockSpec((1, rows, per_group), lambda g: (g, 0, 0)),
+            pl.BlockSpec((1, per_group, rows), lambda g: (g, 0, 0)),
+            pl.BlockSpec((1, per_group, rows), lambda g: (g, 0, 0)),
         ],
-        out_specs=pl.BlockSpec((width_g, Q), lambda b, g: (g, b)),
+        out_specs=pl.BlockSpec((width_g, rows), lambda g: (g, 0)),
         out_shape=jax.ShapeDtypeStruct((groups * width_g, rows), F32),
         interpret=interpret,
     )(state_c, state_c, values_t, acc_g, acc_t, delta_t)

time: 190 us -> 185 us (0.974)
  Pallas kernels: 34.6 us -> 29.5 us
    pallas_call x2, Pallas kernels: 15.2 us -> 10.1 us  [block_intra(): pl.pallas_call(kernel, grid=(groups,), in_specs=[pl.BlockSpec((rows, N),...]
  transfers between devices with their start and end apart: 7 -> 7, of which waited for: 2 -> 2; matrix products, arithmetic and copies ran while one was open for 22% -> 22% of each run, Pallas kernels for 13% -> 11%
where the time goes in v8:
time: 185 us; the launch traced here: 184 us
  waiting for transfers between devices  48.3 us (26%)
  matrix products  37.9 us (20%)
  Pallas kernels  29.5 us (16%)
  other arithmetic  19.2 us (10%)
  local copies, waits for them, and re-layouts  17.7 us (10%)
  starting transfers between devices  17.3 us (9%)
  between operations  14 us (8%)
    reduce_scatter x1, waiting for transfers between devices, on_device(): summed = lax.psum_scatter(partial, 'chan', scatter_dimension=0, tiled=True)  44.5 us
    ppermute x6, starting transfers between devices, shifted(): return lax.ppermute(value, axis, pairs)  17.3 us
    dot_general x2, matrix products, project(): gate_in = jnp.dot(source, w_gate, preferred_element_type=F32).astype(BF16)  12.9 us
    pallas_call x2, Pallas kernels, block_finish(): pl.pallas_call(kernel, grid=(groups,), in_specs=[pl.BlockSpec((width_g, r...  12.3 us
    pallas_call x2, Pallas kernels, block_intra(): pl.pallas_call(kernel, grid=(groups,), in_specs=[pl.BlockSpec((rows, N),...  10.1 us
    dot_general x2, matrix products, project(): jnp.dot(source, w_values, preferred_element_type=F32) * known[:, None]  9.7 us
    pallas_call x2, Pallas kernels, block_states(): pl.pallas_call(kernel, grid=(groups,), in_specs=[pl.BlockSpec((rows, N),...  7.16 us
    transpose x1, other arithmetic, local_scan(): values_t = values_c.T  5.59 us
  transfers between devices with their start and end apart: 7, of which 2 were waited for; matrix products, arithmetic and copies ran while one was open for 22% of the time, Pallas kernels for 11%

profile of v8, /device:TPU:0, one launch (start us, length us, event | category | flops | bytes accessed | tf_op | source)
XLA Modules:
  0.0 184.0 jit_solution(15492880343452867880)
XLA Ops:
  6.5 0.8 compare_select_fusion.2
  7.5 0.8 fusion.72
  8.3 1.3 collective-permute-start.1
  9.7 3.0 %collective-permute-start = (bf16[3,2176]{1,0:T(4,128)(2,1)S(1)}, bf16[3,2176]{1,0:T(4,128)(2,1)S(1)}, u32[]{:S(2)}, u32[]{:S(2)}) collective-permute-start(bf16[3,2176]{1,0:T(4,128)(2,1)S(1)} %pad_maximum_fusion.13), channel_id=1, source_target_pairs={{0,4},{4,8},{8,12},{1,5},{5,9},{9,13},{2,6},{6,10},{10,14},{3,7},{... | collective-permute-start | bytes 39176 | tf_op jit(solution)/shard_map/ppermute | solution.py:25
  12.8 3.6 %convert_bitcast_fusion = bf16[512,16,128]{0,2,1:T(8,128)(2,1)} fusion(bf16[512,2048]{1,0:T(8,128)(2,1)} %param.15), kind=kOutput, calls=%fused_computation.30 | convolution fusion | flops 269516800 | bytes 4194304 | tf_op jit(solution)/shard_map/rki,ij->rkj/dot_general | solution.py:234
  16.4 3.1 %rev.9 = bf16[512,16,128]{0,2,1:T(8,128)(2,1)} reverse(bf16[512,16,128]{0,2,1:T(8,128)(2,1)} %convert_bitcast_fusion), dimensions={1} | reverse | bytes 4194304 | tf_op jit(solution)/shard_map/jit(_flip)/rev | solution.py:237
  19.5 6.3 %multiply_convert_fusion.3 = bf16[512,1024]{0,1:T(8,128)(2,1)} fusion(bf16[512,2048]{1,0:T(8,128)(2,1)} %param.15, bf16[2048,1024]{1,0:T(8,128)(2,1)} %param.18, f32[512]{0:T(512)S(1)} %get-tuple-element.63), kind=kOutput, calls=%fused_computation.32 | convolution fusion | flops 2148532224 | bytes 7342080 | tf_op jit(solution)/shard_map/dot_general | solution.py:256
  25.8 3.4 %multiply_convert_fusion.1 = bf16[512,1024]{0,1:T(8,128)(2,1)} fusion(bf16[512,2048]{0,1:T(8,128)(2,1)S(1)} %bitcast.231, bf16[2048,1024]{1,0:T(8,128)(2,1)S(1)} %copy-done.8, f32[512]{0:T(512)S(1)} %get-tuple-element.63), kind=kOutput, calls=%fused_computation.29 | convolution fusion | flops 2148532224 | bytes 7342080 | tf_op jit(solution)/shard_map/dot_general | solution.py:256
  29.2 1.3 convolution_convert_fusion.3
  30.8 1.3 convolution_convert_fusion.4
  32.1 0.4 compare_select_fusion
  32.6 1.3 broadcast_multiply_fusion.1
  35.3 1.0 copy.121.a_ref
  36.4 1.3 broadcast_in_dim_reshape.5.k_ref
  37.7 1.0 copy.112.a_ref
  39.3 0.4 convolution_convert_fusion.8
  39.7 4.1 %fusion.17 = bf16[6,1024]{0,1:T(8,128)(2,1)S(1)} fusion(bf16[2048,1024]{1,0:T(8,128)(2,1)} %param.18, f32[6]{0:T(128)S(1)} %maximum_convert_fusion, bf16[3,2048]{1,0:T(4,128)(2,1)S(1)} %bitcast.262, bf16[3,2048]{1,0:T(4,128)(2,1)S(1)} %slice.267), kind=kOutput, calls=%fused_computation.46 | convolution fusion | flops 25227264 | bytes 4231192 | tf_op jit(solution)/shard_map/dot_general | solution.py:250
  44.0 5.6 %fusion.26 = (bf16[1024,512]{1,0:T(8,128)(2,1)}, bf16[1024,512]{1,0:T(8,128)(2,1)}) fusion(bf16[512,1024]{0,1:T(8,128)(2,1)S(1)} %copy-done.10, f32[1024]{0:T(1024)S(1)} %bitcast.266, bf16[3,1024]{0,1:T(8,128)(2,1)S(1)} %get-tuple-element.45, f32[1024]{0:T(1024)S(1)} %bitcast.267, f32[1024]{0:T(1024)S(1)} %bitcast.265, f32[1024]{0:T(1024)S(1)} %bitcast.264, ...), kind=kLoop, calls=%fused_computation.65 | loop fusion | flops 27262976 | bytes 4227072 | tf_op jit(solution)/shard_map/transpose | solution.py:287
  49.6 2.4 %multiply_convert_fusion.5 = (bf16[512,512]{1,0:T(8,128)(2,1)}, bf16[512,512]{1,0:T(8,128)(2,1)}) fusion(bf16[512,512]{1,0:T(8,128)(2,1)S(1)} %convolution_convert_fusion.4, bf16[3,512]{1,0:T(4,128)(2,1)S(1)} %get-tuple-element.55, f32[512]{0:T(512)S(1)} %bitcast.270, f32[512]{0:T(512)S(1)} %bitcast.271, f32[512]{0:T(512)S(1)} %bitcast.269, ...), kind=kLoop, calls=%fused_computation.64 | loop fusion | flops 13631488 | bytes 2113536 | tf_op jit(solution)/shard_map/convert_element_type | solution.py:202
  52.0 3.6 %shard_map.149 = f32[4,16,64,128]{3,2,1,0:T(8,128)} custom-call(bf16[512,512]{1,0:T(8,128)(2,1)} %get-tuple-element.54.c_ref.b_ref, bf16[1024,512]{1,0:T(8,128)(2,1)} %get-tuple-element.48.xt_ref, f32[2,8,512]{2,1,0:T(8,128)} %bitcast.254, f32[2,8,512]{2,1,0:T(8,128)} %bitcast.257), custom_call_target="tpu_custom_call" | custom-call | tf_op jit(solution)/shard_map/pallas_call | solution.py:95
  55.5 1.7 fusion.71
  57.3 1.3 fusion.69
  58.7 0.7 pad_maximum_fusion.8
  59.4 1.3 collective-permute-start.4
  60.7 3.6 %shard_map.146 = f32[4,16,64,128]{3,2,1,0:T(8,128)} custom-call(bf16[512,512]{1,0:T(8,128)(2,1)} %get-tuple-element.53.c_ref.b_ref, bf16[1024,512]{1,0:T(8,128)(2,1)} %get-tuple-element.47.xt_ref, f32[2,8,512]{2,1,0:T(8,128)} %bitcast.250, f32[2,8,512]{2,1,0:T(8,128)} %bitcast.259), custom_call_target="tpu_custom_call" | custom-call | tf_op jit(solution)/shard_map/pallas_call | solution.py:95
  64.3 1.7 fusion.70
  66.0 1.3 fusion.68
  67.5 5.1 %shard_map.148.y_ref = f32[1024,512]{1,0:T(8,128)} custom-call(bf16[512,512]{1,0:T(8,128)(2,1)} %get-tuple-element.54.c_ref.b_ref, bf16[512,512]{1,0:T(8,128)(2,1)} %get-tuple-element.54.c_ref.b_ref, bf16[1024,512]{1,0:T(8,128)(2,1)} %get-tuple-element.48.xt_ref, f32[2,512,8]{2,1,0:T(8,128)} %copy.121.a_ref, f32[2,8,512]{2,1,0:T(8,128)} %bitcast.255, ...), custom_call_target="tpu_custom_call" | custom-call | tf_op jit(solution)/shard_map/pallas_call | solution.py:136
  72.5 5.1 %collective-permute-start.2 = (bf16[16,8448]{1,0:T(8,128)(2,1)S(1)}, bf16[16,8448]{1,0:T(8,128)(2,1)S(1)}, u32[]{:S(2)}, u32[]{:S(2)}) collective-permute-start(bf16[16,8448]{1,0:T(8,128)(2,1)S(1)} %pad_maximum_fusion.6), channel_id=1, source_target_pairs={{0,4},{4,8},{8,12},{1,5},{5,9},{9,13},{2,6},{6,10},{10,14},{3,7},{... | collective-permute-start | bytes 811016 | tf_op jit(solution)/shard_map/ppermute | solution.py:25
  77.6 5.1 %shard_map.145.y_ref = f32[1024,512]{1,0:T(8,128)} custom-call(bf16[512,512]{1,0:T(8,128)(2,1)} %get-tuple-element.53.c_ref.b_ref, bf16[512,512]{1,0:T(8,128)(2,1)} %get-tuple-element.53.c_ref.b_ref, bf16[1024,512]{1,0:T(8,128)(2,1)} %get-tuple-element.47.xt_ref, f32[2,512,8]{2,1,0:T(8,128)} %copy.112.a_ref, f32[2,8,512]{2,1,0:T(8,128)} %bitcast.251, ...), custom_call_target="tpu_custom_call" | custom-call | tf_op jit(solution)/shard_map/pallas_call | solution.py:136
  83.2 0.8 pad_maximum_fusion.9
  84.0 1.3 collective-permute-start.5
  85.8 5.3 %collective-permute-start.3 = (bf16[16,8448]{1,0:T(8,128)(2,1)S(1)}, bf16[16,8448]{1,0:T(8,128)(2,1)S(1)}, u32[]{:S(2)}, u32[]{:S(2)}) collective-permute-start(bf16[16,8448]{1,0:T(8,128)(2,1)S(1)} %pad_maximum_fusion.7), channel_id=1, source_target_pairs={{0,8},{4,12},{1,9},{5,13},{2,10},{6,14},{3,11},{7,15},{16,24},{20,... | collective-permute-start | bytes 811016 | tf_op jit(solution)/shard_map/ppermute | solution.py:25
  91.1 3.7 %collective-permute-done.5 = bf16[16,8448]{1,0:T(8,128)(2,1)} collective-permute-done((bf16[16,8448]{1,0:T(8,128)(2,1)}, bf16[16,8448]{1,0:T(8,128)(2,1)}, u32[]{:S(2)}, u32[]{:S(2)}) %collective-permute-start.5) | collective-permute-done | bytes 270368 | tf_op jit(solution)/shard_map/ppermute | solution.py:25
  94.8 1.1 fusion.33
  96.0 0.3 multiply_add_fusion.2
  96.3 1.4 pad_maximum_fusion.1.s_ref
  97.8 6.1 %shard_map.150 = f32[1024,512]{1,0:T(8,128)} custom-call(f32[1024,512]{1,0:T(8,128)} %shard_map.148.y_ref, bf16[512,512]{1,0:T(8,128)(2,1)} %get-tuple-element.54.c_ref.b_ref, bf16[1024,512]{1,0:T(8,128)(2,1)} %get-tuple-element.48.xt_ref, f32[2,8,512]{2,1,0:T(8,128)} %bitcast.256, f32[4,16,64,128]{3,2,1,0:T(8,128)} %pad_maximum_fusion.1.s_ref, ...), custom_call_target="tpu_custom_call" | custom-call | tf_op jit(solution)/shard_map/pallas_call | solution.py:179
  103.9 7.1 %bitcast_reduce_fusion = (f32[512,2]{0,1:T(2,128)S(1)}, f32[512,1024]{0,1:T(8,128)}) fusion(bf16[512,2048]{0,1:T(8,128)(2,1)S(1)} %bitcast.234, bf16[2048,1024]{1,0:T(8,128)(2,1)} %param.17, f32[1024,512]{1,0:T(8,128)} %shard_map.150), kind=kOutput, calls=%fused_computation.22 | convolution fusion | flops 2152201216 | bytes 10489856 | tf_op jit(solution)/shard_map/dot_general | solution.py:255
  111.2 1.3 copy-done.4
  112.8 1.5 pad_maximum_fusion.s_ref
  114.3 6.1 %shard_map.147 = f32[1024,512]{1,0:T(8,128)} custom-call(f32[1024,512]{1,0:T(8,128)} %shard_map.145.y_ref, bf16[512,512]{1,0:T(8,128)(2,1)} %get-tuple-element.53.c_ref.b_ref, bf16[1024,512]{1,0:T(8,128)(2,1)} %get-tuple-element.47.xt_ref, f32[2,8,512]{2,1,0:T(8,128)} %bitcast.252, f32[4,16,64,128]{3,2,1,0:T(8,128)} %pad_maximum_fusion.s_ref, ...), custom_call_target="tpu_custom_call" | custom-call | tf_op jit(solution)/shard_map/pallas_call | solution.py:179
  120.5 5.8 %bitcast_reduce_fusion.1 = (f32[512,2]{0,1:T(2,128)S(1)}, f32[512,1024]{0,1:T(8,128)S(1)}) fusion(bf16[512,2048]{1,0:T(8,128)(2,1)S(1)} %copy-done.7, bf16[2048,1024]{1,0:T(8,128)(2,1)} %param.17, f32[1024,512]{1,0:T(8,128)} %shard_map.147), kind=kOutput, calls=%fused_computation.26 | convolution fusion | flops 2152201216 | bytes 10489856 | tf_op jit(solution)/shard_map/dot_general | solution.py:255
  126.4 0.4 fusion.14
  126.8 1.8 copy-done.23
  128.5 2.5 %convolution_convert_fusion = bf16[512,2048]{1,0:T(8,128)(2,1)S(1)} fusion(bf16[1024,2048]{1,0:T(8,128)(2,1)S(1)} %copy-done.23, bf16[512,1024]{0,1:T(8,128)(2,1)S(1)} %get-tuple-element.62, bf16[512,1024]{0,1:T(8,128)(2,1)S(1)} %get-tuple-element.61), kind=kOutput, calls=%fused_computation | convolution fusion | flops 2150629376 | bytes 8388608 | tf_op jit(solution)/shard_map/dot_general | solution.py:318
  131.1 1.5 copy.190
  132.6 44.5 %reduce-scatter.2.cloned.1.call-done = bf16[1,512,512]{2,1,0:T(8,128)(2,1)} async-done(((bf16[4,512,512]{2,1,0:T(8,128)(2,1)}), bf16[1,512,512]{2,1,0:T(8,128)(2,1)}) %reduce-scatter.2.cloned.1.call-update) | async-done | bytes 524304 | tf_op jit(solution)/shard_map/reduce_scatter | solution.py:320
  (116 shorter events, 4.7 us)
Async XLA Ops:
  6.5 22.7 %copy-start = (bf16[2048,512]{1,0:T(8,128)(2,1)S(1)}, bf16[2048,512]{1,0:T(8,128)(2,1)}, u32[]{:S(2)}) copy-start(bf16[2048,512]{1,0:T(8,128)(2,1)} %param.19) | copy-start | bytes 6291460
  6.5 170.6 %reduce-scatter.2.cloned.1.call-start = ((), (), s32[]{:S(2)}) async-start(), calls=%async_computation.1 | async-start | bytes 2621440 | tf_op jit(solution)/shard_map/reduce_scatter | solution.py:320
  8.3 30.4 %collective-permute-start.1 = (bf16[3,2176]{1,0:T(4,128)(2,1)S(1)}, bf16[3,2176]{1,0:T(4,128)(2,1)S(1)}, u32[]{:S(2)}, u32[]{:S(2)}) collective-permute-start(bf16[3,2176]{1,0:T(4,128)(2,1)S(1)} %pad_maximum_fusion.14), channel_id=1, source_target_pairs={{4,0},{8,4},{12,8},{5,1},{9,5},{13,9},{6,2},{10,6},{14,10},{7,3},{... | collective-permute-start | bytes 39176 | tf_op jit(solution)/shard_map/ppermute | solution.py:25
  9.7 29.4 %collective-permute-start = (bf16[3,2176]{1,0:T(4,128)(2,1)S(1)}, bf16[3,2176]{1,0:T(4,128)(2,1)S(1)}, u32[]{:S(2)}, u32[]{:S(2)}) collective-permute-start(bf16[3,2176]{1,0:T(4,128)(2,1)S(1)} %pad_maximum_fusion.13), channel_id=1, source_target_pairs={{0,4},{4,8},{8,12},{1,5},{5,9},{9,13},{2,6},{6,10},{10,14},{3,7},{... | collective-permute-start | bytes 39176 | tf_op jit(solution)/shard_map/ppermute | solution.py:25
  19.5 6.3 %copy-start.2 = (bf16[512,16,128]{0,2,1:T(8,128)(2,1)S(1)}, bf16[512,16,128]{0,2,1:T(8,128)(2,1)}, u32[]{:S(2)}) copy-start(bf16[512,16,128]{0,2,1:T(8,128)(2,1)} %rev.9) | copy-start | bytes 6291460
  19.5 6.3 %copy-start.8 = (bf16[2048,1024]{1,0:T(8,128)(2,1)S(1)}, bf16[2048,1024]{1,0:T(8,128)(2,1)}, u32[]{:S(2)}) copy-start(bf16[2048,1024]{1,0:T(8,128)(2,1)} %param.18) | copy-start | bytes 12582916
  29.2 1.6 copy-start.6
  30.8 1.3 copy-start.24
  30.8 1.3 copy-start.15
  30.8 1.3 copy-start.21
  32.1 2.2 %copy-start.16 = (f32[4,1024]{1,0:T(4,128)S(1)}, f32[4,1024]{1,0:T(4,128)}, u32[]{:S(2)}) copy-start(f32[4,1024]{1,0:T(4,128)} %param.21) | copy-start | bytes 49156
  32.1 2.2 %copy-start.17 = (f32[4,512]{1,0:T(4,128)S(1)}, f32[4,512]{1,0:T(4,128)}, u32[]{:S(2)}) copy-start(f32[4,512]{1,0:T(4,128)} %param.23) | copy-start | bytes 24580
  32.5 5.2 %copy-start.14 = (f32[512,16]{0,1:T(8,128)}, f32[512,16]{0,1:T(8,128)S(1)}, u32[]{:S(2)}) copy-start(f32[512,16]{0,1:T(8,128)S(1)} %compare_select_fusion) | copy-start | bytes 98308
  32.6 3.7 %copy-start.22 = (f32[16]{0:T(128)S(1)}, f32[16]{0:T(128)}, u32[]{:S(2)}) copy-start(f32[16]{0:T(128)} %param.27) | copy-start | bytes 196
  35.3 8.5 %copy-start.13 = (f32[512,2,8]{0,2,1:T(8,128)}, f32[512,2,8]{0,2,1:T(8,128)S(1)}, u32[]{:S(2)}) copy-start(f32[512,2,8]{0,2,1:T(8,128)S(1)} %reshape_reshape.7) | copy-start | bytes 98308
  37.7 6.1 %copy-start.12 = (f32[512,2,8]{0,2,1:T(8,128)}, f32[512,2,8]{0,2,1:T(8,128)S(1)}, u32[]{:S(2)}) copy-start(f32[512,2,8]{0,2,1:T(8,128)S(1)} %reshape_reshape.6) | copy-start | bytes 98308
  39.7 4.3 %copy-start.10 = (bf16[512,1024]{0,1:T(8,128)(2,1)S(1)}, bf16[512,1024]{0,1:T(8,128)(2,1)}, u32[]{:S(2)}) copy-start(bf16[512,1024]{0,1:T(8,128)(2,1)} %multiply_convert_fusion.3) | copy-start | bytes 3145732
  39.7 4.3 %copy-start.11 = (bf16[512,1024]{0,1:T(8,128)(2,1)S(1)}, bf16[512,1024]{0,1:T(8,128)(2,1)}, u32[]{:S(2)}) copy-start(bf16[512,1024]{0,1:T(8,128)(2,1)} %multiply_convert_fusion.1) | copy-start | bytes 3145732
  39.7 4.3 %copy-start.18 = (f32[1024]{0:T(1024)S(1)}, f32[1024]{0:T(1024)}, u32[]{:S(2)}) copy-start(f32[1024]{0:T(1024)} %param.22) | copy-start | bytes 12292
  44.0 5.6 %copy-start.20 = (f32[512]{0:T(512)S(1)}, f32[512]{0:T(512)}, u32[]{:S(2)}) copy-start(f32[512]{0:T(512)} %param.24) | copy-start | bytes 6148
  59.4 23.3 %collective-permute-start.4 = (bf16[16,8448]{1,0:T(8,128)(2,1)}, bf16[16,8448]{1,0:T(8,128)(2,1)S(1)}, u32[]{:S(2)}, u32[]{:S(2)}) collective-permute-start(bf16[16,8448]{1,0:T(8,128)(2,1)} %pad_maximum_fusion.8), channel_id=1, source_target_pairs={{4,0},{8,4},{12,8},{5,1},{9,5},{13,9},{6,2},{10,6},{14,10},{7,3},{... | collective-permute-start | bytes 811016 | tf_op jit(solution)/shard_map/ppermute | solution.py:25
  72.5 12.7 %collective-permute-start.2 = (bf16[16,8448]{1,0:T(8,128)(2,1)S(1)}, bf16[16,8448]{1,0:T(8,128)(2,1)S(1)}, u32[]{:S(2)}, u32[]{:S(2)}) collective-permute-start(bf16[16,8448]{1,0:T(8,128)(2,1)S(1)} %pad_maximum_fusion.6), channel_id=1, source_target_pairs={{0,4},{4,8},{8,12},{1,5},{5,9},{9,13},{2,6},{6,10},{10,14},{3,7},{... | collective-permute-start | bytes 811016 | tf_op jit(solution)/shard_map/ppermute | solution.py:25
  83.2 12.8 %copy-start.5 = (f32[4,16,64,128]{3,2,1,0:T(8,128)S(1)}, f32[4,16,64,128]{3,2,1,0:T(8,128)}, u32[]{:S(2)}) copy-start(f32[4,16,64,128]{3,2,1,0:T(8,128)} %shard_map.149) | copy-start | bytes 6291460
  84.0 10.8 %collective-permute-start.5 = (bf16[16,8448]{1,0:T(8,128)(2,1)}, bf16[16,8448]{1,0:T(8,128)(2,1)}, u32[]{:S(2)}, u32[]{:S(2)}) collective-permute-start(bf16[16,8448]{1,0:T(8,128)(2,1)} %pad_maximum_fusion.9), channel_id=1, source_target_pairs={{8,0},{12,4},{9,1},{13,5},{10,2},{14,6},{11,3},{15,7},{24,16},{28,... | collective-permute-start | bytes 811016 | tf_op jit(solution)/shard_map/ppermute | solution.py:25
  85.8 25.2 %collective-permute-start.3 = (bf16[16,8448]{1,0:T(8,128)(2,1)S(1)}, bf16[16,8448]{1,0:T(8,128)(2,1)S(1)}, u32[]{:S(2)}, u32[]{:S(2)}) collective-permute-start(bf16[16,8448]{1,0:T(8,128)(2,1)S(1)} %pad_maximum_fusion.7), channel_id=1, source_target_pairs={{0,8},{4,12},{1,9},{5,13},{2,10},{6,14},{3,11},{7,15},{16,24},{20,... | collective-permute-start | bytes 811016 | tf_op jit(solution)/shard_map/ppermute | solution.py:25
  97.8 6.1 %copy-start.3 = (bf16[512,16,128]{0,2,1:T(8,128)(2,1)S(1)}, bf16[512,16,128]{0,2,1:T(8,128)(2,1)}, u32[]{:S(2)}) copy-start(bf16[512,16,128]{0,2,1:T(8,128)(2,1)} %rev.9) | copy-start | bytes 6291460
  110.9 1.6 copy-start.4
  114.3 6.2 %copy-start.7 = (bf16[512,2048]{1,0:T(8,128)(2,1)S(1)}, bf16[512,2048]{1,0:T(8,128)(2,1)}, u32[]{:S(2)}) copy-start(bf16[512,2048]{1,0:T(8,128)(2,1)} %param.15) | copy-start | bytes 6291460
  120.5 5.9 %copy-start.9 = (f32[512,1024]{0,1:T(8,128)S(1)}, f32[512,1024]{0,1:T(8,128)}, u32[]{:S(2)}) copy-start(f32[512,1024]{0,1:T(8,128)} %get-tuple-element.85) | copy-start | bytes 6291460
  120.5 5.9 %copy-start.19 = (f32[1024]{0:T(1024)S(1)}, f32[1024]{0:T(1024)}, u32[]{:S(2)}) copy-start(f32[1024]{0:T(1024)} %param.28) | copy-start | bytes 12292
  126.4 2.2 %copy-start.23 = (bf16[1024,2048]{1,0:T(8,128)(2,1)S(1)}, bf16[1024,2048]{1,0:T(8,128)(2,1)}, u32[]{:S(2)}) copy-start(bf16[1024,2048]{1,0:T(8,128)(2,1)} %param.29) | copy-start | bytes 12582916
  131.0 46.1 %copy-start.1 = (bf16[2048,512]{1,0:T(8,128)(2,1)S(1)}, bf16[2048,512]{1,0:T(8,128)(2,1)}, u32[]{:S(2)}) copy-start(bf16[2048,512]{1,0:T(8,128)(2,1)} %param.19) | copy-start | bytes 6291460
Sparse Core Ops, SparseCore 0:
  132.7 44.3 reduce-scatter.1

commit v9 on v8

--- a/solution.py
+++ b/solution.py
@@ -163,12 +163,9 @@
             c_blk = c_ref[cols, :]
             for j in range(per_group):
                 lo_row, hi_row = j * P_SIZE, (j + 1) * P_SIZE
-                s_j = s_ref[b, j]
-                s_hi = s_j.astype(BF16)
-                s_lo = (s_j - s_hi.astype(F32)).astype(BF16)
                 inter = lax.dot_general(
-                    s_hi, c_blk, dims, preferred_element_type=F32
-                ) + lax.dot_general(s_lo, c_blk, dims, preferred_element_type=F32)
+                    s_ref[b, j].astype(BF16), c_blk, dims, preferred_element_type=F32
+                )
                 inter = inter * jnp.exp(at_ref[0, j : j + 1, cols])
                 o_ref[lo_row:hi_row, cols] = (
                     y_ref[lo_row:hi_row, cols]

time: 185 us -> 182 us (0.984)
  Pallas kernels: 29.5 us -> 26.8 us
    pallas_call x2, Pallas kernels: 12.3 us -> 9.48 us  [block_finish(): pl.pallas_call(kernel, grid=(groups,), in_specs=[pl.BlockSpec((width_g, r...]
  transfers between devices with their start and end apart: 7 -> 7, of which waited for: 2 -> 2; matrix products, arithmetic and copies ran while one was open for 22% -> 22% of each run, Pallas kernels for 11% -> 10%
where the time goes in v9:
time: 182 us; the launch traced here: 181 us
  waiting for transfers between devices  48.3 us (27%)
  matrix products  37.9 us (21%)
  Pallas kernels  26.8 us (15%)
  other arithmetic  19.2 us (11%)
  local copies, waits for them, and re-layouts  17.7 us (10%)
  starting transfers between devices  17.3 us (10%)
  between operations  14 us (8%)
    reduce_scatter x1, waiting for transfers between devices, on_device(): summed = lax.psum_scatter(partial, 'chan', scatter_dimension=0, tiled=True)  44.5 us
    ppermute x6, starting transfers between devices, shifted(): return lax.ppermute(value, axis, pairs)  17.3 us
    dot_general x2, matrix products, project(): gate_in = jnp.dot(source, w_gate, preferred_element_type=F32).astype(BF16)  12.9 us
    pallas_call x2, Pallas kernels, block_intra(): pl.pallas_call(kernel, grid=(groups,), in_specs=[pl.BlockSpec((rows, N),...  10.1 us
    dot_general x2, matrix products, project(): jnp.dot(source, w_values, preferred_element_type=F32) * known[:, None]  9.7 us
    pallas_call x2, Pallas kernels, block_finish(): pl.pallas_call(kernel, grid=(groups,), in_specs=[pl.BlockSpec((width_g, r...  9.48 us
    pallas_call x2, Pallas kernels, block_states(): pl.pallas_call(kernel, grid=(groups,), in_specs=[pl.BlockSpec((rows, N),...  7.16 us
    transpose x1, other arithmetic, local_scan(): values_t = values_c.T  5.59 us
  transfers between devices with their start and end apart: 7, of which 2 were waited for; matrix products, arithmetic and copies ran while one was open for 22% of the time, Pallas kernels for 10%

profile of v9, /device:TPU:0, one launch (start us, length us, event | category | flops | bytes accessed | tf_op | source)
XLA Modules:
  0.0 181.2 jit_solution(5909969517810281910)
XLA Ops:
  6.5 0.8 compare_select_fusion.2
  7.5 0.8 fusion.72
  8.3 1.3 collective-permute-start.1
  9.7 3.0 %collective-permute-start = (bf16[3,2176]{1,0:T(4,128)(2,1)S(1)}, bf16[3,2176]{1,0:T(4,128)(2,1)S(1)}, u32[]{:S(2)}, u32[]{:S(2)}) collective-permute-start(bf16[3,2176]{1,0:T(4,128)(2,1)S(1)} %pad_maximum_fusion.13), channel_id=1, source_target_pairs={{0,4},{4,8},{8,12},{1,5},{5,9},{9,13},{2,6},{6,10},{10,14},{3,7},{... | collective-permute-start | bytes 39176 | tf_op jit(solution)/shard_map/ppermute | solution.py:25
  12.8 3.6 %convert_bitcast_fusion = bf16[512,16,128]{0,2,1:T(8,128)(2,1)} fusion(bf16[512,2048]{1,0:T(8,128)(2,1)} %param.15), kind=kOutput, calls=%fused_computation.30 | convolution fusion | flops 269516800 | bytes 4194304 | tf_op jit(solution)/shard_map/rki,ij->rkj/dot_general | solution.py:231
  16.4 3.1 %rev.9 = bf16[512,16,128]{0,2,1:T(8,128)(2,1)} reverse(bf16[512,16,128]{0,2,1:T(8,128)(2,1)} %convert_bitcast_fusion), dimensions={1} | reverse | bytes 4194304 | tf_op jit(solution)/shard_map/jit(_flip)/rev | solution.py:234
  19.5 6.3 %multiply_convert_fusion.3 = bf16[512,1024]{0,1:T(8,128)(2,1)} fusion(bf16[512,2048]{1,0:T(8,128)(2,1)} %param.15, bf16[2048,1024]{1,0:T(8,128)(2,1)} %param.18, f32[512]{0:T(512)S(1)} %get-tuple-element.63), kind=kOutput, calls=%fused_computation.32 | convolution fusion | flops 2148532224 | bytes 7342080 | tf_op jit(solution)/shard_map/dot_general | solution.py:253
  25.8 3.4 %multiply_convert_fusion.1 = bf16[512,1024]{0,1:T(8,128)(2,1)} fusion(bf16[512,2048]{0,1:T(8,128)(2,1)S(1)} %bitcast.231, bf16[2048,1024]{1,0:T(8,128)(2,1)S(1)} %copy-done.8, f32[512]{0:T(512)S(1)} %get-tuple-element.63), kind=kOutput, calls=%fused_computation.29 | convolution fusion | flops 2148532224 | bytes 7342080 | tf_op jit(solution)/shard_map/dot_general | solution.py:253
  29.2 1.3 convolution_convert_fusion.3
  30.8 1.3 convolution_convert_fusion.4
  32.1 0.4 compare_select_fusion
  32.6 1.3 broadcast_multiply_fusion.1
  35.3 1.0 copy.121.a_ref
  36.4 1.3 broadcast_in_dim_reshape.5.k_ref
  37.7 1.0 copy.112.a_ref
  39.3 0.4 convolution_convert_fusion.8
  39.7 4.1 %fusion.17 = bf16[6,1024]{0,1:T(8,128)(2,1)S(1)} fusion(bf16[2048,1024]{1,0:T(8,128)(2,1)} %param.18, f32[6]{0:T(128)S(1)} %maximum_convert_fusion, bf16[3,2048]{1,0:T(4,128)(2,1)S(1)} %bitcast.262, bf16[3,2048]{1,0:T(4,128)(2,1)S(1)} %slice.267), kind=kOutput, calls=%fused_computation.46 | convolution fusion | flops 25227264 | bytes 4231192 | tf_op jit(solution)/shard_map/dot_general | solution.py:247
  44.0 5.6 %fusion.26 = (bf16[1024,512]{1,0:T(8,128)(2,1)}, bf16[1024,512]{1,0:T(8,128)(2,1)}) fusion(bf16[512,1024]{0,1:T(8,128)(2,1)S(1)} %copy-done.10, f32[1024]{0:T(1024)S(1)} %bitcast.266, bf16[3,1024]{0,1:T(8,128)(2,1)S(1)} %get-tuple-element.45, f32[1024]{0:T(1024)S(1)} %bitcast.267, f32[1024]{0:T(1024)S(1)} %bitcast.265, f32[1024]{0:T(1024)S(1)} %bitcast.264, ...), kind=kLoop, calls=%fused_computation.65 | loop fusion | flops 27262976 | bytes 4227072 | tf_op jit(solution)/shard_map/transpose | solution.py:284
  49.6 2.4 %multiply_convert_fusion.5 = (bf16[512,512]{1,0:T(8,128)(2,1)}, bf16[512,512]{1,0:T(8,128)(2,1)}) fusion(bf16[512,512]{1,0:T(8,128)(2,1)S(1)} %convolution_convert_fusion.4, bf16[3,512]{1,0:T(4,128)(2,1)S(1)} %get-tuple-element.55, f32[512]{0:T(512)S(1)} %bitcast.270, f32[512]{0:T(512)S(1)} %bitcast.271, f32[512]{0:T(512)S(1)} %bitcast.269, ...), kind=kLoop, calls=%fused_computation.64 | loop fusion | flops 13631488 | bytes 2113536 | tf_op jit(solution)/shard_map/convert_element_type | solution.py:199
  52.0 3.6 %shard_map.149 = f32[4,16,64,128]{3,2,1,0:T(8,128)} custom-call(bf16[512,512]{1,0:T(8,128)(2,1)} %get-tuple-element.54.c_ref.b_ref, bf16[1024,512]{1,0:T(8,128)(2,1)} %get-tuple-element.48.xt_ref, f32[2,8,512]{2,1,0:T(8,128)} %bitcast.254, f32[2,8,512]{2,1,0:T(8,128)} %bitcast.257), custom_call_target="tpu_custom_call" | custom-call | tf_op jit(solution)/shard_map/pallas_call | solution.py:95
  55.5 1.7 fusion.71
  57.3 1.3 fusion.69
  58.7 0.7 pad_maximum_fusion.8
  59.4 1.3 collective-permute-start.4
  60.7 3.6 %shard_map.146 = f32[4,16,64,128]{3,2,1,0:T(8,128)} custom-call(bf16[512,512]{1,0:T(8,128)(2,1)} %get-tuple-element.53.c_ref.b_ref, bf16[1024,512]{1,0:T(8,128)(2,1)} %get-tuple-element.47.xt_ref, f32[2,8,512]{2,1,0:T(8,128)} %bitcast.250, f32[2,8,512]{2,1,0:T(8,128)} %bitcast.259), custom_call_target="tpu_custom_call" | custom-call | tf_op jit(solution)/shard_map/pallas_call | solution.py:95
  64.3 1.7 fusion.70
  66.0 1.3 fusion.68
  67.5 5.1 %shard_map.148.y_ref = f32[1024,512]{1,0:T(8,128)} custom-call(bf16[512,512]{1,0:T(8,128)(2,1)} %get-tuple-element.54.c_ref.b_ref, bf16[512,512]{1,0:T(8,128)(2,1)} %get-tuple-element.54.c_ref.b_ref, bf16[1024,512]{1,0:T(8,128)(2,1)} %get-tuple-element.48.xt_ref, f32[2,512,8]{2,1,0:T(8,128)} %copy.121.a_ref, f32[2,8,512]{2,1,0:T(8,128)} %bitcast.255, ...), custom_call_target="tpu_custom_call" | custom-call | tf_op jit(solution)/shard_map/pallas_call | solution.py:136
  72.5 5.1 %collective-permute-start.2 = (bf16[16,8448]{1,0:T(8,128)(2,1)S(1)}, bf16[16,8448]{1,0:T(8,128)(2,1)S(1)}, u32[]{:S(2)}, u32[]{:S(2)}) collective-permute-start(bf16[16,8448]{1,0:T(8,128)(2,1)S(1)} %pad_maximum_fusion.6), channel_id=1, source_target_pairs={{0,4},{4,8},{8,12},{1,5},{5,9},{9,13},{2,6},{6,10},{10,14},{3,7},{... | collective-permute-start | bytes 811016 | tf_op jit(solution)/shard_map/ppermute | solution.py:25
  77.6 5.1 %shard_map.145.y_ref = f32[1024,512]{1,0:T(8,128)} custom-call(bf16[512,512]{1,0:T(8,128)(2,1)} %get-tuple-element.53.c_ref.b_ref, bf16[512,512]{1,0:T(8,128)(2,1)} %get-tuple-element.53.c_ref.b_ref, bf16[1024,512]{1,0:T(8,128)(2,1)} %get-tuple-element.47.xt_ref, f32[2,512,8]{2,1,0:T(8,128)} %copy.112.a_ref, f32[2,8,512]{2,1,0:T(8,128)} %bitcast.251, ...), custom_call_target="tpu_custom_call" | custom-call | tf_op jit(solution)/shard_map/pallas_call | solution.py:136
  83.2 0.8 pad_maximum_fusion.9
  84.0 1.3 collective-permute-start.5
  85.8 5.3 %collective-permute-start.3 = (bf16[16,8448]{1,0:T(8,128)(2,1)S(1)}, bf16[16,8448]{1,0:T(8,128)(2,1)S(1)}, u32[]{:S(2)}, u32[]{:S(2)}) collective-permute-start(bf16[16,8448]{1,0:T(8,128)(2,1)S(1)} %pad_maximum_fusion.7), channel_id=1, source_target_pairs={{0,8},{4,12},{1,9},{5,13},{2,10},{6,14},{3,11},{7,15},{16,24},{20,... | collective-permute-start | bytes 811016 | tf_op jit(solution)/shard_map/ppermute | solution.py:25
  91.1 3.7 %collective-permute-done.5 = bf16[16,8448]{1,0:T(8,128)(2,1)} collective-permute-done((bf16[16,8448]{1,0:T(8,128)(2,1)}, bf16[16,8448]{1,0:T(8,128)(2,1)}, u32[]{:S(2)}, u32[]{:S(2)}) %collective-permute-start.5) | collective-permute-done | bytes 270368 | tf_op jit(solution)/shard_map/ppermute | solution.py:25
  94.8 1.1 fusion.33
  96.0 0.3 multiply_add_fusion.2
  96.3 1.4 pad_maximum_fusion.1.s_ref
  97.8 4.7 %shard_map.150 = f32[1024,512]{1,0:T(8,128)} custom-call(f32[1024,512]{1,0:T(8,128)} %shard_map.148.y_ref, bf16[512,512]{1,0:T(8,128)(2,1)} %get-tuple-element.54.c_ref.b_ref, bf16[1024,512]{1,0:T(8,128)(2,1)} %get-tuple-element.48.xt_ref, f32[2,8,512]{2,1,0:T(8,128)} %bitcast.256, f32[4,16,64,128]{3,2,1,0:T(8,128)} %pad_maximum_fusion.1.s_ref, ...), custom_call_target="tpu_custom_call" | custom-call | tf_op jit(solution)/shard_map/pallas_call | solution.py:176
  102.5 7.1 %bitcast_reduce_fusion = (f32[512,2]{0,1:T(2,128)S(1)}, f32[512,1024]{0,1:T(8,128)}) fusion(bf16[512,2048]{0,1:T(8,128)(2,1)S(1)} %bitcast.234, bf16[2048,1024]{1,0:T(8,128)(2,1)} %param.17, f32[1024,512]{1,0:T(8,128)} %shard_map.150), kind=kOutput, calls=%fused_computation.22 | convolution fusion | flops 2152201216 | bytes 10489856 | tf_op jit(solution)/shard_map/dot_general | solution.py:252
  109.8 1.3 copy-done.4
  111.5 1.5 pad_maximum_fusion.s_ref
  112.9 4.8 %shard_map.147 = f32[1024,512]{1,0:T(8,128)} custom-call(f32[1024,512]{1,0:T(8,128)} %shard_map.145.y_ref, bf16[512,512]{1,0:T(8,128)(2,1)} %get-tuple-element.53.c_ref.b_ref, bf16[1024,512]{1,0:T(8,128)(2,1)} %get-tuple-element.47.xt_ref, f32[2,8,512]{2,1,0:T(8,128)} %bitcast.252, f32[4,16,64,128]{3,2,1,0:T(8,128)} %pad_maximum_fusion.s_ref, ...), custom_call_target="tpu_custom_call" | custom-call | tf_op jit(solution)/shard_map/pallas_call | solution.py:176
  117.7 5.8 %bitcast_reduce_fusion.1 = (f32[512,2]{0,1:T(2,128)S(1)}, f32[512,1024]{0,1:T(8,128)S(1)}) fusion(bf16[512,2048]{1,0:T(8,128)(2,1)S(1)} %copy-done.7, bf16[2048,1024]{1,0:T(8,128)(2,1)} %param.17, f32[1024,512]{1,0:T(8,128)} %shard_map.147), kind=kOutput, calls=%fused_computation.26 | convolution fusion | flops 2152201216 | bytes 10489856 | tf_op jit(solution)/shard_map/dot_general | solution.py:252
  123.6 0.4 fusion.14
  124.0 1.8 copy-done.23
  125.8 2.5 %convolution_convert_fusion = bf16[512,2048]{1,0:T(8,128)(2,1)S(1)} fusion(bf16[1024,2048]{1,0:T(8,128)(2,1)S(1)} %copy-done.23, bf16[512,1024]{0,1:T(8,128)(2,1)S(1)} %get-tuple-element.62, bf16[512,1024]{0,1:T(8,128)(2,1)S(1)} %get-tuple-element.61), kind=kOutput, calls=%fused_computation | convolution fusion | flops 2150629376 | bytes 8388608 | tf_op jit(solution)/shard_map/dot_general | solution.py:315
  128.3 1.5 copy.190
  129.8 44.5 %reduce-scatter.2.cloned.1.call-done = bf16[1,512,512]{2,1,0:T(8,128)(2,1)} async-done(((bf16[4,512,512]{2,1,0:T(8,128)(2,1)}), bf16[1,512,512]{2,1,0:T(8,128)(2,1)}) %reduce-scatter.2.cloned.1.call-update) | async-done | bytes 524304 | tf_op jit(solution)/shard_map/reduce_scatter | solution.py:317
  (116 shorter events, 4.7 us)
Async XLA Ops:
  6.5 22.7 %copy-start = (bf16[2048,512]{1,0:T(8,128)(2,1)S(1)}, bf16[2048,512]{1,0:T(8,128)(2,1)}, u32[]{:S(2)}) copy-start(bf16[2048,512]{1,0:T(8,128)(2,1)} %param.19) | copy-start | bytes 6291460
  6.5 167.8 %reduce-scatter.2.cloned.1.call-start = ((), (), s32[]{:S(2)}) async-start(), calls=%async_computation.1 | async-start | bytes 2621440 | tf_op jit(solution)/shard_map/reduce_scatter | solution.py:317
  8.3 30.4 %collective-permute-start.1 = (bf16[3,2176]{1,0:T(4,128)(2,1)S(1)}, bf16[3,2176]{1,0:T(4,128)(2,1)S(1)}, u32[]{:S(2)}, u32[]{:S(2)}) collective-permute-start(bf16[3,2176]{1,0:T(4,128)(2,1)S(1)} %pad_maximum_fusion.14), channel_id=1, source_target_pairs={{4,0},{8,4},{12,8},{5,1},{9,5},{13,9},{6,2},{10,6},{14,10},{7,3},{... | collective-permute-start | bytes 39176 | tf_op jit(solution)/shard_map/ppermute | solution.py:25
  9.7 29.4 %collective-permute-start = (bf16[3,2176]{1,0:T(4,128)(2,1)S(1)}, bf16[3,2176]{1,0:T(4,128)(2,1)S(1)}, u32[]{:S(2)}, u32[]{:S(2)}) collective-permute-start(bf16[3,2176]{1,0:T(4,128)(2,1)S(1)} %pad_maximum_fusion.13), channel_id=1, source_target_pairs={{0,4},{4,8},{8,12},{1,5},{5,9},{9,13},{2,6},{6,10},{10,14},{3,7},{... | collective-permute-start | bytes 39176 | tf_op jit(solution)/shard_map/ppermute | solution.py:25
  19.5 6.3 %copy-start.2 = (bf16[512,16,128]{0,2,1:T(8,128)(2,1)S(1)}, bf16[512,16,128]{0,2,1:T(8,128)(2,1)}, u32[]{:S(2)}) copy-start(bf16[512,16,128]{0,2,1:T(8,128)(2,1)} %rev.9) | copy-start | bytes 6291460
  19.5 6.3 %copy-start.8 = (bf16[2048,1024]{1,0:T(8,128)(2,1)S(1)}, bf16[2048,1024]{1,0:T(8,128)(2,1)}, u32[]{:S(2)}) copy-start(bf16[2048,1024]{1,0:T(8,128)(2,1)} %param.18) | copy-start | bytes 12582916
  29.2 1.6 copy-start.6
  30.8 1.3 copy-start.24
  30.8 1.3 copy-start.15
  30.8 1.3 copy-start.21
  32.1 2.2 %copy-start.16 = (f32[4,1024]{1,0:T(4,128)S(1)}, f32[4,1024]{1,0:T(4,128)}, u32[]{:S(2)}) copy-start(f32[4,1024]{1,0:T(4,128)} %param.21) | copy-start | bytes 49156
  32.1 2.2 %copy-start.17 = (f32[4,512]{1,0:T(4,128)S(1)}, f32[4,512]{1,0:T(4,128)}, u32[]{:S(2)}) copy-start(f32[4,512]{1,0:T(4,128)} %param.23) | copy-start | bytes 24580
  32.5 5.2 %copy-start.14 = (f32[512,16]{0,1:T(8,128)}, f32[512,16]{0,1:T(8,128)S(1)}, u32[]{:S(2)}) copy-start(f32[512,16]{0,1:T(8,128)S(1)} %compare_select_fusion) | copy-start | bytes 98308
  32.6 3.7 %copy-start.22 = (f32[16]{0:T(128)S(1)}, f32[16]{0:T(128)}, u32[]{:S(2)}) copy-start(f32[16]{0:T(128)} %param.27) | copy-start | bytes 196
  35.3 8.5 %copy-start.13 = (f32[512,2,8]{0,2,1:T(8,128)}, f32[512,2,8]{0,2,1:T(8,128)S(1)}, u32[]{:S(2)}) copy-start(f32[512,2,8]{0,2,1:T(8,128)S(1)} %reshape_reshape.7) | copy-start | bytes 98308
  37.7 6.1 %copy-start.12 = (f32[512,2,8]{0,2,1:T(8,128)}, f32[512,2,8]{0,2,1:T(8,128)S(1)}, u32[]{:S(2)}) copy-start(f32[512,2,8]{0,2,1:T(8,128)S(1)} %reshape_reshape.6) | copy-start | bytes 98308
  39.7 4.3 %copy-start.10 = (bf16[512,1024]{0,1:T(8,128)(2,1)S(1)}, bf16[512,1024]{0,1:T(8,128)(2,1)}, u32[]{:S(2)}) copy-start(bf16[512,1024]{0,1:T(8,128)(2,1)} %multiply_convert_fusion.3) | copy-start | bytes 3145732
  39.7 4.3 %copy-start.11 = (bf16[512,1024]{0,1:T(8,128)(2,1)S(1)}, bf16[512,1024]{0,1:T(8,128)(2,1)}, u32[]{:S(2)}) copy-start(bf16[512,1024]{0,1:T(8,128)(2,1)} %multiply_convert_fusion.1) | copy-start | bytes 3145732
  39.7 4.3 %copy-start.18 = (f32[1024]{0:T(1024)S(1)}, f32[1024]{0:T(1024)}, u32[]{:S(2)}) copy-start(f32[1024]{0:T(1024)} %param.22) | copy-start | bytes 12292
  44.0 5.6 %copy-start.20 = (f32[512]{0:T(512)S(1)}, f32[512]{0:T(512)}, u32[]{:S(2)}) copy-start(f32[512]{0:T(512)} %param.24) | copy-start | bytes 6148
  59.4 23.3 %collective-permute-start.4 = (bf16[16,8448]{1,0:T(8,128)(2,1)}, bf16[16,8448]{1,0:T(8,128)(2,1)S(1)}, u32[]{:S(2)}, u32[]{:S(2)}) collective-permute-start(bf16[16,8448]{1,0:T(8,128)(2,1)} %pad_maximum_fusion.8), channel_id=1, source_target_pairs={{4,0},{8,4},{12,8},{5,1},{9,5},{13,9},{6,2},{10,6},{14,10},{7,3},{... | collective-permute-start | bytes 811016 | tf_op jit(solution)/shard_map/ppermute | solution.py:25
  72.5 12.7 %collective-permute-start.2 = (bf16[16,8448]{1,0:T(8,128)(2,1)S(1)}, bf16[16,8448]{1,0:T(8,128)(2,1)S(1)}, u32[]{:S(2)}, u32[]{:S(2)}) collective-permute-start(bf16[16,8448]{1,0:T(8,128)(2,1)S(1)} %pad_maximum_fusion.6), channel_id=1, source_target_pairs={{0,4},{4,8},{8,12},{1,5},{5,9},{9,13},{2,6},{6,10},{10,14},{3,7},{... | collective-permute-start | bytes 811016 | tf_op jit(solution)/shard_map/ppermute | solution.py:25
  83.2 12.8 %copy-start.5 = (f32[4,16,64,128]{3,2,1,0:T(8,128)S(1)}, f32[4,16,64,128]{3,2,1,0:T(8,128)}, u32[]{:S(2)}) copy-start(f32[4,16,64,128]{3,2,1,0:T(8,128)} %shard_map.149) | copy-start | bytes 6291460
  84.0 10.8 %collective-permute-start.5 = (bf16[16,8448]{1,0:T(8,128)(2,1)}, bf16[16,8448]{1,0:T(8,128)(2,1)}, u32[]{:S(2)}, u32[]{:S(2)}) collective-permute-start(bf16[16,8448]{1,0:T(8,128)(2,1)} %pad_maximum_fusion.9), channel_id=1, source_target_pairs={{8,0},{12,4},{9,1},{13,5},{10,2},{14,6},{11,3},{15,7},{24,16},{28,... | collective-permute-start | bytes 811016 | tf_op jit(solution)/shard_map/ppermute | solution.py:25
  85.8 23.8 %collective-permute-start.3 = (bf16[16,8448]{1,0:T(8,128)(2,1)S(1)}, bf16[16,8448]{1,0:T(8,128)(2,1)S(1)}, u32[]{:S(2)}, u32[]{:S(2)}) collective-permute-start(bf16[16,8448]{1,0:T(8,128)(2,1)S(1)} %pad_maximum_fusion.7), channel_id=1, source_target_pairs={{0,8},{4,12},{1,9},{5,13},{2,10},{6,14},{3,11},{7,15},{16,24},{20,... | collective-permute-start | bytes 811016 | tf_op jit(solution)/shard_map/ppermute | solution.py:25
  97.8 4.7 %copy-start.3 = (bf16[512,16,128]{0,2,1:T(8,128)(2,1)S(1)}, bf16[512,16,128]{0,2,1:T(8,128)(2,1)}, u32[]{:S(2)}) copy-start(bf16[512,16,128]{0,2,1:T(8,128)(2,1)} %rev.9) | copy-start | bytes 6291460
  109.6 1.6 copy-start.4
  112.9 4.8 %copy-start.7 = (bf16[512,2048]{1,0:T(8,128)(2,1)S(1)}, bf16[512,2048]{1,0:T(8,128)(2,1)}, u32[]{:S(2)}) copy-start(bf16[512,2048]{1,0:T(8,128)(2,1)} %param.15) | copy-start | bytes 6291460
  117.7 5.9 %copy-start.9 = (f32[512,1024]{0,1:T(8,128)S(1)}, f32[512,1024]{0,1:T(8,128)}, u32[]{:S(2)}) copy-start(f32[512,1024]{0,1:T(8,128)} %get-tuple-element.85) | copy-start | bytes 6291460
  117.7 5.9 %copy-start.19 = (f32[1024]{0:T(1024)S(1)}, f32[1024]{0:T(1024)}, u32[]{:S(2)}) copy-start(f32[1024]{0:T(1024)} %param.28) | copy-start | bytes 12292
  123.6 2.2 %copy-start.23 = (bf16[1024,2048]{1,0:T(8,128)(2,1)S(1)}, bf16[1024,2048]{1,0:T(8,128)(2,1)}, u32[]{:S(2)}) copy-start(bf16[1024,2048]{1,0:T(8,128)(2,1)} %param.29) | copy-start | bytes 12582916
  128.3 46.1 %copy-start.1 = (bf16[2048,512]{1,0:T(8,128)(2,1)S(1)}, bf16[2048,512]{1,0:T(8,128)(2,1)}, u32[]{:S(2)}) copy-start(bf16[2048,512]{1,0:T(8,128)(2,1)} %param.19) | copy-start | bytes 6291460
Sparse Core Ops, SparseCore 0:
  129.9 44.3 reduce-scatter.1

commit v10 on v9

--- a/solution.py
+++ b/solution.py
@@ -86,11 +86,7 @@
             a_end = a_row[:, Q - 1 : Q] if forward else a_row[:, 0:1]
             xt_j = xt_ref[j * P_SIZE : (j + 1) * P_SIZE, cols]
             tx = (jnp.exp(a_end - a_row) * d_row) * xt_j.astype(F32)
-            t_hi = tx.astype(BF16)
-            t_lo = (tx - t_hi.astype(F32)).astype(BF16)
-            s_ref[blk, j] = jnp.dot(t_hi, b_blk, preferred_element_type=F32) + jnp.dot(
-                t_lo, b_blk, preferred_element_type=F32
-            )
+            s_ref[blk, j] = jnp.dot(tx.astype(BF16), b_blk, preferred_element_type=F32)
 
     return pl.pallas_call(
         kernel,

time: 182 us -> 181 us (level)
  transfers between devices with their start and end apart: 7 -> 7, of which waited for: 2 -> 2; matrix products, arithmetic and copies ran while one was open for 22% -> 23% of each run, Pallas kernels for 10% -> 10%
where the time goes in v10:
time: 181 us; the launch traced here: 180 us
  waiting for transfers between devices  48.3 us (27%)
  matrix products  37.9 us (21%)
  Pallas kernels  25.7 us (14%)
  other arithmetic  19.2 us (11%)
  local copies, waits for them, and re-layouts  17.7 us (10%)
  starting transfers between devices  17.3 us (10%)
  between operations  14 us (8%)
    reduce_scatter x1, waiting for transfers between devices, on_device(): summed = lax.psum_scatter(partial, 'chan', scatter_dimension=0, tiled=True)  44.5 us
    ppermute x6, starting transfers between devices, shifted(): return lax.ppermute(value, axis, pairs)  17.3 us
    dot_general x2, matrix products, project(): gate_in = jnp.dot(source, w_gate, preferred_element_type=F32).astype(BF16)  12.9 us
    pallas_call x2, Pallas kernels, block_intra(): pl.pallas_call(kernel, grid=(groups,), in_specs=[pl.BlockSpec((rows, N),...  10.1 us
    dot_general x2, matrix products, project(): jnp.dot(source, w_values, preferred_element_type=F32) * known[:, None]  9.7 us
    pallas_call x2, Pallas kernels, block_finish(): pl.pallas_call(kernel, grid=(groups,), in_specs=[pl.BlockSpec((width_g, r...  9.48 us
    pallas_call x2, Pallas kernels, block_states(): pl.pallas_call(kernel, grid=(groups,), in_specs=[pl.BlockSpec((rows, N),...  6.08 us
    transpose x1, other arithmetic, local_scan(): values_t = values_c.T  5.59 us
  transfers between devices with their start and end apart: 7, of which 2 were waited for; matrix products, arithmetic and copies ran while one was open for 23% of the time, Pallas kernels for 10%

profile of v10, /device:TPU:0, one launch (start us, length us, event | category | flops | bytes accessed | tf_op | source)
XLA Modules:
  0.0 180.1 jit_solution(6057468196460182405)
XLA Ops:
  6.5 0.8 compare_select_fusion.2
  7.5 0.8 fusion.72
  8.3 1.3 collective-permute-start.1
  9.7 3.0 %collective-permute-start = (bf16[3,2176]{1,0:T(4,128)(2,1)S(1)}, bf16[3,2176]{1,0:T(4,128)(2,1)S(1)}, u32[]{:S(2)}, u32[]{:S(2)}) collective-permute-start(bf16[3,2176]{1,0:T(4,128)(2,1)S(1)} %pad_maximum_fusion.13), channel_id=1, source_target_pairs={{0,4},{4,8},{8,12},{1,5},{5,9},{9,13},{2,6},{6,10},{10,14},{3,7},{... | collective-permute-start | bytes 39176 | tf_op jit(solution)/shard_map/ppermute | solution.py:25
  12.8 3.6 %convert_bitcast_fusion = bf16[512,16,128]{0,2,1:T(8,128)(2,1)} fusion(bf16[512,2048]{1,0:T(8,128)(2,1)} %param.15), kind=kOutput, calls=%fused_computation.30 | convolution fusion | flops 269516800 | bytes 4194304 | tf_op jit(solution)/shard_map/rki,ij->rkj/dot_general | solution.py:227
  16.4 3.1 %rev.9 = bf16[512,16,128]{0,2,1:T(8,128)(2,1)} reverse(bf16[512,16,128]{0,2,1:T(8,128)(2,1)} %convert_bitcast_fusion), dimensions={1} | reverse | bytes 4194304 | tf_op jit(solution)/shard_map/jit(_flip)/rev | solution.py:230
  19.5 6.3 %multiply_convert_fusion.3 = bf16[512,1024]{0,1:T(8,128)(2,1)} fusion(bf16[512,2048]{1,0:T(8,128)(2,1)} %param.15, bf16[2048,1024]{1,0:T(8,128)(2,1)} %param.18, f32[512]{0:T(512)S(1)} %get-tuple-element.63), kind=kOutput, calls=%fused_computation.32 | convolution fusion | flops 2148532224 | bytes 7342080 | tf_op jit(solution)/shard_map/dot_general | solution.py:249
  25.8 3.4 %multiply_convert_fusion.1 = bf16[512,1024]{0,1:T(8,128)(2,1)} fusion(bf16[512,2048]{0,1:T(8,128)(2,1)S(1)} %bitcast.231, bf16[2048,1024]{1,0:T(8,128)(2,1)S(1)} %copy-done.8, f32[512]{0:T(512)S(1)} %get-tuple-element.63), kind=kOutput, calls=%fused_computation.29 | convolution fusion | flops 2148532224 | bytes 7342080 | tf_op jit(solution)/shard_map/dot_general | solution.py:249
  29.2 1.3 convolution_convert_fusion.3
  30.8 1.3 convolution_convert_fusion.4
  32.1 0.4 compare_select_fusion
  32.6 1.3 broadcast_multiply_fusion.1
  35.3 1.0 copy.121.a_ref
  36.4 1.3 broadcast_in_dim_reshape.5.k_ref
  37.7 1.0 copy.112.a_ref
  39.3 0.4 convolution_convert_fusion.8
  39.7 4.1 %fusion.17 = bf16[6,1024]{0,1:T(8,128)(2,1)S(1)} fusion(bf16[2048,1024]{1,0:T(8,128)(2,1)} %param.18, f32[6]{0:T(128)S(1)} %maximum_convert_fusion, bf16[3,2048]{1,0:T(4,128)(2,1)S(1)} %bitcast.262, bf16[3,2048]{1,0:T(4,128)(2,1)S(1)} %slice.267), kind=kOutput, calls=%fused_computation.46 | convolution fusion | flops 25227264 | bytes 4231192 | tf_op jit(solution)/shard_map/dot_general | solution.py:243
  44.0 5.6 %fusion.26 = (bf16[1024,512]{1,0:T(8,128)(2,1)}, bf16[1024,512]{1,0:T(8,128)(2,1)}) fusion(bf16[512,1024]{0,1:T(8,128)(2,1)S(1)} %copy-done.10, f32[1024]{0:T(1024)S(1)} %bitcast.266, bf16[3,1024]{0,1:T(8,128)(2,1)S(1)} %get-tuple-element.45, f32[1024]{0:T(1024)S(1)} %bitcast.267, f32[1024]{0:T(1024)S(1)} %bitcast.265, f32[1024]{0:T(1024)S(1)} %bitcast.264, ...), kind=kLoop, calls=%fused_computation.65 | loop fusion | flops 27262976 | bytes 4227072 | tf_op jit(solution)/shard_map/transpose | solution.py:280
  49.6 2.4 %multiply_convert_fusion.5 = (bf16[512,512]{1,0:T(8,128)(2,1)}, bf16[512,512]{1,0:T(8,128)(2,1)}) fusion(bf16[512,512]{1,0:T(8,128)(2,1)S(1)} %convolution_convert_fusion.4, bf16[3,512]{1,0:T(4,128)(2,1)S(1)} %get-tuple-element.55, f32[512]{0:T(512)S(1)} %bitcast.270, f32[512]{0:T(512)S(1)} %bitcast.271, f32[512]{0:T(512)S(1)} %bitcast.269, ...), kind=kLoop, calls=%fused_computation.64 | loop fusion | flops 13631488 | bytes 2113536 | tf_op jit(solution)/shard_map/convert_element_type | solution.py:195
  52.0 3.0 %shard_map.149 = f32[4,16,64,128]{3,2,1,0:T(8,128)} custom-call(bf16[512,512]{1,0:T(8,128)(2,1)} %get-tuple-element.54.c_ref.b_ref, bf16[1024,512]{1,0:T(8,128)(2,1)} %get-tuple-element.48.xt_ref, f32[2,8,512]{2,1,0:T(8,128)} %bitcast.254, f32[2,8,512]{2,1,0:T(8,128)} %bitcast.257), custom_call_target="tpu_custom_call" | custom-call | tf_op jit(solution)/shard_map/pallas_call | solution.py:91
  55.0 1.7 fusion.71
  56.7 1.3 fusion.69
  58.2 0.7 pad_maximum_fusion.8
  58.9 1.3 collective-permute-start.4
  60.2 3.1 %shard_map.146 = f32[4,16,64,128]{3,2,1,0:T(8,128)} custom-call(bf16[512,512]{1,0:T(8,128)(2,1)} %get-tuple-element.53.c_ref.b_ref, bf16[1024,512]{1,0:T(8,128)(2,1)} %get-tuple-element.47.xt_ref, f32[2,8,512]{2,1,0:T(8,128)} %bitcast.250, f32[2,8,512]{2,1,0:T(8,128)} %bitcast.259), custom_call_target="tpu_custom_call" | custom-call | tf_op jit(solution)/shard_map/pallas_call | solution.py:91
  63.2 1.7 fusion.70
  65.0 1.3 fusion.68
  66.4 5.1 %shard_map.148.y_ref = f32[1024,512]{1,0:T(8,128)} custom-call(bf16[512,512]{1,0:T(8,128)(2,1)} %get-tuple-element.54.c_ref.b_ref, bf16[512,512]{1,0:T(8,128)(2,1)} %get-tuple-element.54.c_ref.b_ref, bf16[1024,512]{1,0:T(8,128)(2,1)} %get-tuple-element.48.xt_ref, f32[2,512,8]{2,1,0:T(8,128)} %copy.121.a_ref, f32[2,8,512]{2,1,0:T(8,128)} %bitcast.255, ...), custom_call_target="tpu_custom_call" | custom-call | tf_op jit(solution)/shard_map/pallas_call | solution.py:132
  71.5 5.1 %collective-permute-start.2 = (bf16[16,8448]{1,0:T(8,128)(2,1)S(1)}, bf16[16,8448]{1,0:T(8,128)(2,1)S(1)}, u32[]{:S(2)}, u32[]{:S(2)}) collective-permute-start(bf16[16,8448]{1,0:T(8,128)(2,1)S(1)} %pad_maximum_fusion.6), channel_id=1, source_target_pairs={{0,4},{4,8},{8,12},{1,5},{5,9},{9,13},{2,6},{6,10},{10,14},{3,7},{... | collective-permute-start | bytes 811016 | tf_op jit(solution)/shard_map/ppermute | solution.py:25
  76.6 5.1 %shard_map.145.y_ref = f32[1024,512]{1,0:T(8,128)} custom-call(bf16[512,512]{1,0:T(8,128)(2,1)} %get-tuple-element.53.c_ref.b_ref, bf16[512,512]{1,0:T(8,128)(2,1)} %get-tuple-element.53.c_ref.b_ref, bf16[1024,512]{1,0:T(8,128)(2,1)} %get-tuple-element.47.xt_ref, f32[2,512,8]{2,1,0:T(8,128)} %copy.112.a_ref, f32[2,8,512]{2,1,0:T(8,128)} %bitcast.251, ...), custom_call_target="tpu_custom_call" | custom-call | tf_op jit(solution)/shard_map/pallas_call | solution.py:132
  82.1 0.8 pad_maximum_fusion.9
  82.9 1.3 collective-permute-start.5
  84.7 5.3 %collective-permute-start.3 = (bf16[16,8448]{1,0:T(8,128)(2,1)S(1)}, bf16[16,8448]{1,0:T(8,128)(2,1)S(1)}, u32[]{:S(2)}, u32[]{:S(2)}) collective-permute-start(bf16[16,8448]{1,0:T(8,128)(2,1)S(1)} %pad_maximum_fusion.7), channel_id=1, source_target_pairs={{0,8},{4,12},{1,9},{5,13},{2,10},{6,14},{3,11},{7,15},{16,24},{20,... | collective-permute-start | bytes 811016 | tf_op jit(solution)/shard_map/ppermute | solution.py:25
  90.0 3.7 %collective-permute-done.5 = bf16[16,8448]{1,0:T(8,128)(2,1)} collective-permute-done((bf16[16,8448]{1,0:T(8,128)(2,1)}, bf16[16,8448]{1,0:T(8,128)(2,1)}, u32[]{:S(2)}, u32[]{:S(2)}) %collective-permute-start.5) | collective-permute-done | bytes 270368 | tf_op jit(solution)/shard_map/ppermute | solution.py:25
  93.7 1.1 fusion.33
  94.9 0.3 multiply_add_fusion.2
  95.3 1.4 pad_maximum_fusion.1.s_ref
  96.7 4.7 %shard_map.150 = f32[1024,512]{1,0:T(8,128)} custom-call(f32[1024,512]{1,0:T(8,128)} %shard_map.148.y_ref, bf16[512,512]{1,0:T(8,128)(2,1)} %get-tuple-element.54.c_ref.b_ref, bf16[1024,512]{1,0:T(8,128)(2,1)} %get-tuple-element.48.xt_ref, f32[2,8,512]{2,1,0:T(8,128)} %bitcast.256, f32[4,16,64,128]{3,2,1,0:T(8,128)} %pad_maximum_fusion.1.s_ref, ...), custom_call_target="tpu_custom_call" | custom-call | tf_op jit(solution)/shard_map/pallas_call | solution.py:172
  101.4 7.1 %bitcast_reduce_fusion = (f32[512,2]{0,1:T(2,128)S(1)}, f32[512,1024]{0,1:T(8,128)}) fusion(bf16[512,2048]{0,1:T(8,128)(2,1)S(1)} %bitcast.234, bf16[2048,1024]{1,0:T(8,128)(2,1)} %param.17, f32[1024,512]{1,0:T(8,128)} %shard_map.150), kind=kOutput, calls=%fused_computation.22 | convolution fusion | flops 2152201216 | bytes 10489856 | tf_op jit(solution)/shard_map/dot_general | solution.py:248
  108.8 1.3 copy-done.4
  110.4 1.5 pad_maximum_fusion.s_ref
  111.9 4.8 %shard_map.147 = f32[1024,512]{1,0:T(8,128)} custom-call(f32[1024,512]{1,0:T(8,128)} %shard_map.145.y_ref, bf16[512,512]{1,0:T(8,128)(2,1)} %get-tuple-element.53.c_ref.b_ref, bf16[1024,512]{1,0:T(8,128)(2,1)} %get-tuple-element.47.xt_ref, f32[2,8,512]{2,1,0:T(8,128)} %bitcast.252, f32[4,16,64,128]{3,2,1,0:T(8,128)} %pad_maximum_fusion.s_ref, ...), custom_call_target="tpu_custom_call" | custom-call | tf_op jit(solution)/shard_map/pallas_call | solution.py:172
  116.6 5.8 %bitcast_reduce_fusion.1 = (f32[512,2]{0,1:T(2,128)S(1)}, f32[512,1024]{0,1:T(8,128)S(1)}) fusion(bf16[512,2048]{1,0:T(8,128)(2,1)S(1)} %copy-done.7, bf16[2048,1024]{1,0:T(8,128)(2,1)} %param.17, f32[1024,512]{1,0:T(8,128)} %shard_map.147), kind=kOutput, calls=%fused_computation.26 | convolution fusion | flops 2152201216 | bytes 10489856 | tf_op jit(solution)/shard_map/dot_general | solution.py:248
  122.5 0.4 fusion.14
  122.9 1.8 copy-done.23
  124.7 2.5 %convolution_convert_fusion = bf16[512,2048]{1,0:T(8,128)(2,1)S(1)} fusion(bf16[1024,2048]{1,0:T(8,128)(2,1)S(1)} %copy-done.23, bf16[512,1024]{0,1:T(8,128)(2,1)S(1)} %get-tuple-element.62, bf16[512,1024]{0,1:T(8,128)(2,1)S(1)} %get-tuple-element.61), kind=kOutput, calls=%fused_computation | convolution fusion | flops 2150629376 | bytes 8388608 | tf_op jit(solution)/shard_map/dot_general | solution.py:311
  127.2 1.5 copy.190
  128.7 44.5 %reduce-scatter.2.cloned.1.call-done = bf16[1,512,512]{2,1,0:T(8,128)(2,1)} async-done(((bf16[4,512,512]{2,1,0:T(8,128)(2,1)}), bf16[1,512,512]{2,1,0:T(8,128)(2,1)}) %reduce-scatter.2.cloned.1.call-update) | async-done | bytes 524304 | tf_op jit(solution)/shard_map/reduce_scatter | solution.py:313
  (116 shorter events, 4.7 us)
Async XLA Ops:
  6.5 22.7 %copy-start = (bf16[2048,512]{1,0:T(8,128)(2,1)S(1)}, bf16[2048,512]{1,0:T(8,128)(2,1)}, u32[]{:S(2)}) copy-start(bf16[2048,512]{1,0:T(8,128)(2,1)} %param.19) | copy-start | bytes 6291460
  6.5 166.7 %reduce-scatter.2.cloned.1.call-start = ((), (), s32[]{:S(2)}) async-start(), calls=%async_computation.1 | async-start | bytes 2621440 | tf_op jit(solution)/shard_map/reduce_scatter | solution.py:313
  8.3 30.4 %collective-permute-start.1 = (bf16[3,2176]{1,0:T(4,128)(2,1)S(1)}, bf16[3,2176]{1,0:T(4,128)(2,1)S(1)}, u32[]{:S(2)}, u32[]{:S(2)}) collective-permute-start(bf16[3,2176]{1,0:T(4,128)(2,1)S(1)} %pad_maximum_fusion.14), channel_id=1, source_target_pairs={{4,0},{8,4},{12,8},{5,1},{9,5},{13,9},{6,2},{10,6},{14,10},{7,3},{... | collective-permute-start | bytes 39176 | tf_op jit(solution)/shard_map/ppermute | solution.py:25
  9.7 29.4 %collective-permute-start = (bf16[3,2176]{1,0:T(4,128)(2,1)S(1)}, bf16[3,2176]{1,0:T(4,128)(2,1)S(1)}, u32[]{:S(2)}, u32[]{:S(2)}) collective-permute-start(bf16[3,2176]{1,0:T(4,128)(2,1)S(1)} %pad_maximum_fusion.13), channel_id=1, source_target_pairs={{0,4},{4,8},{8,12},{1,5},{5,9},{9,13},{2,6},{6,10},{10,14},{3,7},{... | collective-permute-start | bytes 39176 | tf_op jit(solution)/shard_map/ppermute | solution.py:25
  19.5 6.3 %copy-start.2 = (bf16[512,16,128]{0,2,1:T(8,128)(2,1)S(1)}, bf16[512,16,128]{0,2,1:T(8,128)(2,1)}, u32[]{:S(2)}) copy-start(bf16[512,16,128]{0,2,1:T(8,128)(2,1)} %rev.9) | copy-start | bytes 6291460
  19.5 6.3 %copy-start.8 = (bf16[2048,1024]{1,0:T(8,128)(2,1)S(1)}, bf16[2048,1024]{1,0:T(8,128)(2,1)}, u32[]{:S(2)}) copy-start(bf16[2048,1024]{1,0:T(8,128)(2,1)} %param.18) | copy-start | bytes 12582916
  29.2 1.6 copy-start.6
  30.8 1.3 copy-start.24
  30.8 1.3 copy-start.15
  30.8 1.3 copy-start.21
  32.1 2.2 %copy-start.16 = (f32[4,1024]{1,0:T(4,128)S(1)}, f32[4,1024]{1,0:T(4,128)}, u32[]{:S(2)}) copy-start(f32[4,1024]{1,0:T(4,128)} %param.21) | copy-start | bytes 49156
  32.1 2.2 %copy-start.17 = (f32[4,512]{1,0:T(4,128)S(1)}, f32[4,512]{1,0:T(4,128)}, u32[]{:S(2)}) copy-start(f32[4,512]{1,0:T(4,128)} %param.23) | copy-start | bytes 24580
  32.5 5.2 %copy-start.14 = (f32[512,16]{0,1:T(8,128)}, f32[512,16]{0,1:T(8,128)S(1)}, u32[]{:S(2)}) copy-start(f32[512,16]{0,1:T(8,128)S(1)} %compare_select_fusion) | copy-start | bytes 98308
  32.6 3.7 %copy-start.22 = (f32[16]{0:T(128)S(1)}, f32[16]{0:T(128)}, u32[]{:S(2)}) copy-start(f32[16]{0:T(128)} %param.27) | copy-start | bytes 196
  35.3 8.5 %copy-start.13 = (f32[512,2,8]{0,2,1:T(8,128)}, f32[512,2,8]{0,2,1:T(8,128)S(1)}, u32[]{:S(2)}) copy-start(f32[512,2,8]{0,2,1:T(8,128)S(1)} %reshape_reshape.7) | copy-start | bytes 98308
  37.7 6.1 %copy-start.12 = (f32[512,2,8]{0,2,1:T(8,128)}, f32[512,2,8]{0,2,1:T(8,128)S(1)}, u32[]{:S(2)}) copy-start(f32[512,2,8]{0,2,1:T(8,128)S(1)} %reshape_reshape.6) | copy-start | bytes 98308
  39.7 4.3 %copy-start.10 = (bf16[512,1024]{0,1:T(8,128)(2,1)S(1)}, bf16[512,1024]{0,1:T(8,128)(2,1)}, u32[]{:S(2)}) copy-start(bf16[512,1024]{0,1:T(8,128)(2,1)} %multiply_convert_fusion.3) | copy-start | bytes 3145732
  39.7 4.3 %copy-start.11 = (bf16[512,1024]{0,1:T(8,128)(2,1)S(1)}, bf16[512,1024]{0,1:T(8,128)(2,1)}, u32[]{:S(2)}) copy-start(bf16[512,1024]{0,1:T(8,128)(2,1)} %multiply_convert_fusion.1) | copy-start | bytes 3145732
  39.7 4.3 %copy-start.18 = (f32[1024]{0:T(1024)S(1)}, f32[1024]{0:T(1024)}, u32[]{:S(2)}) copy-start(f32[1024]{0:T(1024)} %param.22) | copy-start | bytes 12292
  44.0 5.6 %copy-start.20 = (f32[512]{0:T(512)S(1)}, f32[512]{0:T(512)}, u32[]{:S(2)}) copy-start(f32[512]{0:T(512)} %param.24) | copy-start | bytes 6148
  58.9 22.8 %collective-permute-start.4 = (bf16[16,8448]{1,0:T(8,128)(2,1)}, bf16[16,8448]{1,0:T(8,128)(2,1)S(1)}, u32[]{:S(2)}, u32[]{:S(2)}) collective-permute-start(bf16[16,8448]{1,0:T(8,128)(2,1)} %pad_maximum_fusion.8), channel_id=1, source_target_pairs={{4,0},{8,4},{12,8},{5,1},{9,5},{13,9},{6,2},{10,6},{14,10},{7,3},{... | collective-permute-start | bytes 811016 | tf_op jit(solution)/shard_map/ppermute | solution.py:25
  71.5 12.7 %collective-permute-start.2 = (bf16[16,8448]{1,0:T(8,128)(2,1)S(1)}, bf16[16,8448]{1,0:T(8,128)(2,1)S(1)}, u32[]{:S(2)}, u32[]{:S(2)}) collective-permute-start(bf16[16,8448]{1,0:T(8,128)(2,1)S(1)} %pad_maximum_fusion.6), channel_id=1, source_target_pairs={{0,4},{4,8},{8,12},{1,5},{5,9},{9,13},{2,6},{6,10},{10,14},{3,7},{... | collective-permute-start | bytes 811016 | tf_op jit(solution)/shard_map/ppermute | solution.py:25
  82.1 12.8 %copy-start.5 = (f32[4,16,64,128]{3,2,1,0:T(8,128)S(1)}, f32[4,16,64,128]{3,2,1,0:T(8,128)}, u32[]{:S(2)}) copy-start(f32[4,16,64,128]{3,2,1,0:T(8,128)} %shard_map.149) | copy-start | bytes 6291460
  82.9 10.8 %collective-permute-start.5 = (bf16[16,8448]{1,0:T(8,128)(2,1)}, bf16[16,8448]{1,0:T(8,128)(2,1)}, u32[]{:S(2)}, u32[]{:S(2)}) collective-permute-start(bf16[16,8448]{1,0:T(8,128)(2,1)} %pad_maximum_fusion.9), channel_id=1, source_target_pairs={{8,0},{12,4},{9,1},{13,5},{10,2},{14,6},{11,3},{15,7},{24,16},{28,... | collective-permute-start | bytes 811016 | tf_op jit(solution)/shard_map/ppermute | solution.py:25
  84.7 23.8 %collective-permute-start.3 = (bf16[16,8448]{1,0:T(8,128)(2,1)S(1)}, bf16[16,8448]{1,0:T(8,128)(2,1)S(1)}, u32[]{:S(2)}, u32[]{:S(2)}) collective-permute-start(bf16[16,8448]{1,0:T(8,128)(2,1)S(1)} %pad_maximum_fusion.7), channel_id=1, source_target_pairs={{0,8},{4,12},{1,9},{5,13},{2,10},{6,14},{3,11},{7,15},{16,24},{20,... | collective-permute-start | bytes 811016 | tf_op jit(solution)/shard_map/ppermute | solution.py:25
  96.7 4.7 %copy-start.3 = (bf16[512,16,128]{0,2,1:T(8,128)(2,1)S(1)}, bf16[512,16,128]{0,2,1:T(8,128)(2,1)}, u32[]{:S(2)}) copy-start(bf16[512,16,128]{0,2,1:T(8,128)(2,1)} %rev.9) | copy-start | bytes 6291460
  108.5 1.6 copy-start.4
  111.9 4.8 %copy-start.7 = (bf16[512,2048]{1,0:T(8,128)(2,1)S(1)}, bf16[512,2048]{1,0:T(8,128)(2,1)}, u32[]{:S(2)}) copy-start(bf16[512,2048]{1,0:T(8,128)(2,1)} %param.15) | copy-start | bytes 6291460
  116.6 5.9 %copy-start.9 = (f32[512,1024]{0,1:T(8,128)S(1)}, f32[512,1024]{0,1:T(8,128)}, u32[]{:S(2)}) copy-start(f32[512,1024]{0,1:T(8,128)} %get-tuple-element.85) | copy-start | bytes 6291460
  116.6 5.9 %copy-start.19 = (f32[1024]{0:T(1024)S(1)}, f32[1024]{0:T(1024)}, u32[]{:S(2)}) copy-start(f32[1024]{0:T(1024)} %param.28) | copy-start | bytes 12292
  122.5 2.2 %copy-start.23 = (bf16[1024,2048]{1,0:T(8,128)(2,1)S(1)}, bf16[1024,2048]{1,0:T(8,128)(2,1)}, u32[]{:S(2)}) copy-start(bf16[1024,2048]{1,0:T(8,128)(2,1)} %param.29) | copy-start | bytes 12582916
  127.2 46.1 %copy-start.1 = (bf16[2048,512]{1,0:T(8,128)(2,1)S(1)}, bf16[2048,512]{1,0:T(8,128)(2,1)}, u32[]{:S(2)}) copy-start(bf16[2048,512]{1,0:T(8,128)(2,1)} %param.19) | copy-start | bytes 6291460
Sparse Core Ops, SparseCore 0:
  128.9 44.3 reduce-scatter.1
